TPU v7x, 256 devices: a whole 4x4x8 slice. The times are simulated.
256 devices in a mesh: loop: 4 (over y), inner: 8 (over x, core), batch: 8 (over z).
Axes of the slice: x: 4, y: 4, z: 8, core: 2. Of those that a mesh axis runs over, the one named last changes fastest.
Arguments:
- tokens: bfloat16 [32768, 4096], P(('loop', 'inner', 'batch')), may hold values from -24 to 24
- block_ids: int32 [32768, 4], P(('loop', 'inner', 'batch')), may hold values from 0 to 127, all different within a row; in each aligned block of 128 rows (0 to 127, 128 to 255, ...) at most 5 rows name the same one
- latent_mask: int32 [32768, 4, 64], P(('loop', 'inner', 'batch')), may hold values 0 or 1
- enc_weight: bfloat16 [4096, 8192], P(None, ('loop', 'inner')), may hold values from -0.09375 to 0.09375
- enc_bias: bfloat16 [8192], P(('loop', 'inner')), may hold values from -3 to 3
- dec_weight: bfloat16 [8192, 4096], P(('loop', 'inner')), may hold values from -1 to 1
- dec_bias: bfloat16 [4096], replicated, may hold values from -5 to 5
Outputs:
- grad_enc_weight: float32 [4096, 8192], P('batch', ('loop', 'inner'))
- grad_enc_bias: float32 [8192], P(('loop', 'inner', 'batch'))
- grad_dec_weight: float32 [8192, 4096], P(('loop', 'inner'), 'batch')
Inputs may be any that keep to these rules, and one draw needn't show every extreme that they name: `block_ids`: each row names 4 different blocks. Among the rows of one device no block is named more than 5 times, and some block is named exactly 5 times.
All inputs are finite; a program needn't handle non-finite values. No bound on the sum of `latent_mask` on one device may be relied on, other than what follows from the above.
Results may differ from a plain program's by a relative error of at most 0.015.
Values may be sent and summed in bfloat16 or wider, within the bound.
No kernel may reach another device: no remote copies, remote signals or barrier semaphores. Data moves between devices by JAX's collectives and lax.ppermute only.
A program may use at most 128 MiB of HBM per device.

v0:
```python
import jax
import jax.numpy as jnp
from jax import lax
from jax.sharding import PartitionSpec as P

BLK = 64
OWNER_AXES = ("loop", "inner")


def exchange(rows):
    return lax.all_to_all(rows, OWNER_AXES, split_axis=0, concat_axis=0, tiled=True)


def pick_rows(select, rows):
    return lax.dot_general(
        select, rows, (((0,), (0,)), ((), ())), preferred_element_type=jnp.float32
    ).astype(rows.dtype)


def shards(tokens, block_ids, latent_mask, enc_weight, enc_bias, dec_weight, dec_bias):
    tok_dev, model_width = tokens.shape
    pick_count = block_ids.shape[1]
    local_lat = enc_weight.shape[1]
    local_blocks = local_lat // BLK
    owners = lax.axis_size("loop") * lax.axis_size("inner")
    num_blocks = local_blocks * owners
    n_batch = lax.axis_size("batch")
    capacity = (9 * tok_dev * pick_count + 8 * num_blocks - 1) // (8 * num_blocks)
    slot_count = num_blocks * capacity
    routed = tok_dev * pick_count

    with jax.named_scope("slot_tables"):
        flat_ids = block_ids.reshape(routed)
        row_pos = jnp.arange(routed, dtype=jnp.int32)
        earlier_same = (flat_ids[:, None] == flat_ids[None, :]) & (row_pos[None, :] < row_pos[:, None])
        slot_rank = jnp.sum(earlier_same.astype(jnp.int32), axis=1)
        target = flat_ids * capacity + slot_rank
        row_to_slot = target[:, None] == jnp.arange(slot_count, dtype=jnp.int32)[None, :]
        row_to_slot = row_to_slot.astype(jnp.bfloat16)
        token_to_slot = jnp.sum(
            row_to_slot.reshape(tok_dev, pick_count, slot_count), axis=1
        ).astype(jnp.bfloat16)

    with jax.named_scope("dispatch"):
        send_rows = pick_rows(token_to_slot, tokens)
        mask_rows = latent_mask.reshape(routed, BLK).astype(jnp.bfloat16)
        send_mask = pick_rows(row_to_slot, mask_rows)
        slot_rows = exchange(send_rows)
        got_mask = exchange(send_mask)

    with jax.named_scope("encode_decode"):
        slot_block = (jnp.arange(slot_count, dtype=jnp.int32) // capacity) % local_blocks
        col_block = jnp.arange(local_lat, dtype=jnp.int32) // BLK
        in_block = slot_block[:, None] == col_block[None, :]
        latent_gate = jnp.where(
            in_block, jnp.tile(got_mask.astype(jnp.float32), (1, local_blocks)), 0.0
        )
        preact = jnp.dot(slot_rows, enc_weight, preferred_element_type=jnp.float32)
        preact = preact + enc_bias.astype(jnp.float32)[None, :]
        sparse_latent_code = (preact * latent_gate).astype(jnp.bfloat16)
        partials = jnp.dot(
            sparse_latent_code, dec_weight, preferred_element_type=jnp.float32
        ).astype(jnp.bfloat16)

    with jax.named_scope("combine"):
        returned = exchange(partials)
        rebuilt = jnp.dot(token_to_slot, returned, preferred_element_type=jnp.float32)
        residual_err = rebuilt + dec_bias.astype(jnp.float32)[None, :] - tokens.astype(jnp.float32)
        err_b = residual_err.astype(jnp.bfloat16)
        send_err = pick_rows(token_to_slot, err_b)
        error_rows = exchange(send_err)

    with jax.named_scope("backward"):
        pre_grad = lax.dot_general(
            error_rows, dec_weight, (((1,), (1,)), ((), ())), preferred_element_type=jnp.float32
        ) * latent_gate
        pre_grad_b = pre_grad.astype(jnp.bfloat16)
        enc_grad = lax.dot_general(
            slot_rows, pre_grad_b, (((0,), (0,)), ((), ())), preferred_element_type=jnp.float32
        )
        dec_grad_t = lax.dot_general(
            error_rows, sparse_latent_code, (((0,), (0,)), ((), ())),
            preferred_element_type=jnp.float32,
        )
        bias_grad = jnp.sum(pre_grad, axis=0)

    with jax.named_scope("grad_reduce"):
        rows_per = model_width // n_batch
        bias_per = local_lat // n_batch
        pad_rows = 16
        weights = jnp.concatenate(
            [
                enc_grad.astype(jnp.bfloat16).reshape(n_batch, rows_per, local_lat),
                dec_grad_t.astype(jnp.bfloat16).reshape(n_batch, rows_per, local_lat),
            ],
            axis=2,
        )
        bias_block = jnp.pad(
            bias_grad.astype(jnp.bfloat16).reshape(n_batch, 1, bias_per),
            ((0, 0), (0, pad_rows - 1), (0, 2 * local_lat - bias_per)),
        )
        stacked = jnp.concatenate([weights, bias_block], axis=1).reshape(
            n_batch * (rows_per + pad_rows), 2 * local_lat
        )
        reduced = lax.psum_scatter(stacked, "batch", scatter_dimension=0, tiled=True).astype(
            jnp.float32
        )
        grad_enc_weight = reduced[:rows_per, :local_lat]
        grad_dec_weight = reduced[:rows_per, local_lat:].T
        bias_share = reduced[rows_per, :bias_per]
    return (grad_enc_weight, bias_share, grad_dec_weight)


def solution(mesh):
    in_specs = (
        P(("loop", "inner", "batch"), None),
        P(("loop", "inner", "batch"), None),
        P(("loop", "inner", "batch"), None, None),
        P(None, ("loop", "inner")),
        P(("loop", "inner")),
        P(("loop", "inner"), None),
        P(),
    )
    out_specs = (
        P("batch", ("loop", "inner")),
        P(("loop", "inner", "batch")),
        P(("loop", "inner"), "batch"),
    )
    return jax.shard_map(shards, mesh=mesh, in_specs=in_specs, out_specs=out_specs, check_vma=False)
```

profile of v0, /device:TPU:6, one launch (start us, length us, event | category | flops | bytes accessed | tf_op | source)
XLA Modules:
  0.0 417.0 jit_solution(7061321738117097370)
XLA Ops:
  7.2 0.0 copy-start
  7.2 0.9 copy.33
  8.1 0.1 eq.50
  8.2 0.3 convert_reduce_fusion
  8.5 0.9 convert_element_type.83
  9.4 0.1 copy.35
  9.6 0.4 fusion.8
  10.0 0.2 copy.36
  10.2 0.1 all_to_all.33
  10.2 0.8 reshape.113
  11.0 7.6 %all-to-all-start.1 = ((bf16[32,2,640]{2,1,0:T(2,128)(2,1)}), bf16[32,2,640]{2,1,0:T(2,128)(2,1)S(1)}, u32[]{:S(2)}, u32[]{:S(2)}) async-start(bf16[32,2,640]{2,1,0:T(2,128)(2,1)} %reshape.113), calls=%async_computation.1 | async-start | bytes 163840 | tf_op jit(solution)/shard_map/dispatch/all_to_all | solution.py:11
  18.6 0.1 reduce_sum.33
  18.7 0.1 copy.34
  18.7 0.7 multiply_add_fusion.1
  19.5 0.2 fusion.11
  19.7 5.1 %convolution_convert_fusion.2 = bf16[640,4096]{1,0:T(8,128)(2,1)} fusion(bf16[128,640]{1,0:T(8,128)(2,1)S(1)} %fusion.11, bf16[128,4096]{1,0:T(8,128)(2,1)} %param.7), kind=kOutput, calls=%fused_computation.4 | convolution fusion | flops 673710080 | bytes 6455296 | tf_op jit(solution)/shard_map/dispatch/dot_general | solution.py:15
  24.7 7.6 %all_to_all.30 = bf16[32,20,4096]{2,1,0:T(8,128)(2,1)} reshape(bf16[640,4096]{1,0:T(8,128)(2,1)} %convolution_convert_fusion.2) | data formatting | bytes 10485760 | tf_op jit(solution)/shard_map/dispatch/all_to_all | solution.py:11
  32.3 0.0 copy-start.7
  32.3 0.0 all-to-all-done.1
  32.3 7.6 %all-to-all-start = ((bf16[32,20,4096]{2,1,0:T(8,128)(2,1)}), bf16[32,20,4096]{2,1,0:T(8,128)(2,1)}, u32[]{:S(2)}, u32[]{:S(2)}) async-start(bf16[32,20,4096]{2,1,0:T(8,128)(2,1)} %all_to_all.30), calls=%async_computation | async-start | bytes 12582912 | tf_op jit(solution)/shard_map/dispatch/all_to_all | solution.py:11
  39.9 0.0 copy-done.7
  40.0 0.2 reshape.114
  40.2 0.1 copy.37
  40.4 1.1 copy.38
  41.5 0.0 copy-start.3
  41.5 72.1 %all-to-all-done = bf16[32,20,4096]{2,1,0:T(8,128)(2,1)} async-done(((bf16[32,20,4096]{2,1,0:T(8,128)(2,1)}), bf16[32,20,4096]{2,1,0:T(8,128)(2,1)}, u32[]{:S(2)}, u32[]{:S(2)}) %all-to-all-start) | async-done | bytes 5242912 | tf_op jit(solution)/shard_map/dispatch/all_to_all | solution.py:11
  113.6 7.8 %all_to_all.32 = bf16[640,4096]{1,0:T(8,128)(2,1)} reshape(bf16[32,20,4096]{2,1,0:T(8,128)(2,1)} %all-to-all-done) | data formatting | bytes 10485760 | tf_op jit(solution)/shard_map/dispatch/all_to_all | solution.py:11
  121.4 0.0 copy-done.3
  121.4 4.7 %fusion.7 = bf16[640,256]{1,0:T(8,128)(2,1)S(1)} fusion(bf16[640,4096]{1,0:T(8,128)(2,1)} %all_to_all.32, bf16[4096,256]{1,0:T(8,128)(2,1)} %param.10, f32[640,256]{1,0:T(8,128)S(1)} %copy-done.3, s32[256]{0:T(256)S(1)} %and_select_fusion, f32[256]{0:T(256)S(1)} %convert_element_type.82, s32[640]{0:T(1024)S(1)} %add_select_fusion), kind=kOutput, calls=%fused_computation.18 | convolution fusion | flops 1342996480 | bytes 8327680 | tf_op jit(solution)/shard_map/encode_decode/dot_general | solution.py:58
  126.1 0.0 copy-done
  126.1 0.0 copy-start.4
  126.1 3.9 convolution_convert_fusion.1
  130.0 7.6 %all_to_all.35 = bf16[32,20,4096]{2,1,0:T(8,128)(2,1)} reshape(bf16[640,4096]{1,0:T(8,128)(2,1)} %convolution_convert_fusion.1) | data formatting | bytes 10485760 | tf_op jit(solution)/shard_map/combine/all_to_all | solution.py:11
  137.6 0.0 copy-done.4
  137.6 0.0 copy-start.6
  137.6 9.1 %all-to-all-start.2 = ((bf16[32,20,4096]{2,1,0:T(8,128)(2,1)}), bf16[32,20,4096]{2,1,0:T(8,128)(2,1)}, u32[]{:S(2)}, u32[]{:S(2)}) async-start(bf16[32,20,4096]{2,1,0:T(8,128)(2,1)} %all_to_all.35), calls=%async_computation.2 | async-start | bytes 12582912 | tf_op jit(solution)/shard_map/combine/all_to_all | solution.py:11
  146.8 0.0 reduce-scatter.2.cloned.1.call-start
  146.8 0.0 copy-done.6
  146.8 0.0 copy-start.2
  146.8 73.6 %all-to-all-done.2 = bf16[32,20,4096]{2,1,0:T(8,128)(2,1)} async-done(((bf16[32,20,4096]{2,1,0:T(8,128)(2,1)}), bf16[32,20,4096]{2,1,0:T(8,128)(2,1)}, u32[]{:S(2)}, u32[]{:S(2)}) %all-to-all-start.2) | async-done | bytes 5242912 | tf_op jit(solution)/shard_map/combine/all_to_all | solution.py:11
  220.5 7.8 %all_to_all.37 = bf16[640,4096]{1,0:T(8,128)(2,1)} reshape(bf16[32,20,4096]{2,1,0:T(8,128)(2,1)} %all-to-all-done.2) | data formatting | bytes 10485760 | tf_op jit(solution)/shard_map/combine/all_to_all | solution.py:11
  228.3 0.0 copy-done.2
  228.3 7.2 %convolution_convert_fusion = bf16[640,4096]{1,0:T(8,128)(2,1)} fusion(bf16[128,640]{1,0:T(8,128)(2,1)S(1)} %fusion.11, bf16[640,4096]{1,0:T(8,128)(2,1)} %all_to_all.37, bf16[128,4096]{1,0:T(8,128)(2,1)S(1)} %copy-done.2, f32[4096]{0:T(1024)S(1)} %convert_element_type.90), kind=kOutput, calls=%fused_computation.2 | convolution fusion | flops 1346895872 | bytes 11714560 | tf_op jit(solution)/shard_map/combine/dot_general | solution.py:15
  235.5 7.6 %all_to_all.38 = bf16[32,20,4096]{2,1,0:T(8,128)(2,1)} reshape(bf16[640,4096]{1,0:T(8,128)(2,1)} %convolution_convert_fusion) | data formatting | bytes 10485760 | tf_op jit(solution)/shard_map/combine/all_to_all | solution.py:11
  243.1 80.0 %all_to_all.45 = bf16[32,20,4096]{2,1,0:T(8,128)(2,1)} all-to-all(bf16[32,20,4096]{2,1,0:T(8,128)(2,1)} %all_to_all.38), channel_id=1, replica_groups=mesh['loop'=4,'inner'=8,'batch'=8] {'loop','inner'}, dimensions={0} | all-to-all | bytes 10485760 | tf_op jit(solution)/shard_map/combine/all_to_all | solution.py:11
  323.1 0.0 slice-start
  323.1 7.9 %all_to_all.40 = bf16[640,4096]{1,0:T(8,128)(2,1)} reshape(bf16[32,20,4096]{2,1,0:T(8,128)(2,1)} %all_to_all.45) | data formatting | bytes 10485760 | tf_op jit(solution)/shard_map/combine/all_to_all | solution.py:11
  331.1 0.0 copy-start.1
  331.1 0.0 copy-start.5
  331.1 4.4 %fusion.18 = (bf16[256]{0:T(256)(128)(2,1)S(1)}, bf16[640,256]{1,0:T(8,128)(2,1)S(1)}) fusion(f32[640,256]{1,0:T(8,128)} %copy.38, s32[256]{0:T(256)S(1)} %and_select_fusion, s32[640]{0:T(1024)S(1)} %add_select_fusion, bf16[640,4096]{1,0:T(8,128)(2,1)} %all_to_all.40, bf16[256,4096]{1,0:T(8,128)(2,1)S(1)} %copy-done), kind=kOutput, calls=%fused_computation.47 | convolution fusion | flops 1342996224 | bytes 8327168 | tf_op jit(solution)/shard_map/backward/dot_general | solution.py:74
  335.4 0.0 copy-done.1
  335.5 0.0 copy-done.5
  335.5 3.3 convolution_convert_fusion.3
  338.7 0.0 slice-done
  338.7 0.0 slice-done.1
  338.7 3.3 convolution_convert_fusion.4
  342.0 0.1 convert_element_type.101
  342.1 3.7 fusion.3
  345.8 0.0 reduce-scatter.2.cloned.1.call-update
  345.8 59.8 %reduce-scatter.2.cloned.1.call-done = bf16[528,512]{1,0:T(8,128)(2,1)} async-done(((bf16[4224,512]{1,0:T(8,128)(2,1)}), bf16[528,512]{1,0:T(8,128)(2,1)}) %reduce-scatter.2.cloned.1.call-update) | async-done | bytes 540688 | tf_op jit(solution)/shard_map/grad_reduce/reduce_scatter | solution.py:105
  405.6 1.2 convert_element_type.99
  406.8 0.5 slice_bitcast_fusion.1
  407.3 1.0 copy.40
  408.3 1.8 slice.12
  (10 shorter events, 0.2 us)
Async XLA Ops:
  7.2 118.9 %copy-start = (bf16[256,4096]{1,0:T(8,128)(2,1)S(1)}, bf16[256,4096]{1,0:T(8,128)(2,1)}, u32[]{:S(2)}) copy-start(bf16[256,4096]{1,0:T(8,128)(2,1)} %param.12) | copy-start | bytes 6291460
  11.0 21.3 %all-to-all-start.1 = ((bf16[32,2,640]{2,1,0:T(2,128)(2,1)}), bf16[32,2,640]{2,1,0:T(2,128)(2,1)S(1)}, u32[]{:S(2)}, u32[]{:S(2)}) async-start(bf16[32,2,640]{2,1,0:T(2,128)(2,1)} %reshape.113), calls=%async_computation.1 | async-start | bytes 163840 | tf_op jit(solution)/shard_map/dispatch/all_to_all | solution.py:11
  32.3 7.6 %copy-start.7 = (bf16[256]{0:T(256)(128)(2,1)S(1)}, bf16[256]{0:T(256)(128)(2,1)}, u32[]{:S(2)}) copy-start(bf16[256]{0:T(256)(128)(2,1)} %param.11) | copy-start | bytes 1540
  32.3 81.3 %all-to-all-start = ((bf16[32,20,4096]{2,1,0:T(8,128)(2,1)}), bf16[32,20,4096]{2,1,0:T(8,128)(2,1)}, u32[]{:S(2)}, u32[]{:S(2)}) async-start(bf16[32,20,4096]{2,1,0:T(8,128)(2,1)} %all_to_all.30), calls=%async_computation | async-start | bytes 12582912 | tf_op jit(solution)/shard_map/dispatch/all_to_all | solution.py:11
  41.5 79.9 %copy-start.3 = (f32[640,256]{1,0:T(8,128)S(1)}, f32[640,256]{1,0:T(8,128)}, u32[]{:S(2)}) copy-start(f32[640,256]{1,0:T(8,128)} %copy.38) | copy-start | bytes 1966084
  126.1 11.5 %copy-start.4 = (bf16[640,256]{1,0:T(8,128)(2,1)}, bf16[640,256]{1,0:T(8,128)(2,1)S(1)}, u32[]{:S(2)}) copy-start(bf16[640,256]{1,0:T(8,128)(2,1)S(1)} %fusion.7) | copy-start | bytes 983044
  137.6 9.2 %copy-start.6 = (bf16[4096]{0:T(1024)(128)(2,1)S(1)}, bf16[4096]{0:T(1024)(128)(2,1)}, u32[]{:S(2)}) copy-start(bf16[4096]{0:T(1024)(128)(2,1)} %param.13) | copy-start | bytes 24580
  137.6 82.9 %all-to-all-start.2 = ((bf16[32,20,4096]{2,1,0:T(8,128)(2,1)}), bf16[32,20,4096]{2,1,0:T(8,128)(2,1)}, u32[]{:S(2)}, u32[]{:S(2)}) async-start(bf16[32,20,4096]{2,1,0:T(8,128)(2,1)} %all_to_all.35), calls=%async_computation.2 | async-start | bytes 12582912 | tf_op jit(solution)/shard_map/combine/all_to_all | solution.py:11
  146.8 258.8 %reduce-scatter.2.cloned.1.call-start = ((), (), s32[]{:S(2)}) async-start(), calls=%async_computation.5 | async-start | bytes 4866048 | tf_op jit(solution)/shard_map/grad_reduce/reduce_scatter | solution.py:105
  146.8 81.5 %copy-start.2 = (bf16[128,4096]{1,0:T(8,128)(2,1)S(1)}, bf16[128,4096]{1,0:T(8,128)(2,1)}, u32[]{:S(2)}) copy-start(bf16[128,4096]{1,0:T(8,128)(2,1)} %param.7) | copy-start | bytes 3145732
  323.1 15.6 %slice-start = ((s8[5242880]{0:T(1024)(128)(4,1)}), s8[1048576]{0:T(1024)(128)(4,1)S(1)}, s32[]{:S(2)}) async-start(s8[5242880]{0:T(1024)(128)(4,1)} %bitcast.26), calls=%async_computation.6 | async-start | bytes 2097152
  331.1 4.4 %copy-start.1 = (bf16[640,4096]{1,0:T(8,128)(2,1)S(1)}, bf16[640,4096]{1,0:T(8,128)(2,1)}, u32[]{:S(2)}) copy-start(bf16[640,4096]{1,0:T(8,128)(2,1)} %all_to_all.40) | copy-start | bytes 15728644
  331.1 4.4 %copy-start.5 = (bf16[640,256]{1,0:T(8,128)(2,1)S(1)}, bf16[640,256]{1,0:T(8,128)(2,1)}, u32[]{:S(2)}) copy-start(bf16[640,256]{1,0:T(8,128)(2,1)} %copy-done.4) | copy-start | bytes 983044
  331.1 7.7 %slice-start.1 = ((s8[5242880]{0:T(1024)(128)(4,1)}), s8[4194304]{0:T(1024)(128)(4,1)S(1)}, s32[]{:S(2)}) async-start(s8[5242880]{0:T(1024)(128)(4,1)} %bitcast.26), calls=%async_computation.7 | async-start | bytes 8388608
Sparse Core Ops, SparseCore 0:
  346.0 59.5 reduce-scatter.1
where the time goes:
time: 419 us; the launch traced here: 417 us
  waiting for transfers between devices  206 us (49%)
  blocking collectives  80 us (19%)
  local copies, waits for them, and re-layouts  53.6 us (13%)
  matrix products  32.2 us (8%)
  starting transfers between devices  24.3 us (6%)
  between operations  14.2 us (3%)
  other arithmetic  7.03 us (2%)
    all_to_all x3, waiting for transfers between devices, exchange(): lax.all_to_all(rows, OWNER_AXES, split_axis=0, concat_axis=0, tiled=True)  146 us
    all_to_all x1, blocking collectives, exchange(): lax.all_to_all(rows, OWNER_AXES, split_axis=0, concat_axis=0, tiled=True)  80 us
    reduce_scatter x1, waiting for transfers between devices, shards(): lax.psum_scatter(stacked, 'batch', scatter_dimension=0, tiled=True)  59.8 us
    all_to_all x7, local copies, waits for them, and re-layouts, exchange(): lax.all_to_all(rows, OWNER_AXES, split_axis=0, concat_axis=0, tiled=True)  46.3 us
    all_to_all x3, starting transfers between devices, exchange(): lax.all_to_all(rows, OWNER_AXES, split_axis=0, concat_axis=0, tiled=True)  24.2 us
    dot_general x3, matrix products, pick_rows(): lax.dot_general(select, rows, (((0,), (0,)), ((), ())), preferred_element...  12.7 us
  transfers between devices with their start and end apart: 4, of which 3 were waited for; matrix products, arithmetic and copies ran while one was open for 2% of the time, Pallas kernels for 0%

commit v1 on v0

--- a/solution.py
+++ b/solution.py
@@ -34,55 +34,63 @@
         row_pos = jnp.arange(routed, dtype=jnp.int32)
         earlier_same = (flat_ids[:, None] == flat_ids[None, :]) & (row_pos[None, :] < row_pos[:, None])
         slot_rank = jnp.sum(earlier_same.astype(jnp.int32), axis=1)
-        target = flat_ids * capacity + slot_rank
+        target = ((flat_ids // local_blocks) * capacity + slot_rank) * local_blocks + flat_ids % local_blocks
         row_to_slot = target[:, None] == jnp.arange(slot_count, dtype=jnp.int32)[None, :]
         row_to_slot = row_to_slot.astype(jnp.bfloat16)
         token_to_slot = jnp.sum(
             row_to_slot.reshape(tok_dev, pick_count, slot_count), axis=1
         ).astype(jnp.bfloat16)
+        groups = slot_count // local_blocks
+        token_to_group = token_to_slot.reshape(tok_dev, groups, local_blocks)
 
     with jax.named_scope("dispatch"):
-        send_rows = pick_rows(token_to_slot, tokens)
+        send_rows = pick_rows(token_to_group, tokens)
         mask_rows = latent_mask.reshape(routed, BLK).astype(jnp.bfloat16)
         send_mask = pick_rows(row_to_slot, mask_rows)
         slot_rows = exchange(send_rows)
-        got_mask = exchange(send_mask)
+        got_mask = exchange(send_mask).reshape(groups, local_blocks, BLK)
 
     with jax.named_scope("encode_decode"):
-        slot_block = (jnp.arange(slot_count, dtype=jnp.int32) // capacity) % local_blocks
+        slot_block = jnp.arange(local_blocks, dtype=jnp.int32)
         col_block = jnp.arange(local_lat, dtype=jnp.int32) // BLK
         in_block = slot_block[:, None] == col_block[None, :]
         latent_gate = jnp.where(
-            in_block, jnp.tile(got_mask.astype(jnp.float32), (1, local_blocks)), 0.0
+            in_block[None], jnp.tile(got_mask.astype(jnp.float32), (1, 1, local_blocks)), 0.0
         )
-        preact = jnp.dot(slot_rows, enc_weight, preferred_element_type=jnp.float32)
-        preact = preact + enc_bias.astype(jnp.float32)[None, :]
+        preact = lax.dot_general(
+            slot_rows, enc_weight, (((2,), (0,)), ((), ())), preferred_element_type=jnp.float32
+        )
+        preact = preact + enc_bias.astype(jnp.float32)[None, None, :]
         sparse_latent_code = (preact * latent_gate).astype(jnp.bfloat16)
-        partials = jnp.dot(
-            sparse_latent_code, dec_weight, preferred_element_type=jnp.float32
+        partials = lax.dot_general(
+            sparse_latent_code, dec_weight, (((2,), (0,)), ((), ())),
+            preferred_element_type=jnp.float32,
         ).astype(jnp.bfloat16)
 
     with jax.named_scope("combine"):
         returned = exchange(partials)
-        rebuilt = jnp.dot(token_to_slot, returned, preferred_element_type=jnp.float32)
+        rebuilt = lax.dot_general(
+            token_to_group, returned, (((1, 2), (0, 1)), ((), ())),
+            preferred_element_type=jnp.float32,
+        )
         residual_err = rebuilt + dec_bias.astype(jnp.float32)[None, :] - tokens.astype(jnp.float32)
         err_b = residual_err.astype(jnp.bfloat16)
-        send_err = pick_rows(token_to_slot, err_b)
+        send_err = pick_rows(token_to_group, err_b)
         error_rows = exchange(send_err)
 
     with jax.named_scope("backward"):
         pre_grad = lax.dot_general(
-            error_rows, dec_weight, (((1,), (1,)), ((), ())), preferred_element_type=jnp.float32
+            error_rows, dec_weight, (((2,), (1,)), ((), ())), preferred_element_type=jnp.float32
         ) * latent_gate
         pre_grad_b = pre_grad.astype(jnp.bfloat16)
         enc_grad = lax.dot_general(
-            slot_rows, pre_grad_b, (((0,), (0,)), ((), ())), preferred_element_type=jnp.float32
+            slot_rows, pre_grad_b, (((0, 1), (0, 1)), ((), ())), preferred_element_type=jnp.float32
         )
         dec_grad_t = lax.dot_general(
-            error_rows, sparse_latent_code, (((0,), (0,)), ((), ())),
+            error_rows, sparse_latent_code, (((0, 1), (0, 1)), ((), ())),
             preferred_element_type=jnp.float32,
         )
-        bias_grad = jnp.sum(pre_grad, axis=0)
+        bias_grad = jnp.sum(pre_grad, axis=(0, 1))
 
     with jax.named_scope("grad_reduce"):
         rows_per = model_width // n_batch

time: 419 us -> 377 us (0.90)
  the two profiles are of different devices: /device:TPU:6 before, /device:TPU:1 now
where the time goes in v1:
time: 377 us; the launch traced here: 370 us
  waiting for transfers between devices  176 us (47%)
  blocking collectives  69.7 us (18%)
  matrix products  50.2 us (13%)
  local copies, waits for them, and re-layouts  28.7 us (8%)
  starting transfers between devices  25.9 us (7%)
  between operations  14.5 us (4%)
  other arithmetic  5.51 us (1%)
    all_to_all x3, waiting for transfers between devices, exchange(): lax.all_to_all(rows, OWNER_AXES, split_axis=0, concat_axis=0, tiled=True)  119 us
    all_to_all x1, blocking collectives, exchange(): lax.all_to_all(rows, OWNER_AXES, split_axis=0, concat_axis=0, tiled=True)  69.7 us
    reduce_scatter x1, waiting for transfers between devices, shards(): lax.psum_scatter(stacked, 'batch', scatter_dimension=0, tiled=True)  56.7 us
    all_to_all x3, starting transfers between devices, exchange(): lax.all_to_all(rows, OWNER_AXES, split_axis=0, concat_axis=0, tiled=True)  25.5 us
    dot_general x3, matrix products, pick_rows(): lax.dot_general(select, rows, (((0,), (0,)), ((), ())), preferred_element...  15.5 us
    convert_element_type x3, local copies, waits for them, and re-layouts, pick_rows(): return lax.dot_general(select, rows, (((0,), (0,)), ((), ())), preferred_...  13.1 us
    dot_general x1, matrix products, shards(): lax.dot_general(error_rows, sparse_latent_code, (((0, 1), (0, 1)), ((), (...  9.24 us
    dot_general x1, matrix products, shards(): lax.dot_general(slot_rows, pre_grad_b, (((0, 1), (0, 1)), ((), ())), pref...  9.04 us
  transfers between devices with their start and end apart: 4, of which 3 were waited for; matrix products, arithmetic and copies ran while one was open for 4% of the time, Pallas kernels for 0%

profile of v1, /device:TPU:1, one launch (start us, length us, event | category | flops | bytes accessed | tf_op | source)
XLA Modules:
  0.0 370.1 jit_solution(8896072859111287726)
XLA Ops:
  7.2 0.0 copy-start
  7.2 0.9 copy.105
  8.1 0.1 eq.54
  8.2 0.3 convert_reduce_fusion
  8.5 0.9 convert_element_type.83
  9.4 0.1 copy.111
  9.6 0.4 fusion.54
  10.0 0.2 copy.112
  10.2 0.1 all_to_all.16
  10.2 0.8 reshape.162
  11.0 8.6 %all-to-all-start.1 = ((bf16[32,2,640]{2,1,0:T(2,128)(2,1)}), bf16[32,2,640]{2,1,0:T(2,128)(2,1)S(1)}, u32[]{:S(2)}, u32[]{:S(2)}) async-start(bf16[32,2,640]{2,1,0:T(2,128)(2,1)} %reshape.162), calls=%async_computation.1 | async-start | bytes 163840 | tf_op jit(solution)/shard_map/dispatch/all_to_all | solution.py:11
  19.6 0.1 reduce_sum.33
  19.7 0.1 copy.106
  19.8 0.7 fusion.67
  20.5 0.2 fusion.58
  20.7 0.2 copy.107
  20.9 2.7 convolution_convert_fusion.2
  23.6 6.4 %copy.109 = bf16[160,4,4096]{2,1,0:T(4,128)(2,1)} copy(bf16[160,4,4096]{2,0,1:T(8,128)(2,1)S(1)} %convolution_convert_fusion.2) | data formatting | bytes 10485760 | tf_op jit(solution)/shard_map/dispatch/convert_element_type | solution.py:17
  30.0 0.0 copy-start.7
  30.0 0.0 all-to-all-done.1
  30.0 7.7 %all-to-all-start = ((bf16[160,4,4096]{2,1,0:T(4,128)(2,1)}), bf16[160,4,4096]{2,1,0:T(4,128)(2,1)}, u32[]{:S(2)}, u32[]{:S(2)}) async-start(bf16[160,4,4096]{2,1,0:T(4,128)(2,1)} %copy.109), calls=%async_computation | async-start | bytes 10485760 | tf_op jit(solution)/shard_map/dispatch/all_to_all | solution.py:11
  37.8 0.0 copy-done.7
  37.8 0.2 reshape.163
  38.0 0.1 reshape.154
  38.1 0.9 copy.113
  39.0 1.0 tile.4
  40.1 1.2 copy.114
  41.2 57.8 %all-to-all-done = bf16[160,4,4096]{2,1,0:T(4,128)(2,1)} async-done(((bf16[160,4,4096]{2,1,0:T(4,128)(2,1)}), bf16[160,4,4096]{2,1,0:T(4,128)(2,1)}, u32[]{:S(2)}, u32[]{:S(2)}) %all-to-all-start) | async-done | bytes 5242912 | tf_op jit(solution)/shard_map/dispatch/all_to_all | solution.py:11
  99.1 8.9 %fusion.49 = bf16[160,4,256]{2,0,1:T(8,128)(2,1)S(1)} fusion(bf16[4096,256]{1,0:T(8,128)(2,1)} %param.10, bf16[160,4,4096]{2,1,0:T(4,128)(2,1)} %all-to-all-done, f32[160,4,256]{2,0,1:T(8,128)} %copy.114, f32[256]{0:T(256)S(1)} %convert_element_type.82, pred[4,256]{1,0:T(4,128)(4,1)S(1)} %iota_compare_fusion.7), kind=kOutput, calls=%fused_computation.33 | convolution fusion | flops 1342832640 | bytes 8325120 | tf_op jit(solution)/shard_map/encode_decode/dot_general | solution.py:60
  108.0 0.0 copy-done
  108.0 0.0 copy-start.3
  108.0 1.5 convolution_convert_fusion.1
  109.5 0.0 copy-done.3
  109.6 6.4 %copy.115 = bf16[160,4,4096]{2,1,0:T(4,128)(2,1)} copy(bf16[160,4,4096]{2,0,1:T(8,128)(2,1)S(1)} %convolution_convert_fusion.1) | data formatting | bytes 10485760 | tf_op jit(solution)/shard_map/encode_decode/convert_element_type | solution.py:68
  116.0 0.0 copy-start.6
  116.0 0.0 copy-start.2
  116.0 9.2 %all-to-all-start.2 = ((bf16[160,4,4096]{2,1,0:T(4,128)(2,1)}), bf16[160,4,4096]{2,1,0:T(4,128)(2,1)}, u32[]{:S(2)}, u32[]{:S(2)}) async-start(bf16[160,4,4096]{2,1,0:T(4,128)(2,1)} %copy.115), calls=%async_computation.2 | async-start | bytes 10485760 | tf_op jit(solution)/shard_map/combine/all_to_all | solution.py:11
  125.1 0.4 reduce-scatter.2.cloned.1.call-start
  125.6 0.0 copy-done.6
  125.6 61.1 %all-to-all-done.2 = bf16[160,4,4096]{2,1,0:T(4,128)(2,1)} async-done(((bf16[160,4,4096]{2,1,0:T(4,128)(2,1)}), bf16[160,4,4096]{2,1,0:T(4,128)(2,1)}, u32[]{:S(2)}, u32[]{:S(2)}) %all-to-all-start.2) | async-done | bytes 5242912 | tf_op jit(solution)/shard_map/combine/all_to_all | solution.py:11
  186.7 0.0 copy-done.2
  186.7 12.3 %convolution_convert_fusion = bf16[160,4,4096]{2,0,1:T(8,128)(2,1)} fusion(bf16[160,4,4096]{2,1,0:T(4,128)(2,1)} %all-to-all-done.2, bf16[128,4096]{1,0:T(8,128)(2,1)S(1)} %copy-done.2, f32[4096]{0:T(1024)S(1)} %convert_element_type.90, bf16[128,160,4]{0,2,1:T(4,128)(2,1)S(1)} %bitcast.62), kind=kOutput, calls=%fused_computation.2 | convolution fusion | flops 1346895872 | bytes 11714560 | tf_op jit(solution)/shard_map/combine/dot_general | solution.py:15
  199.0 6.5 %copy.119 = bf16[160,4,4096]{2,1,0:T(4,128)(2,1)S(1)} copy(bf16[160,4,4096]{2,0,1:T(8,128)(2,1)} %convolution_convert_fusion) | data formatting | bytes 10485760 | tf_op jit(solution)/shard_map/combine/convert_element_type | solution.py:17
  205.6 0.0 copy-start.5
  205.6 69.7 %all_to_all.24 = bf16[160,4,4096]{2,1,0:T(4,128)(2,1)S(1)} all-to-all(bf16[160,4,4096]{2,1,0:T(4,128)(2,1)S(1)} %copy.119), channel_id=1, replica_groups=mesh['loop'=4,'inner'=8,'batch'=8] {'loop','inner'}, dimensions={0} | all-to-all | bytes 10485760 | tf_op jit(solution)/shard_map/combine/all_to_all | solution.py:11
  275.2 0.0 copy-done.5
  275.2 0.0 copy-start.1
  275.2 0.0 copy-start.4
  275.2 6.0 %fusion.76 = (bf16[256]{0:T(256)(128)(2,1)S(1)}, bf16[160,4,256]{2,0,1:T(8,128)(2,1)S(1)}) fusion(f32[160,4,256]{2,0,1:T(8,128)S(1)} %copy-done.5, pred[4,256]{1,0:T(4,128)(4,1)S(1)} %iota_compare_fusion.7, bf16[256,4096]{1,0:T(8,128)(2,1)S(1)} %copy-done, bf16[160,4,4096]{2,1,0:T(4,128)(2,1)S(1)} %all_to_all.24), kind=kOutput, calls=%fused_computation.76 | convolution fusion | flops 1342832384 | bytes 8324608 | tf_op jit(solution)/shard_map/backward/dot_general | solution.py:82
  281.2 0.0 copy-done.1
  281.2 0.1 convert_element_type.101
  281.3 0.0 copy-done.4
  281.3 9.2 %fusion.4 = bf16[4096,256]{1,0:T(8,128)(2,1)S(1)} fusion(bf16[160,4,256]{2,0,1:T(8,128)(2,1)S(1)} %copy-done.4, bf16[160,4,4096]{2,1,0:T(4,128)(2,1)} %copy-done.1), kind=kOutput, calls=%fused_computation.10 | convolution fusion | flops 1343225856 | bytes 7667712 | tf_op jit(solution)/shard_map/backward/dot_general | solution.py:89
  290.5 9.0 %fusion.3 = bf16[4096,256]{1,0:T(8,128)(2,1)S(1)} fusion(bf16[160,4,4096]{2,1,0:T(4,128)(2,1)} %all-to-all-done, bf16[160,4,256]{2,0,1:T(8,128)(2,1)S(1)} %get-tuple-element.22), kind=kOutput, calls=%fused_computation.9 | convolution fusion | flops 1343225856 | bytes 7667712 | tf_op jit(solution)/shard_map/backward/dot_general | solution.py:86
  299.6 2.2 fusion.26
  301.8 0.0 reduce-scatter.2.cloned.1.call-update
  301.8 56.7 %reduce-scatter.2.cloned.1.call-done = bf16[528,512]{1,0:T(8,128)(2,1)} async-done(((bf16[4224,512]{1,0:T(8,128)(2,1)}), bf16[528,512]{1,0:T(8,128)(2,1)}) %reduce-scatter.2.cloned.1.call-update) | async-done | bytes 540688 | tf_op jit(solution)/shard_map/grad_reduce/reduce_scatter | solution.py:113
  358.5 1.2 convert_element_type.99
  359.7 0.5 slice_bitcast_fusion.1
  360.3 1.0 copy.124
  361.2 1.8 slice.12
  (6 shorter events, 0.1 us)
Async XLA Ops:
  7.2 100.8 %copy-start = (bf16[256,4096]{1,0:T(8,128)(2,1)S(1)}, bf16[256,4096]{1,0:T(8,128)(2,1)}, u32[]{:S(2)}) copy-start(bf16[256,4096]{1,0:T(8,128)(2,1)} %param.12) | copy-start | bytes 6291460
  11.0 19.0 %all-to-all-start.1 = ((bf16[32,2,640]{2,1,0:T(2,128)(2,1)}), bf16[32,2,640]{2,1,0:T(2,128)(2,1)S(1)}, u32[]{:S(2)}, u32[]{:S(2)}) async-start(bf16[32,2,640]{2,1,0:T(2,128)(2,1)} %reshape.162), calls=%async_computation.1 | async-start | bytes 163840 | tf_op jit(solution)/shard_map/dispatch/all_to_all | solution.py:11
  30.0 7.8 %copy-start.7 = (bf16[256]{0:T(256)(128)(2,1)S(1)}, bf16[256]{0:T(256)(128)(2,1)}, u32[]{:S(2)}) copy-start(bf16[256]{0:T(256)(128)(2,1)} %param.11) | copy-start | bytes 1540
  30.0 69.1 %all-to-all-start = ((bf16[160,4,4096]{2,1,0:T(4,128)(2,1)}), bf16[160,4,4096]{2,1,0:T(4,128)(2,1)}, u32[]{:S(2)}, u32[]{:S(2)}) async-start(bf16[160,4,4096]{2,1,0:T(4,128)(2,1)} %copy.109), calls=%async_computation | async-start | bytes 10485760 | tf_op jit(solution)/shard_map/dispatch/all_to_all | solution.py:11
  108.0 1.6 copy-start.3
  116.0 9.6 %copy-start.6 = (bf16[4096]{0:T(1024)(128)(2,1)S(1)}, bf16[4096]{0:T(1024)(128)(2,1)}, u32[]{:S(2)}) copy-start(bf16[4096]{0:T(1024)(128)(2,1)} %param.13) | copy-start | bytes 24580
  116.0 70.7 %copy-start.2 = (bf16[128,4096]{1,0:T(8,128)(2,1)S(1)}, bf16[128,4096]{1,0:T(8,128)(2,1)}, u32[]{:S(2)}) copy-start(bf16[128,4096]{1,0:T(8,128)(2,1)} %param.7) | copy-start | bytes 3145732
  116.0 70.7 %all-to-all-start.2 = ((bf16[160,4,4096]{2,1,0:T(4,128)(2,1)}), bf16[160,4,4096]{2,1,0:T(4,128)(2,1)}, u32[]{:S(2)}, u32[]{:S(2)}) async-start(bf16[160,4,4096]{2,1,0:T(4,128)(2,1)} %copy.115), calls=%async_computation.2 | async-start | bytes 10485760 | tf_op jit(solution)/shard_map/combine/all_to_all | solution.py:11
  125.1 233.4 %reduce-scatter.2.cloned.1.call-start = ((), (), s32[]{:S(2)}) async-start(), calls=%async_computation.5 | async-start | bytes 4866048 | tf_op jit(solution)/shard_map/grad_reduce/reduce_scatter | solution.py:113
  205.6 69.7 %copy-start.5 = (f32[160,4,256]{2,0,1:T(8,128)S(1)}, f32[160,4,256]{2,0,1:T(8,128)}, u32[]{:S(2)}) copy-start(f32[160,4,256]{2,0,1:T(8,128)} %copy.114) | copy-start | bytes 1966084
  275.2 6.0 %copy-start.1 = (bf16[160,4,4096]{2,1,0:T(4,128)(2,1)}, bf16[160,4,4096]{2,1,0:T(4,128)(2,1)S(1)}, u32[]{:S(2)}) copy-start(bf16[160,4,4096]{2,1,0:T(4,128)(2,1)S(1)} %all_to_all.24) | copy-start | bytes 15728644
  275.2 6.1 %copy-start.4 = (bf16[160,4,256]{2,0,1:T(8,128)(2,1)S(1)}, bf16[160,4,256]{2,0,1:T(8,128)(2,1)}, u32[]{:S(2)}) copy-start(bf16[160,4,256]{2,0,1:T(8,128)(2,1)} %copy-done.3) | copy-start | bytes 983044
Sparse Core Ops, SparseCore 0:
  301.9 56.5 reduce-scatter.1

commit v2 on v0

v2 whole, which is shorter than its diff:
```python
import jax
import jax.numpy as jnp
from jax import lax
from jax.sharding import PartitionSpec as P

BLK = 64
OWNER_AXES = ("loop", "inner")


def exchange(rows):
    return lax.all_to_all(rows, OWNER_AXES, split_axis=0, concat_axis=0, tiled=True)


def pick_rows(select, rows):
    return lax.dot_general(
        select, rows, (((0,), (0,)), ((), ())), preferred_element_type=jnp.float32
    ).astype(rows.dtype)


def shards(tokens, block_ids, latent_mask, enc_weight, enc_bias, dec_weight, dec_bias):
    tok_dev, model_width = tokens.shape
    pick_count = block_ids.shape[1]
    local_lat = enc_weight.shape[1]
    local_blocks = local_lat // BLK
    owners = lax.axis_size("loop") * lax.axis_size("inner")
    num_blocks = local_blocks * owners
    n_batch = lax.axis_size("batch")
    capacity = (9 * tok_dev * pick_count + 8 * num_blocks - 1) // (8 * num_blocks)
    routed = tok_dev * pick_count
    main_ranks = min(capacity, (capacity * local_blocks // 8) * 8 // local_blocks)
    rank_sets = [(0, main_ranks), (main_ranks, capacity)] if main_ranks < capacity else [(0, capacity)]
    extra = 2 * BLK

    with jax.named_scope("slot_tables"):
        flat_ids = block_ids.reshape(routed)
        row_pos = jnp.arange(routed, dtype=jnp.int32)
        earlier_same = (flat_ids[:, None] == flat_ids[None, :]) & (row_pos[None, :] < row_pos[:, None])
        slot_rank = jnp.sum(earlier_same.astype(jnp.int32), axis=1)
        owner_of = flat_ids // local_blocks
        local_of = flat_ids % local_blocks
        row_to_slot, token_to_slot = [], []
        for lo, hi in rank_sets:
            per_owner = (hi - lo) * local_blocks
            target = owner_of * per_owner + (slot_rank - lo) * local_blocks + local_of
            target = jnp.where((slot_rank >= lo) & (slot_rank < hi), target, -1)
            hit = target[:, None] == jnp.arange(owners * per_owner, dtype=jnp.int32)[None, :]
            row_to_slot.append(hit.astype(jnp.bfloat16))
            token_to_slot.append(
                jnp.sum(hit.reshape(tok_dev, pick_count, -1).astype(jnp.int32), axis=1).astype(
                    jnp.bfloat16
                )
            )

    with jax.named_scope("dispatch"):
        tokens_ext = jnp.pad(tokens, ((0, 0), (0, extra)))
        mask_rows = latent_mask.reshape(routed, BLK).astype(jnp.float32)
        payload = []
        for k in range(len(rank_sets)):
            send_mask = lax.dot_general(
                row_to_slot[k], mask_rows, (((0,), (0,)), ((), ())),
                preferred_element_type=jnp.float32,
            )
            send_mask = jnp.pad(send_mask, ((0, 0), (model_width, extra - BLK)))
            picked = lax.dot_general(
                token_to_slot[k], tokens_ext, (((0,), (0,)), ((), ())),
                preferred_element_type=jnp.float32,
            )
            payload.append(exchange((picked + send_mask).astype(jnp.bfloat16)))
        enc_ext = jnp.pad(enc_weight, ((0, extra), (0, 0)))

    with jax.named_scope("encode_decode"):
        col_block = jnp.arange(local_lat, dtype=jnp.int32) // BLK
        gates, codes, returned = [], [], []
        for k in range(len(rank_sets)):
            rows = payload[k].shape[0]
            row_block = jnp.arange(rows, dtype=jnp.int32) % local_blocks
            in_block = row_block[:, None] == col_block[None, :]
            mask_k = payload[k][:, model_width:model_width + BLK].astype(jnp.float32)
            gate_k = jnp.where(in_block, jnp.tile(mask_k, (1, local_blocks)), 0.0)
            preact = jnp.dot(payload[k], enc_ext, preferred_element_type=jnp.float32)
            preact = preact + enc_bias.astype(jnp.float32)[None, :]
            code_k = (preact * gate_k).astype(jnp.bfloat16)
            partials = jnp.dot(code_k, dec_weight, preferred_element_type=jnp.float32).astype(
                jnp.bfloat16
            )
            gates.append(gate_k)
            codes.append(code_k)
            returned.append(exchange(partials))

    with jax.named_scope("combine"):
        rebuilt = dec_bias.astype(jnp.float32)[None, :] - tokens.astype(jnp.float32)
        for k in range(len(rank_sets)):
            rebuilt = rebuilt + jnp.dot(
                token_to_slot[k], returned[k], preferred_element_type=jnp.float32
            )
        err_b = rebuilt.astype(jnp.bfloat16)
        error_rows = [exchange(pick_rows(token_to_slot[k], err_b)) for k in range(len(rank_sets))]

    with jax.named_scope("backward"):
        enc_grad = dec_grad_t = bias_grad = 0.0
        for k in range(len(rank_sets)):
            pre_grad = lax.dot_general(
                error_rows[k], dec_weight, (((1,), (1,)), ((), ())),
                preferred_element_type=jnp.float32,
            ) * gates[k]
            pre_grad_b = pre_grad.astype(jnp.bfloat16)
            enc_grad = enc_grad + lax.dot_general(
                payload[k], pre_grad_b, (((0,), (0,)), ((), ())),
                preferred_element_type=jnp.float32,
            )[:model_width]
            dec_grad_t = dec_grad_t + lax.dot_general(
                error_rows[k], codes[k], (((0,), (0,)), ((), ())),
                preferred_element_type=jnp.float32,
            )
            bias_grad = bias_grad + jnp.sum(pre_grad, axis=0)

    with jax.named_scope("grad_reduce"):
        rows_per = model_width // n_batch
        bias_per = local_lat // n_batch
        pad_rows = 16
        weights = jnp.concatenate(
            [
                enc_grad.astype(jnp.bfloat16).reshape(n_batch, rows_per, local_lat),
                dec_grad_t.astype(jnp.bfloat16).reshape(n_batch, rows_per, local_lat),
            ],
            axis=2,
        )
        bias_block = jnp.pad(
            bias_grad.astype(jnp.bfloat16).reshape(n_batch, 1, bias_per),
            ((0, 0), (0, pad_rows - 1), (0, 2 * local_lat - bias_per)),
        )
        stacked = jnp.concatenate([weights, bias_block], axis=1).reshape(
            n_batch * (rows_per + pad_rows), 2 * local_lat
        )
        reduced = lax.psum_scatter(stacked, "batch", scatter_dimension=0, tiled=True).astype(
            jnp.float32
        )
        grad_enc_weight = reduced[:rows_per, :local_lat]
        grad_dec_weight = reduced[:rows_per, local_lat:].T
        bias_share = reduced[rows_per, :bias_per]
    return (grad_enc_weight, bias_share, grad_dec_weight)


def solution(mesh):
    in_specs = (
        P(("loop", "inner", "batch"), None),
        P(("loop", "inner", "batch"), None),
        P(("loop", "inner", "batch"), None, None),
        P(None, ("loop", "inner")),
        P(("loop", "inner")),
        P(("loop", "inner"), None),
        P(),
    )
    out_specs = (
        P("batch", ("loop", "inner")),
        P(("loop", "inner", "batch")),
        P(("loop", "inner"), "batch"),
    )
    return jax.shard_map(shards, mesh=mesh, in_specs=in_specs, out_specs=out_specs, check_vma=False)
```

time: 419 us -> 352 us (0.84)
  blocking collectives: 80 us -> 0 us
  local copies, waits for them, and re-layouts: 53.6 us -> 28.3 us
  starting transfers between devices: 24.3 us -> 48 us
  matrix products: 32.2 us -> 45.6 us
    all_to_all x1 -> x0, blocking collectives: 80 us -> none  [exchange(): lax.all_to_all(rows, OWNER_AXES, split_axis=0, concat_axis=0, tiled=True)]
    all_to_all x7 -> x6, local copies, waits for them, and re-layouts: 46.3 us -> 10.6 us  [exchange(): lax.all_to_all(rows, OWNER_AXES, split_axis=0, concat_axis=0, tiled=True)]
    all_to_all x3 -> x6, starting transfers between devices: 24.2 us -> 48 us  [exchange(): lax.all_to_all(rows, OWNER_AXES, split_axis=0, concat_axis=0, tiled=True)]
    dot_general x5 -> x16, matrix products: 19.5 us -> 40.8 us  [the longest x2 7.6 us: shards(): lax.dot_general(error_rows[k], codes[k], (((0,), (0,)), ((), ())), prefer...]
    dot_general x3 -> x2, matrix products: 12.7 us -> 4.78 us  [pick_rows(): lax.dot_general(select, rows, (((0,), (0,)), ((), ())), preferred_element...]
    another operation x2 -> x4, local copies, waits for them, and re-layouts: 1.16 us -> 6.2 us  [shards(): gate_k = jnp.where(in_block, jnp.tile(mask_k, (1, local_blocks)), 0.0)]
    unnamed x24 -> x46, local copies, waits for them, and re-layouts: 2.93 us -> 7.51 us
    all_to_all x3 -> x6, waiting for transfers between devices: 146 us -> 146 us  [exchange(): lax.all_to_all(rows, OWNER_AXES, split_axis=0, concat_axis=0, tiled=True)]
  transfers between devices with their start and end apart: 4 -> 7, of which waited for: 3 -> 6; matrix products, arithmetic and copies ran while one was open for 2% -> 11% of each run, Pallas kernels for 0% -> 0%
where the time goes in v2:
time: 352 us; the launch traced here: 350 us
  waiting for transfers between devices  206 us (59%)
  starting transfers between devices  48 us (14%)
  matrix products  45.6 us (13%)
  local copies, waits for them, and re-layouts  28.3 us (8%)
  between operations  14.4 us (4%)
  other arithmetic  7.51 us (2%)
    all_to_all x6, waiting for transfers between devices, exchange(): lax.all_to_all(rows, OWNER_AXES, split_axis=0, concat_axis=0, tiled=True)  146 us
    reduce_scatter x1, waiting for transfers between devices, shards(): lax.psum_scatter(stacked, 'batch', scatter_dimension=0, tiled=True)  59.7 us
    all_to_all x6, starting transfers between devices, exchange(): lax.all_to_all(rows, OWNER_AXES, split_axis=0, concat_axis=0, tiled=True)  48 us
    all_to_all x6, local copies, waits for them, and re-layouts, exchange(): lax.all_to_all(rows, OWNER_AXES, split_axis=0, concat_axis=0, tiled=True)  10.6 us
    dot_general x2, matrix products, shards(): lax.dot_general(error_rows[k], codes[k], (((0,), (0,)), ((), ())), prefer...  7.6 us
    unnamed x46, local copies, waits for them, and re-layouts  7.51 us
  transfers between devices with their start and end apart: 7, of which 6 were waited for; matrix products, arithmetic and copies ran while one was open for 11% of the time, Pallas kernels for 0%

profile of v2, /device:TPU:6, one launch (start us, length us, event | category | flops | bytes accessed | tf_op | source)
XLA Modules:
  0.0 349.8 jit_solution(17242194341114007822)
XLA Ops:
  7.2 0.8 broadcast_compare_fusion
  8.0 0.8 copy.33
  8.8 0.1 copy.39
  9.0 0.3 convert_reduce_fusion.1
  9.5 0.1 and.121
  10.0 0.2 convert_reduce_fusion.2
  10.1 0.9 convert_element_type.107
  11.1 0.1 copy.42
  11.2 0.6 copy-done.14
  11.9 0.3 fusion.37
  12.2 1.7 fusion.1
  13.9 1.1 all_to_all.54
  15.1 7.6 %all-to-all-start.2 = ((bf16[32,4,4224]{2,1,0:T(4,128)(2,1)}), bf16[32,4,4224]{2,1,0:T(4,128)(2,1)S(1)}, u32[]{:S(2)}, u32[]{:S(2)}) async-start(bf16[32,4,4224]{2,1,0:T(4,128)(2,1)} %all_to_all.54), calls=%async_computation.2 | async-start | bytes 2162688 | tf_op jit(solution)/shard_map/dispatch/all_to_all | solution.py:11
  22.7 0.2 convert_reduce_fusion
  22.9 1.5 fusion.32
  24.4 4.6 %add_convert_fusion = bf16[512,4224]{1,0:T(8,128)(2,1)} fusion(f32[512,64]{1,0:T(8,128)S(1)} %fusion.32, bf16[128,4096]{1,0:T(8,128)(2,1)} %param.7, s32[128,512]{1,0:T(8,128)S(1)} %convert_reduce_fusion), kind=kOutput, calls=%fused_computation.1 | convolution fusion | flops 558039040 | bytes 5767168 | tf_op jit(solution)/shard_map/dispatch/dot_general | solution.py:64
  29.0 8.6 %all-to-all-done.2 = bf16[32,4,4224]{2,1,0:T(4,128)(2,1)S(1)} async-done(((bf16[32,4,4224]{2,1,0:T(4,128)(2,1)}), bf16[32,4,4224]{2,1,0:T(4,128)(2,1)S(1)}, u32[]{:S(2)}, u32[]{:S(2)}) %all-to-all-start.2) | async-done | bytes 1081376 | tf_op jit(solution)/shard_map/dispatch/all_to_all | solution.py:11
  37.6 1.0 copy-done.3
  38.6 7.5 %all-to-all-start = ((bf16[32,16,4224]{2,1,0:T(8,128)(2,1)}), bf16[32,16,4224]{2,1,0:T(8,128)(2,1)}, u32[]{:S(2)}, u32[]{:S(2)}) async-start(bf16[32,16,4224]{2,1,0:T(8,128)(2,1)} %bitcast.42), calls=%async_computation | async-start | bytes 8650752 | tf_op jit(solution)/shard_map/dispatch/all_to_all | solution.py:11
  46.1 0.5 convert_element_type.112
  46.6 0.5 and_select_fusion
  47.1 0.5 and_select_fusion.1
  47.7 1.3 all_to_all.56
  49.1 0.8 tile.20
  50.0 1.6 copy.49
  51.6 2.1 fusion.26
  53.7 0.6 copy-done.12
  54.4 1.4 convolution_convert_fusion.3
  55.8 2.2 all_to_all.57
  58.1 38.5 %all-to-all-done = bf16[32,16,4224]{2,1,0:T(8,128)(2,1)} async-done(((bf16[32,16,4224]{2,1,0:T(8,128)(2,1)}), bf16[32,16,4224]{2,1,0:T(8,128)(2,1)}, u32[]{:S(2)}, u32[]{:S(2)}) %all-to-all-start) | async-done | bytes 4325408 | tf_op jit(solution)/shard_map/dispatch/all_to_all | solution.py:11
  96.6 8.6 %all-to-all-start.3 = ((bf16[32,4,4096]{2,1,0:T(4,128)(2,1)}), bf16[32,4,4096]{2,1,0:T(4,128)(2,1)S(1)}, u32[]{:S(2)}, u32[]{:S(2)}) async-start(bf16[32,4,4096]{2,1,0:T(4,128)(2,1)} %all_to_all.57), calls=%async_computation.3 | async-start | bytes 2097152 | tf_op jit(solution)/shard_map/encode_decode/all_to_all | solution.py:11
  105.2 1.6 slice.31
  106.8 1.6 copy.54
  108.4 1.7 tile.8
  110.1 2.0 copy.45
  112.2 4.2 %fusion.17 = bf16[512,256]{1,0:T(8,128)(2,1)S(1)} fusion(bf16[512,4224]{1,0:T(8,128)(2,1)} %bitcast.2, bf16[4096,256]{1,0:T(8,128)(2,1)} %param.10, f32[512,256]{1,0:T(8,128)} %copy.45, s32[256]{0:T(256)S(1)} %copy-done.17, f32[256]{0:T(256)S(1)} %copy-done.19, s32[512]{0:T(512)S(1)} %add_select_fusion.4), kind=kOutput, calls=%fused_computation.25 | convolution fusion | flops 1107951616 | bytes 7213056 | tf_op jit(solution)/shard_map/encode_decode/dot_general | solution.py:80
  116.4 0.7 copy-done.10
  117.1 3.3 convolution_convert_fusion.1
  120.4 1.0 copy-done.6
  121.3 7.5 %all-to-all-start.1 = ((bf16[32,16,4096]{2,1,0:T(8,128)(2,1)}), bf16[32,16,4096]{2,1,0:T(8,128)(2,1)}, u32[]{:S(2)}, u32[]{:S(2)}) async-start(bf16[32,16,4096]{2,1,0:T(8,128)(2,1)} %bitcast.40), calls=%async_computation.1 | async-start | bytes 8388608 | tf_op jit(solution)/shard_map/encode_decode/all_to_all | solution.py:11
  128.9 2.3 all_to_all.59
  131.2 46.5 %all-to-all-done.1 = bf16[32,16,4096]{2,1,0:T(8,128)(2,1)} async-done(((bf16[32,16,4096]{2,1,0:T(8,128)(2,1)}), bf16[32,16,4096]{2,1,0:T(8,128)(2,1)}, u32[]{:S(2)}, u32[]{:S(2)}) %all-to-all-start.1) | async-done | bytes 4194336 | tf_op jit(solution)/shard_map/encode_decode/all_to_all | solution.py:11
  177.7 3.0 convolution_add_fusion.4
  180.7 0.4 fusion.4
  181.1 1.5 convolution_convert_fusion.2
  182.6 2.3 all_to_all.63
  184.9 9.3 %all-to-all-start.5 = ((bf16[32,4,4096]{2,1,0:T(4,128)(2,1)}), bf16[32,4,4096]{2,1,0:T(4,128)(2,1)}, u32[]{:S(2)}, u32[]{:S(2)}) async-start(bf16[32,4,4096]{2,1,0:T(4,128)(2,1)} %all_to_all.63), calls=%async_computation.5 | async-start | bytes 2097152 | tf_op jit(solution)/shard_map/combine/all_to_all | solution.py:11
  194.2 3.3 convolution_convert_fusion
  197.5 11.4 %all-to-all-done.5 = bf16[32,4,4096]{2,1,0:T(4,128)(2,1)} async-done(((bf16[32,4,4096]{2,1,0:T(4,128)(2,1)}), bf16[32,4,4096]{2,1,0:T(4,128)(2,1)}, u32[]{:S(2)}, u32[]{:S(2)}) %all-to-all-start.5) | async-done | bytes 1048608 | tf_op jit(solution)/shard_map/combine/all_to_all | solution.py:11
  208.9 7.6 %all-to-all-start.4 = ((bf16[32,16,4096]{2,1,0:T(8,128)(2,1)}), bf16[32,16,4096]{2,1,0:T(8,128)(2,1)}, u32[]{:S(2)}, u32[]{:S(2)}) async-start(bf16[32,16,4096]{2,1,0:T(8,128)(2,1)} %bitcast.38), calls=%async_computation.4 | async-start | bytes 8388608 | tf_op jit(solution)/shard_map/combine/all_to_all | solution.py:11
  216.5 1.3 all_to_all.65
  217.9 0.8 fusion.56
  218.8 2.7 fusion.57
  221.5 2.7 fusion.29
  224.2 41.1 %all-to-all-done.4 = bf16[32,16,4096]{2,1,0:T(8,128)(2,1)} async-done(((bf16[32,16,4096]{2,1,0:T(8,128)(2,1)}), bf16[32,16,4096]{2,1,0:T(8,128)(2,1)}, u32[]{:S(2)}, u32[]{:S(2)}) %all-to-all-start.4) | async-done | bytes 4194336 | tf_op jit(solution)/shard_map/combine/all_to_all | solution.py:11
  265.3 3.5 %fusion.55 = (f32[256]{0:T(256)S(1)}, bf16[512,256]{1,0:T(8,128)(2,1)S(1)}) fusion(f32[512,256]{1,0:T(8,128)S(1)} %copy-done.15, s32[256]{0:T(256)S(1)} %copy-done.17, s32[512]{0:T(512)S(1)} %add_select_fusion.4, bf16[512,4096]{1,0:T(8,128)(2,1)} %bitcast.8, bf16[256,4096]{1,0:T(8,128)(2,1)S(1)} %copy-done), kind=kOutput, calls=%fused_computation.98 | convolution fusion | flops 1074396928 | bytes 7081984 | tf_op jit(solution)/shard_map/backward/dot_general | solution.py:102
  268.9 4.9 %fusion.2 = bf16[4096,256]{1,0:T(8,128)(2,1)S(1)} fusion(f32[4096,256]{1,0:T(8,128)} %fusion.57, bf16[512,4096]{1,0:T(8,128)(2,1)} %bitcast.8, bf16[512,256]{1,0:T(8,128)(2,1)S(1)} %copy-done.11), kind=kOutput, calls=%fused_computation.9 | convolution fusion | flops 1075838976 | bytes 10747904 | tf_op jit(solution)/shard_map/backward/dot_general | solution.py:111
  273.8 3.6 %fusion.3 = bf16[4096,256]{1,0:T(8,128)(2,1)S(1)} fusion(f32[4096,256]{1,0:T(8,128)S(1)} %copy-done.5, bf16[512,4224]{1,0:T(8,128)(2,1)} %bitcast.2, bf16[512,256]{1,0:T(8,128)(2,1)S(1)} %get-tuple-element.27), kind=kOutput, calls=%fused_computation.10 | convolution fusion | flops 1075838976 | bytes 10747904 | tf_op jit(solution)/shard_map/backward/dot_general | solution.py:107
  277.4 2.2 fusion.5
  279.6 59.7 %reduce-scatter.2.cloned.1.call-done = bf16[528,512]{1,0:T(8,128)(2,1)} async-done(((bf16[4224,512]{1,0:T(8,128)(2,1)}), bf16[528,512]{1,0:T(8,128)(2,1)}) %reduce-scatter.2.cloned.1.call-update) | async-done | bytes 540688 | tf_op jit(solution)/shard_map/grad_reduce/reduce_scatter | solution.py:135
  339.3 1.2 convert_element_type.131
  340.6 0.5 slice_bitcast_fusion.1
  341.1 1.0 copy.51
  342.1 0.8 slice.34
  (55 shorter events, 1.0 us)
Async XLA Ops:
  7.2 47.2 %copy-start = (bf16[256,4096]{1,0:T(8,128)(2,1)S(1)}, bf16[256,4096]{1,0:T(8,128)(2,1)}, u32[]{:S(2)}) copy-start(bf16[256,4096]{1,0:T(8,128)(2,1)} %param.12) | copy-start | bytes 6291460
  11.2 0.7 copy-start.14
  15.1 22.5 %all-to-all-start.2 = ((bf16[32,4,4224]{2,1,0:T(4,128)(2,1)}), bf16[32,4,4224]{2,1,0:T(4,128)(2,1)S(1)}, u32[]{:S(2)}, u32[]{:S(2)}) async-start(bf16[32,4,4224]{2,1,0:T(4,128)(2,1)} %all_to_all.54), calls=%async_computation.2 | async-start | bytes 2162688 | tf_op jit(solution)/shard_map/dispatch/all_to_all | solution.py:11
  37.6 1.0 copy-start.3
  37.6 8.5 %copy-start.20 = (bf16[256]{0:T(256)(128)(2,1)S(1)}, bf16[256]{0:T(256)(128)(2,1)}, u32[]{:S(2)}) copy-start(bf16[256]{0:T(256)(128)(2,1)} %param.11) | copy-start | bytes 1540
  38.6 58.0 %all-to-all-start = ((bf16[32,16,4224]{2,1,0:T(8,128)(2,1)}), bf16[32,16,4224]{2,1,0:T(8,128)(2,1)}, u32[]{:S(2)}, u32[]{:S(2)}) async-start(bf16[32,16,4224]{2,1,0:T(8,128)(2,1)} %bitcast.42), calls=%async_computation | async-start | bytes 8650752 | tf_op jit(solution)/shard_map/dispatch/all_to_all | solution.py:11
  49.0 6.8 %copy-start.1 = (bf16[128,4224]{1,0:T(8,128)(2,1)}, bf16[128,4224]{1,0:T(8,128)(2,1)S(1)}, u32[]{:S(2)}) copy-start(bf16[128,4224]{1,0:T(8,128)(2,1)S(1)} %all_to_all.56) | copy-start | bytes 3244036
  53.7 0.6 copy-start.12
  58.1 54.1 %copy-start.17 = (s32[256]{0:T(256)S(1)}, s32[256]{0:T(256)}, u32[]{:S(2)}) copy-start(s32[256]{0:T(256)} %and_select_fusion.1) | copy-start | bytes 3076
  58.1 54.1 %copy-start.19 = (f32[256]{0:T(256)S(1)}, f32[256]{0:T(256)}, u32[]{:S(2)}) copy-start(f32[256]{0:T(256)} %convert_element_type.112) | copy-start | bytes 3076
  96.6 23.7 %all-to-all-start.3 = ((bf16[32,4,4096]{2,1,0:T(4,128)(2,1)}), bf16[32,4,4096]{2,1,0:T(4,128)(2,1)S(1)}, u32[]{:S(2)}, u32[]{:S(2)}) async-start(bf16[32,4,4096]{2,1,0:T(4,128)(2,1)} %all_to_all.57), calls=%async_computation.3 | async-start | bytes 2097152 | tf_op jit(solution)/shard_map/encode_decode/all_to_all | solution.py:11
  116.4 0.7 copy-start.10
  120.4 1.0 copy-start.6
  120.4 8.5 %copy-start.16 = (bf16[4096]{0:T(1024)(128)(2,1)S(1)}, bf16[4096]{0:T(1024)(128)(2,1)}, u32[]{:S(2)}) copy-start(bf16[4096]{0:T(1024)(128)(2,1)} %param.13) | copy-start | bytes 24580
  121.3 56.3 %all-to-all-start.1 = ((bf16[32,16,4096]{2,1,0:T(8,128)(2,1)}), bf16[32,16,4096]{2,1,0:T(8,128)(2,1)}, u32[]{:S(2)}, u32[]{:S(2)}) async-start(bf16[32,16,4096]{2,1,0:T(8,128)(2,1)} %bitcast.40), calls=%async_computation.1 | async-start | bytes 8388608 | tf_op jit(solution)/shard_map/encode_decode/all_to_all | solution.py:11
  128.9 48.8 %copy-start.4 = (bf16[128,4096]{1,0:T(8,128)(2,1)S(1)}, bf16[128,4096]{1,0:T(8,128)(2,1)}, u32[]{:S(2)}) copy-start(bf16[128,4096]{1,0:T(8,128)(2,1)} %param.7) | copy-start | bytes 3145732
  177.7 3.0 copy-start.7
  184.9 24.0 %all-to-all-start.5 = ((bf16[32,4,4096]{2,1,0:T(4,128)(2,1)}), bf16[32,4,4096]{2,1,0:T(4,128)(2,1)}, u32[]{:S(2)}, u32[]{:S(2)}) async-start(bf16[32,4,4096]{2,1,0:T(4,128)(2,1)} %all_to_all.63), calls=%async_computation.5 | async-start | bytes 2097152 | tf_op jit(solution)/shard_map/combine/all_to_all | solution.py:11
  208.9 9.0 %copy-start.18 = (s32[128]{0:T(128)S(1)}, s32[128]{0:T(128)}, u32[]{:S(2)}) copy-start(s32[128]{0:T(128)} %and_select_fusion) | copy-start | bytes 1540
  208.9 56.3 %all-to-all-start.4 = ((bf16[32,16,4096]{2,1,0:T(8,128)(2,1)}), bf16[32,16,4096]{2,1,0:T(8,128)(2,1)}, u32[]{:S(2)}, u32[]{:S(2)}) async-start(bf16[32,16,4096]{2,1,0:T(8,128)(2,1)} %bitcast.38), calls=%async_computation.4 | async-start | bytes 8388608 | tf_op jit(solution)/shard_map/combine/all_to_all | solution.py:11
  216.5 1.4 copy-start.9
  216.5 122.8 %reduce-scatter.2.cloned.1.call-start = ((), (), s32[]{:S(2)}) async-start(), calls=%async_computation.7 | async-start | bytes 4866048 | tf_op jit(solution)/shard_map/grad_reduce/reduce_scatter | solution.py:135
  217.9 0.9 copy-start.13
  218.8 2.7 copy-start.2
  221.5 43.8 %copy-start.15 = (f32[512,256]{1,0:T(8,128)S(1)}, f32[512,256]{1,0:T(8,128)}, u32[]{:S(2)}) copy-start(f32[512,256]{1,0:T(8,128)} %copy.45) | copy-start | bytes 1572868
  265.3 3.6 %copy-start.11 = (bf16[512,256]{1,0:T(8,128)(2,1)S(1)}, bf16[512,256]{1,0:T(8,128)(2,1)}, u32[]{:S(2)}) copy-start(bf16[512,256]{1,0:T(8,128)(2,1)} %copy-done.10) | copy-start | bytes 786436
  268.9 4.9 %copy-start.5 = (f32[4096,256]{1,0:T(8,128)S(1)}, f32[4096,256]{1,0:T(8,128)}, u32[]{:S(2)}) copy-start(f32[4096,256]{1,0:T(8,128)} %fusion.29) | copy-start | bytes 12582916
  339.3 2.8 copy-start.8
Sparse Core Ops, SparseCore 0:
  279.8 59.4 reduce-scatter.1

commit v3 on v2

--- a/solution.py
+++ b/solution.py
@@ -94,7 +94,12 @@
                 token_to_slot[k], returned[k], preferred_element_type=jnp.float32
             )
         err_b = rebuilt.astype(jnp.bfloat16)
-        error_rows = [exchange(pick_rows(token_to_slot[k], err_b)) for k in range(len(rank_sets))]
+        error_rows = []
+        for k in range(len(rank_sets)):
+            send_err = pick_rows(token_to_slot[k], err_b)
+            if error_rows:
+                send_err = send_err + 0 * error_rows[0][:1, :1]
+            error_rows.append(exchange(send_err))
 
     with jax.named_scope("backward"):
         enc_grad = dec_grad_t = bias_grad = 0.0
@@ -113,6 +118,10 @@
                 preferred_element_type=jnp.float32,
             )
             bias_grad = bias_grad + jnp.sum(pre_grad, axis=0)
+            if k == 0:
+                enc_grad, dec_grad_t, bias_grad = lax.optimization_barrier(
+                    (enc_grad, dec_grad_t, bias_grad)
+                )
 
     with jax.named_scope("grad_reduce"):
         rows_per = model_width // n_batch

time: 352 us -> 352 us (level)
  blocking collectives: 0 us -> 56.3 us
  waiting for transfers between devices: 206 us -> 154 us
  starting transfers between devices: 48 us -> 39.2 us
    all_to_all x0 -> x1, blocking collectives: none -> 56.3 us  [exchange(): lax.all_to_all(rows, OWNER_AXES, split_axis=0, concat_axis=0, tiled=True)]
    all_to_all x6 -> x5, waiting for transfers between devices: 146 us -> 96 us  [exchange(): lax.all_to_all(rows, OWNER_AXES, split_axis=0, concat_axis=0, tiled=True)]
    all_to_all x6 -> x5, starting transfers between devices: 48 us -> 39.2 us  [exchange(): lax.all_to_all(rows, OWNER_AXES, split_axis=0, concat_axis=0, tiled=True)]
    unnamed x46 -> x44, local copies, waits for them, and re-layouts: 7.51 us -> 8.34 us
  transfers between devices with their start and end apart: 7 -> 6, of which waited for: 6 -> 5; matrix products, arithmetic and copies ran while one was open for 11% -> 12% of each run, Pallas kernels for 0% -> 0%
where the time goes in v3:
time: 352 us; the launch traced here: 350 us
  waiting for transfers between devices  154 us (44%)
  blocking collectives  56.3 us (16%)
  matrix products  47.8 us (14%)
  starting transfers between devices  39.2 us (11%)
  local copies, waits for them, and re-layouts  30.3 us (9%)
  between operations  15.1 us (4%)
  other arithmetic  7.43 us (2%)
    all_to_all x5, waiting for transfers between devices, exchange(): lax.all_to_all(rows, OWNER_AXES, split_axis=0, concat_axis=0, tiled=True)  96 us
    reduce_scatter x1, waiting for transfers between devices, shards(): lax.psum_scatter(stacked, 'batch', scatter_dimension=0, tiled=True)  58.3 us
    all_to_all x1, blocking collectives, exchange(): lax.all_to_all(rows, OWNER_AXES, split_axis=0, concat_axis=0, tiled=True)  56.3 us
    all_to_all x5, starting transfers between devices, exchange(): lax.all_to_all(rows, OWNER_AXES, split_axis=0, concat_axis=0, tiled=True)  39.2 us
    all_to_all x6, local copies, waits for them, and re-layouts, exchange(): lax.all_to_all(rows, OWNER_AXES, split_axis=0, concat_axis=0, tiled=True)  11.3 us
    dot_general x2, matrix products, shards(): lax.dot_general(error_rows[k], codes[k], (((0,), (0,)), ((), ())), prefer...  9.96 us
    dot_general x2, matrix products, shards(): lax.dot_general(payload[k], pre_grad_b, (((0,), (0,)), ((), ())), preferr...  8.54 us
    unnamed x44, local copies, waits for them, and re-layouts  8.34 us
  transfers between devices with their start and end apart: 6, of which 5 were waited for; matrix products, arithmetic and copies ran while one was open for 12% of the time, Pallas kernels for 0%

profile of v3, /device:TPU:6, one launch (start us, length us, event | category | flops | bytes accessed | tf_op | source)
XLA Modules:
  0.0 350.3 jit_solution(9780895434146979987)
XLA Ops:
  7.2 0.9 copy.33
  8.1 0.7 broadcast_compare_fusion
  8.9 0.3 convert_reduce_fusion.1
  9.5 0.1 and.121
  9.7 0.1 copy.39
  9.8 0.9 convert_element_type.97
  10.7 0.1 copy.42
  11.0 0.2 convert_reduce_fusion.2
  11.2 0.3 copy-done.13
  11.5 0.3 fusion.38
  11.9 1.7 fusion.1
  13.6 1.1 all_to_all.54
  14.7 7.6 %all-to-all-start.2 = ((bf16[32,4,4224]{2,1,0:T(4,128)(2,1)}), bf16[32,4,4224]{2,1,0:T(4,128)(2,1)S(1)}, u32[]{:S(2)}, u32[]{:S(2)}) async-start(bf16[32,4,4224]{2,1,0:T(4,128)(2,1)} %all_to_all.54), calls=%async_computation.2 | async-start | bytes 2162688 | tf_op jit(solution)/shard_map/dispatch/all_to_all | solution.py:11
  22.4 0.2 convert_reduce_fusion
  22.6 1.5 fusion.33
  24.0 4.6 %add_convert_fusion = bf16[512,4224]{1,0:T(8,128)(2,1)} fusion(f32[512,64]{1,0:T(8,128)S(1)} %fusion.33, bf16[128,4096]{1,0:T(8,128)(2,1)} %param.7, s32[128,512]{1,0:T(8,128)S(1)} %convert_reduce_fusion), kind=kOutput, calls=%fused_computation.1 | convolution fusion | flops 558039040 | bytes 5767168 | tf_op jit(solution)/shard_map/dispatch/dot_general | solution.py:64
  28.6 8.6 %all-to-all-done.2 = bf16[32,4,4224]{2,1,0:T(4,128)(2,1)S(1)} async-done(((bf16[32,4,4224]{2,1,0:T(4,128)(2,1)}), bf16[32,4,4224]{2,1,0:T(4,128)(2,1)S(1)}, u32[]{:S(2)}, u32[]{:S(2)}) %all-to-all-start.2) | async-done | bytes 1081376 | tf_op jit(solution)/shard_map/dispatch/all_to_all | solution.py:11
  37.3 1.0 copy-done.5
  38.3 7.5 %all-to-all-start = ((bf16[32,16,4224]{2,1,0:T(8,128)(2,1)}), bf16[32,16,4224]{2,1,0:T(8,128)(2,1)}, u32[]{:S(2)}, u32[]{:S(2)}) async-start(bf16[32,16,4224]{2,1,0:T(8,128)(2,1)} %bitcast.47), calls=%async_computation | async-start | bytes 8650752 | tf_op jit(solution)/shard_map/dispatch/all_to_all | solution.py:11
  45.8 0.6 convert_element_type.102
  46.3 0.5 and_select_fusion
  46.9 0.6 and_select_fusion.1
  47.4 1.3 all_to_all.56
  48.9 0.7 tile.20
  49.6 1.6 copy.49
  51.2 2.1 fusion.28
  53.4 0.6 copy-done.11
  54.0 1.4 convolution_convert_fusion.3
  55.4 2.3 all_to_all.57
  57.7 38.6 %all-to-all-done = bf16[32,16,4224]{2,1,0:T(8,128)(2,1)} async-done(((bf16[32,16,4224]{2,1,0:T(8,128)(2,1)}), bf16[32,16,4224]{2,1,0:T(8,128)(2,1)}, u32[]{:S(2)}, u32[]{:S(2)}) %all-to-all-start) | async-done | bytes 4325408 | tf_op jit(solution)/shard_map/dispatch/all_to_all | solution.py:11
  96.3 9.3 %all-to-all-start.3 = ((bf16[32,4,4096]{2,1,0:T(4,128)(2,1)}), bf16[32,4,4096]{2,1,0:T(4,128)(2,1)}, u32[]{:S(2)}, u32[]{:S(2)}) async-start(bf16[32,4,4096]{2,1,0:T(4,128)(2,1)} %all_to_all.57), calls=%async_computation.3 | async-start | bytes 2097152 | tf_op jit(solution)/shard_map/encode_decode/all_to_all | solution.py:11
  105.6 1.6 slice.35
  107.2 1.6 copy.54
  108.8 1.7 tile.8
  110.5 2.0 copy.45
  112.5 4.2 %fusion.19 = bf16[512,256]{1,0:T(8,128)(2,1)S(1)} fusion(bf16[512,4224]{1,0:T(8,128)(2,1)} %bitcast.2, bf16[4096,256]{1,0:T(8,128)(2,1)} %param.10, f32[512,256]{1,0:T(8,128)} %copy.45, s32[256]{0:T(256)S(1)} %copy-done.16, f32[256]{0:T(256)S(1)} %copy-done.18, s32[512]{0:T(512)S(1)} %add_select_fusion.4), kind=kOutput, calls=%fused_computation.27 | convolution fusion | flops 1107951616 | bytes 7213056 | tf_op jit(solution)/shard_map/encode_decode/dot_general | solution.py:80
  116.7 0.7 copy-done.9
  117.4 3.3 convolution_convert_fusion.1
  120.7 7.6 %all-to-all-start.1 = ((bf16[32,16,4096]{2,1,0:T(8,128)(2,1)}), bf16[32,16,4096]{2,1,0:T(8,128)(2,1)}, u32[]{:S(2)}, u32[]{:S(2)}) async-start(bf16[32,16,4096]{2,1,0:T(8,128)(2,1)} %bitcast.44), calls=%async_computation.1 | async-start | bytes 8388608 | tf_op jit(solution)/shard_map/encode_decode/all_to_all | solution.py:11
  128.4 2.1 all_to_all.59
  130.5 46.6 %all-to-all-done.1 = bf16[32,16,4096]{2,1,0:T(8,128)(2,1)} async-done(((bf16[32,16,4096]{2,1,0:T(8,128)(2,1)}), bf16[32,16,4096]{2,1,0:T(8,128)(2,1)}, u32[]{:S(2)}, u32[]{:S(2)}) %all-to-all-start.1) | async-done | bytes 4194336 | tf_op jit(solution)/shard_map/encode_decode/all_to_all | solution.py:11
  177.2 3.3 convolution_add_fusion.4
  180.5 0.4 fusion.4
  180.9 1.3 convolution_convert_fusion
  182.2 56.3 %all_to_all.72 = bf16[32,16,4096]{2,1,0:T(8,128)(2,1)S(1)} all-to-all(bf16[32,16,4096]{2,1,0:T(8,128)(2,1)S(1)} %bitcast.39), channel_id=1, replica_groups=mesh['loop'=4,'inner'=8,'batch'=8] {'loop','inner'}, dimensions={0} | all-to-all | bytes 8388608 | tf_op jit(solution)/shard_map/combine/all_to_all | solution.py:11
  238.5 2.0 copy-done.1
  240.5 0.6 slice.38
  241.7 1.5 fusion.5
  243.2 2.3 all_to_all.63
  245.5 7.2 %all-to-all-start.5 = ((bf16[32,4,4096]{2,1,0:T(4,128)(2,1)}), bf16[32,4,4096]{2,1,0:T(4,128)(2,1)}, u32[]{:S(2)}, u32[]{:S(2)}) async-start(bf16[32,4,4096]{2,1,0:T(4,128)(2,1)} %all_to_all.63), calls=%async_computation.5 | async-start | bytes 2097152 | tf_op jit(solution)/shard_map/combine/all_to_all | solution.py:11
  252.8 5.6 %fusion.58 = f32[4096,256]{1,0:T(8,128)} fusion(bf16[512,4096]{1,0:T(8,128)(2,1)} %bitcast.41, bf16[512,256]{1,0:T(8,128)(2,1)S(1)} %copy-done.10), kind=kOutput, calls=%fused_computation.101 | convolution fusion | flops 1073741824 | bytes 8650752 | tf_op jit(solution)/shard_map/backward/dot_general | solution.py:116
  258.4 1.4 fusion.56
  259.9 5.5 %fusion.7 = f32[4096,256]{1,0:T(8,128)} fusion(bf16[512,4224]{1,0:T(8,128)(2,1)} %bitcast.2, bf16[512,256]{1,0:T(8,128)(2,1)S(1)} %get-tuple-element.33), kind=kOutput, calls=%fused_computation.18 | convolution fusion | flops 1073741824 | bytes 8650752 | tf_op jit(solution)/shard_map/backward/dot_general | solution.py:112
  265.4 2.1 all-to-all-done.5
  267.5 2.1 all_to_all.65
  269.6 2.2 fusion.57
  271.8 4.3 %fusion.2 = bf16[4096,256]{1,0:T(8,128)(2,1)} fusion(f32[4096,256]{1,0:T(8,128)} %fusion.58, bf16[128,4096]{1,0:T(8,128)(2,1)S(1)} %copy-done.3, bf16[128,256]{1,0:T(8,128)(2,1)S(1)} %copy-done.12), kind=kOutput, calls=%fused_computation.9 | convolution fusion | flops 270532608 | bytes 7405568 | tf_op jit(solution)/shard_map/backward/dot_general | solution.py:116
  276.2 3.1 fusion.3
  279.3 2.2 fusion.6
  281.5 58.3 %reduce-scatter.2.cloned.1.call-done = bf16[528,512]{1,0:T(8,128)(2,1)} async-done(((bf16[4224,512]{1,0:T(8,128)(2,1)}), bf16[528,512]{1,0:T(8,128)(2,1)}) %reduce-scatter.2.cloned.1.call-update) | async-done | bytes 540688 | tf_op jit(solution)/shard_map/grad_reduce/reduce_scatter | solution.py:144
  339.8 1.2 convert_element_type.120
  341.1 0.5 slice_bitcast_fusion.1
  341.6 1.0 copy.51
  342.6 0.8 slice.39
  (53 shorter events, 1.0 us)
Async XLA Ops:
  7.2 46.8 %copy-start = (bf16[256,4096]{1,0:T(8,128)(2,1)S(1)}, bf16[256,4096]{1,0:T(8,128)(2,1)}, u32[]{:S(2)}) copy-start(bf16[256,4096]{1,0:T(8,128)(2,1)} %param.12) | copy-start | bytes 6291460
  10.9 0.7 copy-start.13
  14.7 22.5 %all-to-all-start.2 = ((bf16[32,4,4224]{2,1,0:T(4,128)(2,1)}), bf16[32,4,4224]{2,1,0:T(4,128)(2,1)S(1)}, u32[]{:S(2)}, u32[]{:S(2)}) async-start(bf16[32,4,4224]{2,1,0:T(4,128)(2,1)} %all_to_all.54), calls=%async_computation.2 | async-start | bytes 2162688 | tf_op jit(solution)/shard_map/dispatch/all_to_all | solution.py:11
  37.3 1.0 copy-start.5
  37.3 8.5 %copy-start.19 = (bf16[256]{0:T(256)(128)(2,1)S(1)}, bf16[256]{0:T(256)(128)(2,1)}, u32[]{:S(2)}) copy-start(bf16[256]{0:T(256)(128)(2,1)} %param.11) | copy-start | bytes 1540
  38.3 58.0 %all-to-all-start = ((bf16[32,16,4224]{2,1,0:T(8,128)(2,1)}), bf16[32,16,4224]{2,1,0:T(8,128)(2,1)}, u32[]{:S(2)}, u32[]{:S(2)}) async-start(bf16[32,16,4224]{2,1,0:T(8,128)(2,1)} %bitcast.47), calls=%async_computation | async-start | bytes 8650752 | tf_op jit(solution)/shard_map/dispatch/all_to_all | solution.py:11
  53.3 0.6 copy-start.11
  57.7 54.8 %copy-start.16 = (s32[256]{0:T(256)S(1)}, s32[256]{0:T(256)}, u32[]{:S(2)}) copy-start(s32[256]{0:T(256)} %and_select_fusion.1) | copy-start | bytes 3076
  57.7 54.8 %copy-start.18 = (f32[256]{0:T(256)S(1)}, f32[256]{0:T(256)}, u32[]{:S(2)}) copy-start(f32[256]{0:T(256)} %convert_element_type.102) | copy-start | bytes 3076
  96.3 24.4 %all-to-all-start.3 = ((bf16[32,4,4096]{2,1,0:T(4,128)(2,1)}), bf16[32,4,4096]{2,1,0:T(4,128)(2,1)}, u32[]{:S(2)}, u32[]{:S(2)}) async-start(bf16[32,4,4096]{2,1,0:T(4,128)(2,1)} %all_to_all.57), calls=%async_computation.3 | async-start | bytes 2097152 | tf_op jit(solution)/shard_map/encode_decode/all_to_all | solution.py:11
  116.7 0.7 copy-start.9
  120.7 7.7 %copy-start.15 = (bf16[4096]{0:T(1024)(128)(2,1)S(1)}, bf16[4096]{0:T(1024)(128)(2,1)}, u32[]{:S(2)}) copy-start(bf16[4096]{0:T(1024)(128)(2,1)} %param.13) | copy-start | bytes 24580
  120.7 56.5 %all-to-all-start.1 = ((bf16[32,16,4096]{2,1,0:T(8,128)(2,1)}), bf16[32,16,4096]{2,1,0:T(8,128)(2,1)}, u32[]{:S(2)}, u32[]{:S(2)}) async-start(bf16[32,16,4096]{2,1,0:T(8,128)(2,1)} %bitcast.44), calls=%async_computation.1 | async-start | bytes 8388608 | tf_op jit(solution)/shard_map/encode_decode/all_to_all | solution.py:11
  177.2 3.3 copy-start.6
  238.5 2.0 copy-start.1
  243.2 9.6 %copy-start.10 = (bf16[512,256]{1,0:T(8,128)(2,1)S(1)}, bf16[512,256]{1,0:T(8,128)(2,1)}, u32[]{:S(2)}) copy-start(bf16[512,256]{1,0:T(8,128)(2,1)} %copy-done.9) | copy-start | bytes 786436
  245.5 22.0 %all-to-all-start.5 = ((bf16[32,4,4096]{2,1,0:T(4,128)(2,1)}), bf16[32,4,4096]{2,1,0:T(4,128)(2,1)}, u32[]{:S(2)}, u32[]{:S(2)}) async-start(bf16[32,4,4096]{2,1,0:T(4,128)(2,1)} %all_to_all.63), calls=%async_computation.5 | async-start | bytes 2097152 | tf_op jit(solution)/shard_map/combine/all_to_all | solution.py:11
  252.7 87.1 %reduce-scatter.2.cloned.1.call-start = ((), (), s32[]{:S(2)}) async-start(), calls=%async_computation.7 | async-start | bytes 4866048 | tf_op jit(solution)/shard_map/grad_reduce/reduce_scatter | solution.py:144
  252.8 5.7 %copy-start.2 = (bf16[32,16,4096]{2,1,0:T(8,128)(2,1)S(1)}, bf16[32,16,4096]{2,1,0:T(8,128)(2,1)}, u32[]{:S(2)}) copy-start(bf16[32,16,4096]{2,1,0:T(8,128)(2,1)} %copy-done.1) | copy-start | bytes 12582916
  252.8 5.7 %copy-start.14 = (f32[512,256]{1,0:T(8,128)S(1)}, f32[512,256]{1,0:T(8,128)}, u32[]{:S(2)}) copy-start(f32[512,256]{1,0:T(8,128)} %copy.45) | copy-start | bytes 1572868
  259.9 9.7 %copy-start.17 = (s32[128]{0:T(128)S(1)}, s32[128]{0:T(128)}, u32[]{:S(2)}) copy-start(s32[128]{0:T(128)} %and_select_fusion) | copy-start | bytes 1540
  265.4 4.2 %copy-start.8 = (f32[128,256]{1,0:T(8,128)S(1)}, f32[128,256]{1,0:T(8,128)}, u32[]{:S(2)}) copy-start(f32[128,256]{1,0:T(8,128)} %copy.49) | copy-start | bytes 393220
  269.6 2.2 copy-start.3
  269.6 2.2 copy-start.12
  276.2 3.1 copy-start.4
  339.8 2.8 copy-start.7
Sparse Core Ops, SparseCore 0:
  281.7 58.1 reduce-scatter.1

commit v4 on v2

--- a/solution.py
+++ b/solution.py
@@ -97,22 +97,28 @@
         error_rows = [exchange(pick_rows(token_to_slot[k], err_b)) for k in range(len(rank_sets))]
 
     with jax.named_scope("backward"):
-        enc_grad = dec_grad_t = bias_grad = 0.0
+        enc_parts, dec_parts, bias_grad = [], [], 0.0
         for k in range(len(rank_sets)):
             pre_grad = lax.dot_general(
                 error_rows[k], dec_weight, (((1,), (1,)), ((), ())),
                 preferred_element_type=jnp.float32,
             ) * gates[k]
             pre_grad_b = pre_grad.astype(jnp.bfloat16)
-            enc_grad = enc_grad + lax.dot_general(
+            enc_parts.append(lax.dot_general(
                 payload[k], pre_grad_b, (((0,), (0,)), ((), ())),
                 preferred_element_type=jnp.float32,
-            )[:model_width]
-            dec_grad_t = dec_grad_t + lax.dot_general(
+            )[:model_width])
+            dec_parts.append(lax.dot_general(
                 error_rows[k], codes[k], (((0,), (0,)), ((), ())),
                 preferred_element_type=jnp.float32,
-            )
+            ))
             bias_grad = bias_grad + jnp.sum(pre_grad, axis=0)
+        enc_grad, dec_grad_t = enc_parts[0], dec_parts[0]
+        for k in range(1, len(rank_sets)):
+            enc_grad = enc_grad + enc_parts[k].astype(jnp.bfloat16).astype(jnp.float32)
+            dec_grad_t = dec_grad_t + dec_parts[k].astype(jnp.bfloat16).astype(jnp.float32)
+        enc_grad = enc_grad.astype(jnp.bfloat16)
+        dec_grad_t = dec_grad_t.astype(jnp.bfloat16)
 
     with jax.named_scope("grad_reduce"):
         rows_per = model_width // n_batch
@@ -120,8 +126,8 @@
         pad_rows = 16
         weights = jnp.concatenate(
             [
-                enc_grad.astype(jnp.bfloat16).reshape(n_batch, rows_per, local_lat),
-                dec_grad_t.astype(jnp.bfloat16).reshape(n_batch, rows_per, local_lat),
+                enc_grad.reshape(n_batch, rows_per, local_lat),
+                dec_grad_t.reshape(n_batch, rows_per, local_lat),
             ],
             axis=2,
         )

time: 352 us -> 351 us (level)
    unnamed x46 -> x44, local copies, waits for them, and re-layouts: 7.51 us -> 7.41 us
where the time goes in v4:
time: 351 us; the launch traced here: 349 us
  waiting for transfers between devices  206 us (59%)
  starting transfers between devices  48 us (14%)
  matrix products  45.1 us (13%)
  local copies, waits for them, and re-layouts  28.2 us (8%)
  between operations  14.4 us (4%)
  other arithmetic  7.42 us (2%)
    all_to_all x6, waiting for transfers between devices, exchange(): lax.all_to_all(rows, OWNER_AXES, split_axis=0, concat_axis=0, tiled=True)  146 us
    reduce_scatter x1, waiting for transfers between devices, shards(): lax.psum_scatter(stacked, 'batch', scatter_dimension=0, tiled=True)  59.6 us
    all_to_all x6, starting transfers between devices, exchange(): lax.all_to_all(rows, OWNER_AXES, split_axis=0, concat_axis=0, tiled=True)  48 us
    all_to_all x6, local copies, waits for them, and re-layouts, exchange(): lax.all_to_all(rows, OWNER_AXES, split_axis=0, concat_axis=0, tiled=True)  10.6 us
    dot_general x2, matrix products, shards(): lax.dot_general(error_rows[k], codes[k], (((0,), (0,)), ((), ())), prefer...  7.58 us
    unnamed x44, local copies, waits for them, and re-layouts  7.41 us
  transfers between devices with their start and end apart: 7, of which 6 were waited for; matrix products, arithmetic and copies ran while one was open for 11% of the time, Pallas kernels for 0%

profile of v4, /device:TPU:6, one launch (start us, length us, event | category | flops | bytes accessed | tf_op | source)
XLA Modules:
  0.0 349.2 jit_solution(16860901052475501563)
XLA Ops:
  7.2 0.9 copy.33
  8.1 0.7 broadcast_compare_fusion
  8.8 0.9 convert_element_type.117
  9.7 0.1 copy.42
  10.0 0.3 convert_reduce_fusion.1
  10.3 0.1 and.121
  10.5 0.1 copy.39
  11.0 0.2 convert_reduce_fusion.2
  11.2 0.3 fusion.36
  11.6 1.7 fusion.1
  13.3 1.2 all_to_all.54
  14.4 7.6 %all-to-all-start.2 = ((bf16[32,4,4224]{2,1,0:T(4,128)(2,1)}), bf16[32,4,4224]{2,1,0:T(4,128)(2,1)S(1)}, u32[]{:S(2)}, u32[]{:S(2)}) async-start(bf16[32,4,4224]{2,1,0:T(4,128)(2,1)} %all_to_all.54), calls=%async_computation.2 | async-start | bytes 2162688 | tf_op jit(solution)/shard_map/dispatch/all_to_all | solution.py:11
  22.1 0.2 convert_reduce_fusion
  22.3 1.5 fusion.31
  23.7 4.6 %add_convert_fusion = bf16[512,4224]{1,0:T(8,128)(2,1)} fusion(f32[512,64]{1,0:T(8,128)S(1)} %fusion.31, bf16[128,4096]{1,0:T(8,128)(2,1)} %param.7, s32[128,512]{1,0:T(8,128)S(1)} %convert_reduce_fusion), kind=kOutput, calls=%fused_computation.1 | convolution fusion | flops 558039040 | bytes 5767168 | tf_op jit(solution)/shard_map/dispatch/dot_general | solution.py:64
  28.3 8.6 %all-to-all-done.2 = bf16[32,4,4224]{2,1,0:T(4,128)(2,1)S(1)} async-done(((bf16[32,4,4224]{2,1,0:T(4,128)(2,1)}), bf16[32,4,4224]{2,1,0:T(4,128)(2,1)S(1)}, u32[]{:S(2)}, u32[]{:S(2)}) %all-to-all-start.2) | async-done | bytes 1081376 | tf_op jit(solution)/shard_map/dispatch/all_to_all | solution.py:11
  37.0 1.0 copy-done.3
  38.0 7.5 %all-to-all-start = ((bf16[32,16,4224]{2,1,0:T(8,128)(2,1)}), bf16[32,16,4224]{2,1,0:T(8,128)(2,1)}, u32[]{:S(2)}, u32[]{:S(2)}) async-start(bf16[32,16,4224]{2,1,0:T(8,128)(2,1)} %bitcast.43), calls=%async_computation | async-start | bytes 8650752 | tf_op jit(solution)/shard_map/dispatch/all_to_all | solution.py:11
  45.5 0.5 convert_element_type.122
  46.0 0.5 and_select_fusion
  46.5 0.6 and_select_fusion.1
  47.1 1.3 all_to_all.56
  48.6 0.9 tile.20
  49.4 1.6 copy.49
  51.1 2.1 fusion.27
  53.2 0.6 copy-done.12
  53.8 1.4 convolution_convert_fusion.4
  55.3 2.3 all_to_all.57
  57.5 38.5 %all-to-all-done = bf16[32,16,4224]{2,1,0:T(8,128)(2,1)} async-done(((bf16[32,16,4224]{2,1,0:T(8,128)(2,1)}), bf16[32,16,4224]{2,1,0:T(8,128)(2,1)}, u32[]{:S(2)}, u32[]{:S(2)}) %all-to-all-start) | async-done | bytes 4325408 | tf_op jit(solution)/shard_map/dispatch/all_to_all | solution.py:11
  96.0 8.6 %all-to-all-start.3 = ((bf16[32,4,4096]{2,1,0:T(4,128)(2,1)}), bf16[32,4,4096]{2,1,0:T(4,128)(2,1)S(1)}, u32[]{:S(2)}, u32[]{:S(2)}) async-start(bf16[32,4,4096]{2,1,0:T(4,128)(2,1)} %all_to_all.57), calls=%async_computation.3 | async-start | bytes 2097152 | tf_op jit(solution)/shard_map/encode_decode/all_to_all | solution.py:11
  104.6 1.6 slice.31
  106.2 1.6 copy.54
  107.8 1.7 tile.8
  109.5 2.0 copy.45
  111.5 4.2 %fusion.18 = bf16[512,256]{1,0:T(8,128)(2,1)S(1)} fusion(bf16[512,4224]{1,0:T(8,128)(2,1)} %bitcast.2, bf16[4096,256]{1,0:T(8,128)(2,1)} %param.10, f32[512,256]{1,0:T(8,128)} %copy.45, s32[256]{0:T(256)S(1)} %copy-done.16, f32[256]{0:T(256)S(1)} %copy-done.18, s32[512]{0:T(512)S(1)} %add_select_fusion.4), kind=kOutput, calls=%fused_computation.28 | convolution fusion | flops 1107951616 | bytes 7213056 | tf_op jit(solution)/shard_map/encode_decode/dot_general | solution.py:80
  115.8 0.7 copy-done.10
  116.5 3.3 convolution_convert_fusion.1
  119.8 1.0 copy-done.5
  120.8 7.5 %all-to-all-start.1 = ((bf16[32,16,4096]{2,1,0:T(8,128)(2,1)}), bf16[32,16,4096]{2,1,0:T(8,128)(2,1)}, u32[]{:S(2)}, u32[]{:S(2)}) async-start(bf16[32,16,4096]{2,1,0:T(8,128)(2,1)} %bitcast.41), calls=%async_computation.1 | async-start | bytes 8388608 | tf_op jit(solution)/shard_map/encode_decode/all_to_all | solution.py:11
  128.3 2.2 all_to_all.59
  130.5 46.5 %all-to-all-done.1 = bf16[32,16,4096]{2,1,0:T(8,128)(2,1)} async-done(((bf16[32,16,4096]{2,1,0:T(8,128)(2,1)}), bf16[32,16,4096]{2,1,0:T(8,128)(2,1)}, u32[]{:S(2)}, u32[]{:S(2)}) %all-to-all-start.1) | async-done | bytes 4194336 | tf_op jit(solution)/shard_map/encode_decode/all_to_all | solution.py:11
  177.1 3.0 convolution_add_fusion.4
  180.1 0.4 fusion.5
  180.5 1.5 convolution_convert_fusion.3
  182.0 2.3 all_to_all.63
  184.3 9.3 %all-to-all-start.5 = ((bf16[32,4,4096]{2,1,0:T(4,128)(2,1)}), bf16[32,4,4096]{2,1,0:T(4,128)(2,1)}, u32[]{:S(2)}, u32[]{:S(2)}) async-start(bf16[32,4,4096]{2,1,0:T(4,128)(2,1)} %all_to_all.63), calls=%async_computation.5 | async-start | bytes 2097152 | tf_op jit(solution)/shard_map/combine/all_to_all | solution.py:11
  193.6 3.3 convolution_convert_fusion
  196.9 11.4 %all-to-all-done.5 = bf16[32,4,4096]{2,1,0:T(4,128)(2,1)} async-done(((bf16[32,4,4096]{2,1,0:T(4,128)(2,1)}), bf16[32,4,4096]{2,1,0:T(4,128)(2,1)}, u32[]{:S(2)}, u32[]{:S(2)}) %all-to-all-start.5) | async-done | bytes 1048608 | tf_op jit(solution)/shard_map/combine/all_to_all | solution.py:11
  208.3 7.5 %all-to-all-start.4 = ((bf16[32,16,4096]{2,1,0:T(8,128)(2,1)}), bf16[32,16,4096]{2,1,0:T(8,128)(2,1)}, u32[]{:S(2)}, u32[]{:S(2)}) async-start(bf16[32,16,4096]{2,1,0:T(8,128)(2,1)} %bitcast.39), calls=%async_computation.4 | async-start | bytes 8388608 | tf_op jit(solution)/shard_map/combine/all_to_all | solution.py:11
  215.9 1.3 all_to_all.65
  217.3 0.9 fusion.56
  218.2 0.4 copy-done.2
  218.5 2.1 fusion.38
  220.7 2.7 fusion.4
  223.3 41.3 %all-to-all-done.4 = bf16[32,16,4096]{2,1,0:T(8,128)(2,1)} async-done(((bf16[32,16,4096]{2,1,0:T(8,128)(2,1)}), bf16[32,16,4096]{2,1,0:T(8,128)(2,1)}, u32[]{:S(2)}, u32[]{:S(2)}) %all-to-all-start.4) | async-done | bytes 4194336 | tf_op jit(solution)/shard_map/combine/all_to_all | solution.py:11
  264.6 3.7 %fusion.55 = (f32[256]{0:T(256)S(1)}, bf16[512,256]{1,0:T(8,128)(2,1)S(1)}) fusion(f32[512,256]{1,0:T(8,128)} %copy.45, s32[256]{0:T(256)S(1)} %copy-done.16, s32[512]{0:T(512)S(1)} %add_select_fusion.4, bf16[512,4096]{1,0:T(8,128)(2,1)} %bitcast.8, bf16[256,4096]{1,0:T(8,128)(2,1)S(1)} %copy-done), kind=kOutput, calls=%fused_computation.100 | convolution fusion | flops 1074396928 | bytes 7081984 | tf_op jit(solution)/shard_map/backward/dot_general | solution.py:102
  268.4 4.9 %fusion.2 = bf16[4096,256]{1,0:T(8,128)(2,1)S(1)} fusion(f32[4096,256]{1,0:T(8,128)} %fusion.4, bf16[512,4096]{1,0:T(8,128)(2,1)} %bitcast.8, bf16[512,256]{1,0:T(8,128)(2,1)S(1)} %copy-done.11), kind=kOutput, calls=%fused_computation.9 | convolution fusion | flops 1075838976 | bytes 10747904 | tf_op jit(solution)/shard_map/backward/dot_general | solution.py:111
  273.3 3.5 %fusion.3 = bf16[4096,256]{1,0:T(8,128)(2,1)S(1)} fusion(bf16[512,4224]{1,0:T(8,128)(2,1)} %bitcast.2, bf16[4224,256]{1,0:T(8,128)(2,1)S(1)} %copy-done.7, bf16[512,256]{1,0:T(8,128)(2,1)S(1)} %get-tuple-element.27), kind=kOutput, calls=%fused_computation.10 | convolution fusion | flops 1076887552 | bytes 8650752 | tf_op jit(solution)/shard_map/backward/dot_general | solution.py:107
  276.8 2.2 fusion.6
  279.1 59.6 %reduce-scatter.2.cloned.1.call-done = bf16[528,512]{1,0:T(8,128)(2,1)} async-done(((bf16[4224,512]{1,0:T(8,128)(2,1)}), bf16[528,512]{1,0:T(8,128)(2,1)}) %reduce-scatter.2.cloned.1.call-update) | async-done | bytes 540688 | tf_op jit(solution)/shard_map/grad_reduce/reduce_scatter | solution.py:141
  338.7 1.2 convert_element_type.144
  340.0 0.5 slice_bitcast_fusion.1
  340.5 1.0 copy.51
  341.5 0.8 slice.34
  (53 shorter events, 1.0 us)
Async XLA Ops:
  7.2 46.7 %copy-start = (bf16[256,4096]{1,0:T(8,128)(2,1)S(1)}, bf16[256,4096]{1,0:T(8,128)(2,1)}, u32[]{:S(2)}) copy-start(bf16[256,4096]{1,0:T(8,128)(2,1)} %param.12) | copy-start | bytes 6291460
  9.9 1.3 copy-start.14
  14.4 22.5 %all-to-all-start.2 = ((bf16[32,4,4224]{2,1,0:T(4,128)(2,1)}), bf16[32,4,4224]{2,1,0:T(4,128)(2,1)S(1)}, u32[]{:S(2)}, u32[]{:S(2)}) async-start(bf16[32,4,4224]{2,1,0:T(4,128)(2,1)} %all_to_all.54), calls=%async_computation.2 | async-start | bytes 2162688 | tf_op jit(solution)/shard_map/dispatch/all_to_all | solution.py:11
  37.0 1.0 copy-start.3
  37.0 8.5 %copy-start.19 = (bf16[256]{0:T(256)(128)(2,1)S(1)}, bf16[256]{0:T(256)(128)(2,1)}, u32[]{:S(2)}) copy-start(bf16[256]{0:T(256)(128)(2,1)} %param.11) | copy-start | bytes 1540
  38.0 58.0 %all-to-all-start = ((bf16[32,16,4224]{2,1,0:T(8,128)(2,1)}), bf16[32,16,4224]{2,1,0:T(8,128)(2,1)}, u32[]{:S(2)}, u32[]{:S(2)}) async-start(bf16[32,16,4224]{2,1,0:T(8,128)(2,1)} %bitcast.43), calls=%async_computation | async-start | bytes 8650752 | tf_op jit(solution)/shard_map/dispatch/all_to_all | solution.py:11
  48.4 6.8 %copy-start.1 = (bf16[128,4224]{1,0:T(8,128)(2,1)}, bf16[128,4224]{1,0:T(8,128)(2,1)S(1)}, u32[]{:S(2)}) copy-start(bf16[128,4224]{1,0:T(8,128)(2,1)S(1)} %all_to_all.56) | copy-start | bytes 3244036
  53.2 0.6 copy-start.12
  57.5 54.0 %copy-start.16 = (s32[256]{0:T(256)S(1)}, s32[256]{0:T(256)}, u32[]{:S(2)}) copy-start(s32[256]{0:T(256)} %and_select_fusion.1) | copy-start | bytes 3076
  57.5 54.0 %copy-start.18 = (f32[256]{0:T(256)S(1)}, f32[256]{0:T(256)}, u32[]{:S(2)}) copy-start(f32[256]{0:T(256)} %convert_element_type.122) | copy-start | bytes 3076
  96.0 23.8 %all-to-all-start.3 = ((bf16[32,4,4096]{2,1,0:T(4,128)(2,1)}), bf16[32,4,4096]{2,1,0:T(4,128)(2,1)S(1)}, u32[]{:S(2)}, u32[]{:S(2)}) async-start(bf16[32,4,4096]{2,1,0:T(4,128)(2,1)} %all_to_all.57), calls=%async_computation.3 | async-start | bytes 2097152 | tf_op jit(solution)/shard_map/encode_decode/all_to_all | solution.py:11
  115.7 0.7 copy-start.10
  119.7 1.0 copy-start.5
  119.7 8.5 %copy-start.15 = (bf16[4096]{0:T(1024)(128)(2,1)S(1)}, bf16[4096]{0:T(1024)(128)(2,1)}, u32[]{:S(2)}) copy-start(bf16[4096]{0:T(1024)(128)(2,1)} %param.13) | copy-start | bytes 24580
  120.8 56.3 %all-to-all-start.1 = ((bf16[32,16,4096]{2,1,0:T(8,128)(2,1)}), bf16[32,16,4096]{2,1,0:T(8,128)(2,1)}, u32[]{:S(2)}, u32[]{:S(2)}) async-start(bf16[32,16,4096]{2,1,0:T(8,128)(2,1)} %bitcast.41), calls=%async_computation.1 | async-start | bytes 8388608 | tf_op jit(solution)/shard_map/encode_decode/all_to_all | solution.py:11
  128.3 48.8 %copy-start.4 = (bf16[128,4096]{1,0:T(8,128)(2,1)S(1)}, bf16[128,4096]{1,0:T(8,128)(2,1)}, u32[]{:S(2)}) copy-start(bf16[128,4096]{1,0:T(8,128)(2,1)} %param.7) | copy-start | bytes 3145732
  177.1 3.0 copy-start.6
  184.3 24.0 %all-to-all-start.5 = ((bf16[32,4,4096]{2,1,0:T(4,128)(2,1)}), bf16[32,4,4096]{2,1,0:T(4,128)(2,1)}, u32[]{:S(2)}, u32[]{:S(2)}) async-start(bf16[32,4,4096]{2,1,0:T(4,128)(2,1)} %all_to_all.63), calls=%async_computation.5 | async-start | bytes 2097152 | tf_op jit(solution)/shard_map/combine/all_to_all | solution.py:11
  208.3 9.0 %copy-start.17 = (s32[128]{0:T(128)S(1)}, s32[128]{0:T(128)}, u32[]{:S(2)}) copy-start(s32[128]{0:T(128)} %and_select_fusion) | copy-start | bytes 1540
  208.3 56.3 %all-to-all-start.4 = ((bf16[32,16,4096]{2,1,0:T(8,128)(2,1)}), bf16[32,16,4096]{2,1,0:T(8,128)(2,1)}, u32[]{:S(2)}, u32[]{:S(2)}) async-start(bf16[32,16,4096]{2,1,0:T(8,128)(2,1)} %bitcast.39), calls=%async_computation.4 | async-start | bytes 8388608 | tf_op jit(solution)/shard_map/combine/all_to_all | solution.py:11
  215.9 1.4 copy-start.9
  215.9 122.8 %reduce-scatter.2.cloned.1.call-start = ((), (), s32[]{:S(2)}) async-start(), calls=%async_computation.7 | async-start | bytes 4866048 | tf_op jit(solution)/shard_map/grad_reduce/reduce_scatter | solution.py:141
  217.3 1.2 copy-start.2
  218.2 2.5 copy-start.13
  264.6 3.8 %copy-start.11 = (bf16[512,256]{1,0:T(8,128)(2,1)S(1)}, bf16[512,256]{1,0:T(8,128)(2,1)}, u32[]{:S(2)}) copy-start(bf16[512,256]{1,0:T(8,128)(2,1)} %copy-done.10) | copy-start | bytes 786436
  268.4 4.9 %copy-start.7 = (bf16[4224,256]{1,0:T(8,128)(2,1)S(1)}, bf16[4224,256]{1,0:T(8,128)(2,1)}, u32[]{:S(2)}) copy-start(bf16[4224,256]{1,0:T(8,128)(2,1)} %fusion.38) | copy-start | bytes 6488068
  338.7 2.8 copy-start.8
Sparse Core Ops, SparseCore 0:
  279.2 59.4 reduce-scatter.1

commit v5 on v3

--- a/solution.py
+++ b/solution.py
@@ -119,9 +119,10 @@
             )
             bias_grad = bias_grad + jnp.sum(pre_grad, axis=0)
             if k == 0:
-                enc_grad, dec_grad_t, bias_grad = lax.optimization_barrier(
-                    (enc_grad, dec_grad_t, bias_grad)
+                enc_b, dec_b, bias_grad = lax.optimization_barrier(
+                    (enc_grad.astype(jnp.bfloat16), dec_grad_t.astype(jnp.bfloat16), bias_grad)
                 )
+                enc_grad, dec_grad_t = enc_b.astype(jnp.float32), dec_b.astype(jnp.float32)
 
     with jax.named_scope("grad_reduce"):
         rows_per = model_width // n_batch

time: 352 us -> 350 us (level)
  matrix products: 47.8 us -> 42.3 us
    dot_general x2, matrix products: 9.96 us -> 4.69 us  [shards(): lax.dot_general(error_rows[k], codes[k], (((0,), (0,)), ((), ())), prefer...]
  transfers between devices with their start and end apart: 6 -> 6, of which waited for: 5 -> 5; matrix products, arithmetic and copies ran while one was open for 12% -> 11% of each run, Pallas kernels for 0% -> 0%
where the time goes in v5:
time: 350 us; the launch traced here: 347 us
  waiting for transfers between devices  154 us (44%)
  blocking collectives  56.3 us (16%)
  matrix products  42.3 us (12%)
  starting transfers between devices  39.2 us (11%)
  local copies, waits for them, and re-layouts  33.2 us (9%)
  between operations  15 us (4%)
  other arithmetic  7.43 us (2%)
    all_to_all x5, waiting for transfers between devices, exchange(): lax.all_to_all(rows, OWNER_AXES, split_axis=0, concat_axis=0, tiled=True)  95.8 us
    reduce_scatter x1, waiting for transfers between devices, shards(): lax.psum_scatter(stacked, 'batch', scatter_dimension=0, tiled=True)  58.3 us
    all_to_all x1, blocking collectives, exchange(): lax.all_to_all(rows, OWNER_AXES, split_axis=0, concat_axis=0, tiled=True)  56.3 us
    all_to_all x5, starting transfers between devices, exchange(): lax.all_to_all(rows, OWNER_AXES, split_axis=0, concat_axis=0, tiled=True)  39.2 us
    all_to_all x6, local copies, waits for them, and re-layouts, exchange(): lax.all_to_all(rows, OWNER_AXES, split_axis=0, concat_axis=0, tiled=True)  11.3 us
    unnamed x44, local copies, waits for them, and re-layouts  9.83 us
  transfers between devices with their start and end apart: 6, of which 5 were waited for; matrix products, arithmetic and copies ran while one was open for 11% of the time, Pallas kernels for 0%

profile of v5, /device:TPU:6, one launch (start us, length us, event | category | flops | bytes accessed | tf_op | source)
XLA Modules:
  0.0 347.5 jit_solution(18417753919312433760)
XLA Ops:
  7.2 0.9 copy.33
  8.1 0.7 broadcast_compare_fusion
  8.9 0.3 convert_reduce_fusion.1
  9.7 0.1 copy.39
  9.8 0.9 convert_element_type.107
  11.0 0.2 convert_reduce_fusion.2
  11.2 0.3 copy-done.12
  11.5 0.3 fusion.37
  11.9 1.7 fusion.1
  13.6 1.1 all_to_all.54
  14.7 7.6 %all-to-all-start.2 = ((bf16[32,4,4224]{2,1,0:T(4,128)(2,1)}), bf16[32,4,4224]{2,1,0:T(4,128)(2,1)S(1)}, u32[]{:S(2)}, u32[]{:S(2)}) async-start(bf16[32,4,4224]{2,1,0:T(4,128)(2,1)} %all_to_all.54), calls=%async_computation.2 | async-start | bytes 2162688 | tf_op jit(solution)/shard_map/dispatch/all_to_all | solution.py:11
  22.4 0.2 convert_reduce_fusion
  22.6 1.5 fusion.31
  24.0 4.6 %add_convert_fusion = bf16[512,4224]{1,0:T(8,128)(2,1)} fusion(f32[512,64]{1,0:T(8,128)S(1)} %fusion.31, bf16[128,4096]{1,0:T(8,128)(2,1)} %param.7, s32[128,512]{1,0:T(8,128)S(1)} %convert_reduce_fusion), kind=kOutput, calls=%fused_computation.1 | convolution fusion | flops 558039040 | bytes 5767168 | tf_op jit(solution)/shard_map/dispatch/dot_general | solution.py:64
  28.6 8.6 %all-to-all-done.2 = bf16[32,4,4224]{2,1,0:T(4,128)(2,1)S(1)} async-done(((bf16[32,4,4224]{2,1,0:T(4,128)(2,1)}), bf16[32,4,4224]{2,1,0:T(4,128)(2,1)S(1)}, u32[]{:S(2)}, u32[]{:S(2)}) %all-to-all-start.2) | async-done | bytes 1081376 | tf_op jit(solution)/shard_map/dispatch/all_to_all | solution.py:11
  37.3 1.0 copy-done.3
  38.3 7.5 %all-to-all-start = ((bf16[32,16,4224]{2,1,0:T(8,128)(2,1)}), bf16[32,16,4224]{2,1,0:T(8,128)(2,1)}, u32[]{:S(2)}, u32[]{:S(2)}) async-start(bf16[32,16,4224]{2,1,0:T(8,128)(2,1)} %bitcast.45), calls=%async_computation | async-start | bytes 8650752 | tf_op jit(solution)/shard_map/dispatch/all_to_all | solution.py:11
  45.8 0.6 convert_element_type.112
  46.3 0.5 and_select_fusion
  46.9 0.6 and_select_fusion.1
  47.4 1.3 all_to_all.56
  48.9 0.7 tile.20
  49.6 1.6 copy.49
  51.2 2.1 fusion.26
  53.4 0.6 copy-done.10
  54.0 1.4 convolution_convert_fusion.4
  55.4 2.3 all_to_all.57
  57.7 38.6 %all-to-all-done = bf16[32,16,4224]{2,1,0:T(8,128)(2,1)} async-done(((bf16[32,16,4224]{2,1,0:T(8,128)(2,1)}), bf16[32,16,4224]{2,1,0:T(8,128)(2,1)}, u32[]{:S(2)}, u32[]{:S(2)}) %all-to-all-start) | async-done | bytes 4325408 | tf_op jit(solution)/shard_map/dispatch/all_to_all | solution.py:11
  96.3 9.3 %all-to-all-start.3 = ((bf16[32,4,4096]{2,1,0:T(4,128)(2,1)}), bf16[32,4,4096]{2,1,0:T(4,128)(2,1)}, u32[]{:S(2)}, u32[]{:S(2)}) async-start(bf16[32,4,4096]{2,1,0:T(4,128)(2,1)} %all_to_all.57), calls=%async_computation.3 | async-start | bytes 2097152 | tf_op jit(solution)/shard_map/encode_decode/all_to_all | solution.py:11
  105.6 1.6 slice.34
  107.2 1.6 copy.54
  108.8 1.7 tile.8
  110.5 2.0 copy.45
  112.5 4.2 %fusion.17 = bf16[512,256]{1,0:T(8,128)(2,1)S(1)} fusion(bf16[512,4224]{1,0:T(8,128)(2,1)} %bitcast.2, bf16[4096,256]{1,0:T(8,128)(2,1)} %param.10, f32[512,256]{1,0:T(8,128)} %copy.45, s32[256]{0:T(256)S(1)} %copy-done.16, f32[256]{0:T(256)S(1)} %copy-done.18, s32[512]{0:T(512)S(1)} %add_select_fusion.4), kind=kOutput, calls=%fused_computation.27 | convolution fusion | flops 1107951616 | bytes 7213056 | tf_op jit(solution)/shard_map/encode_decode/dot_general | solution.py:80
  116.7 0.7 copy-done.13
  117.4 3.3 convolution_convert_fusion.1
  120.7 7.6 %all-to-all-start.1 = ((bf16[32,16,4096]{2,1,0:T(8,128)(2,1)}), bf16[32,16,4096]{2,1,0:T(8,128)(2,1)}, u32[]{:S(2)}, u32[]{:S(2)}) async-start(bf16[32,16,4096]{2,1,0:T(8,128)(2,1)} %bitcast.42), calls=%async_computation.1 | async-start | bytes 8388608 | tf_op jit(solution)/shard_map/encode_decode/all_to_all | solution.py:11
  128.4 2.1 all_to_all.59
  130.5 46.6 %all-to-all-done.1 = bf16[32,16,4096]{2,1,0:T(8,128)(2,1)} async-done(((bf16[32,16,4096]{2,1,0:T(8,128)(2,1)}), bf16[32,16,4096]{2,1,0:T(8,128)(2,1)}, u32[]{:S(2)}, u32[]{:S(2)}) %all-to-all-start.1) | async-done | bytes 4194336 | tf_op jit(solution)/shard_map/encode_decode/all_to_all | solution.py:11
  177.2 3.3 convolution_add_fusion.4
  180.5 0.4 fusion.4
  180.9 1.3 convolution_convert_fusion
  182.2 56.3 %all_to_all.72 = bf16[32,16,4096]{2,1,0:T(8,128)(2,1)S(1)} all-to-all(bf16[32,16,4096]{2,1,0:T(8,128)(2,1)S(1)} %bitcast.40), channel_id=1, replica_groups=mesh['loop'=4,'inner'=8,'batch'=8] {'loop','inner'}, dimensions={0} | all-to-all | bytes 8388608 | tf_op jit(solution)/shard_map/combine/all_to_all | solution.py:11
  238.5 2.0 copy-done.4
  240.5 0.5 slice.38
  241.6 1.5 fusion.5
  243.2 2.3 all_to_all.63
  245.4 7.2 %all-to-all-start.5 = ((bf16[32,4,4096]{2,1,0:T(4,128)(2,1)}), bf16[32,4,4096]{2,1,0:T(4,128)(2,1)}, u32[]{:S(2)}, u32[]{:S(2)}) async-start(bf16[32,4,4096]{2,1,0:T(4,128)(2,1)} %all_to_all.63), calls=%async_computation.5 | async-start | bytes 2097152 | tf_op jit(solution)/shard_map/combine/all_to_all | solution.py:11
  252.7 3.6 %fusion.55 = (f32[256]{0:T(256)S(1)}, bf16[512,256]{1,0:T(8,128)(2,1)S(1)}) fusion(f32[512,256]{1,0:T(8,128)} %copy.45, s32[256]{0:T(256)S(1)} %copy-done.16, s32[512]{0:T(512)S(1)} %add_select_fusion.4, bf16[512,4096]{1,0:T(8,128)(2,1)} %bitcast.47, bf16[256,4096]{1,0:T(8,128)(2,1)S(1)} %copy-done), kind=kOutput, calls=%fused_computation.100 | convolution fusion | flops 1074396928 | bytes 7081984 | tf_op jit(solution)/shard_map/backward/dot_general | solution.py:107
  256.3 3.6 %fusion.35 = bf16[4224,256]{1,0:T(8,128)(2,1)S(1)} fusion(bf16[512,4224]{1,0:T(8,128)(2,1)} %bitcast.2, bf16[512,256]{1,0:T(8,128)(2,1)S(1)} %get-tuple-element.33), kind=kOutput, calls=%fused_computation.45 | convolution fusion | flops 1107296256 | bytes 6750208 | tf_op jit(solution)/shard_map/backward/dot_general | solution.py:112
  260.0 1.5 slice.47
  261.4 1.5 copy-done.5
  262.9 2.6 convolution_convert_fusion.2
  265.5 1.9 all-to-all-done.5
  267.4 2.1 all_to_all.65
  269.6 2.2 fusion.56
  271.8 2.1 fusion.2
  274.0 2.5 fusion.3
  276.5 2.2 fusion.6
  278.7 58.3 %reduce-scatter.2.cloned.1.call-done = bf16[528,512]{1,0:T(8,128)(2,1)} async-done(((bf16[4224,512]{1,0:T(8,128)(2,1)}), bf16[528,512]{1,0:T(8,128)(2,1)}) %reduce-scatter.2.cloned.1.call-update) | async-done | bytes 540688 | tf_op jit(solution)/shard_map/grad_reduce/reduce_scatter | solution.py:145
  337.0 1.2 convert_element_type.133
  338.3 0.5 slice_bitcast_fusion.1
  338.8 1.0 copy.51
  339.8 0.8 slice.39
  (54 shorter events, 1.3 us)
Async XLA Ops:
  7.2 46.8 %copy-start = (bf16[256,4096]{1,0:T(8,128)(2,1)S(1)}, bf16[256,4096]{1,0:T(8,128)(2,1)}, u32[]{:S(2)}) copy-start(bf16[256,4096]{1,0:T(8,128)(2,1)} %param.12) | copy-start | bytes 6291460
  10.9 0.7 copy-start.12
  14.7 22.5 %all-to-all-start.2 = ((bf16[32,4,4224]{2,1,0:T(4,128)(2,1)}), bf16[32,4,4224]{2,1,0:T(4,128)(2,1)S(1)}, u32[]{:S(2)}, u32[]{:S(2)}) async-start(bf16[32,4,4224]{2,1,0:T(4,128)(2,1)} %all_to_all.54), calls=%async_computation.2 | async-start | bytes 2162688 | tf_op jit(solution)/shard_map/dispatch/all_to_all | solution.py:11
  37.3 1.0 copy-start.3
  37.3 8.5 %copy-start.19 = (bf16[256]{0:T(256)(128)(2,1)S(1)}, bf16[256]{0:T(256)(128)(2,1)}, u32[]{:S(2)}) copy-start(bf16[256]{0:T(256)(128)(2,1)} %param.11) | copy-start | bytes 1540
  38.3 58.0 %all-to-all-start = ((bf16[32,16,4224]{2,1,0:T(8,128)(2,1)}), bf16[32,16,4224]{2,1,0:T(8,128)(2,1)}, u32[]{:S(2)}, u32[]{:S(2)}) async-start(bf16[32,16,4224]{2,1,0:T(8,128)(2,1)} %bitcast.45), calls=%async_computation | async-start | bytes 8650752 | tf_op jit(solution)/shard_map/dispatch/all_to_all | solution.py:11
  53.3 0.6 copy-start.10
  57.7 54.8 %copy-start.16 = (s32[256]{0:T(256)S(1)}, s32[256]{0:T(256)}, u32[]{:S(2)}) copy-start(s32[256]{0:T(256)} %and_select_fusion.1) | copy-start | bytes 3076
  57.7 54.8 %copy-start.18 = (f32[256]{0:T(256)S(1)}, f32[256]{0:T(256)}, u32[]{:S(2)}) copy-start(f32[256]{0:T(256)} %convert_element_type.112) | copy-start | bytes 3076
  96.3 24.4 %all-to-all-start.3 = ((bf16[32,4,4096]{2,1,0:T(4,128)(2,1)}), bf16[32,4,4096]{2,1,0:T(4,128)(2,1)}, u32[]{:S(2)}, u32[]{:S(2)}) async-start(bf16[32,4,4096]{2,1,0:T(4,128)(2,1)} %all_to_all.57), calls=%async_computation.3 | async-start | bytes 2097152 | tf_op jit(solution)/shard_map/encode_decode/all_to_all | solution.py:11
  116.7 0.7 copy-start.13
  120.7 7.7 %copy-start.15 = (bf16[4096]{0:T(1024)(128)(2,1)S(1)}, bf16[4096]{0:T(1024)(128)(2,1)}, u32[]{:S(2)}) copy-start(bf16[4096]{0:T(1024)(128)(2,1)} %param.13) | copy-start | bytes 24580
  120.7 56.5 %all-to-all-start.1 = ((bf16[32,16,4096]{2,1,0:T(8,128)(2,1)}), bf16[32,16,4096]{2,1,0:T(8,128)(2,1)}, u32[]{:S(2)}, u32[]{:S(2)}) async-start(bf16[32,16,4096]{2,1,0:T(8,128)(2,1)} %bitcast.42), calls=%async_computation.1 | async-start | bytes 8388608 | tf_op jit(solution)/shard_map/encode_decode/all_to_all | solution.py:11
  177.2 3.3 copy-start.6
  238.5 2.0 copy-start.4
  245.4 22.0 %all-to-all-start.5 = ((bf16[32,4,4096]{2,1,0:T(4,128)(2,1)}), bf16[32,4,4096]{2,1,0:T(4,128)(2,1)}, u32[]{:S(2)}, u32[]{:S(2)}) async-start(bf16[32,4,4096]{2,1,0:T(4,128)(2,1)} %all_to_all.63), calls=%async_computation.5 | async-start | bytes 2097152 | tf_op jit(solution)/shard_map/combine/all_to_all | solution.py:11
  252.6 84.3 %reduce-scatter.2.cloned.1.call-start = ((), (), s32[]{:S(2)}) async-start(), calls=%async_computation.7 | async-start | bytes 4866048 | tf_op jit(solution)/shard_map/grad_reduce/reduce_scatter | solution.py:145
  256.3 5.1 %copy-start.14 = (bf16[512,256]{1,0:T(8,128)(2,1)S(1)}, bf16[512,256]{1,0:T(8,128)(2,1)}, u32[]{:S(2)}) copy-start(bf16[512,256]{1,0:T(8,128)(2,1)} %copy-done.13) | copy-start | bytes 786436
  259.9 2.9 copy-start.5
  262.9 6.7 %copy-start.17 = (s32[128]{0:T(128)S(1)}, s32[128]{0:T(128)}, u32[]{:S(2)}) copy-start(s32[128]{0:T(128)} %and_select_fusion) | copy-start | bytes 1540
  265.5 4.0 %copy-start.9 = (f32[128,256]{1,0:T(8,128)S(1)}, f32[128,256]{1,0:T(8,128)}, u32[]{:S(2)}) copy-start(f32[128,256]{1,0:T(8,128)} %copy.49) | copy-start | bytes 393220
  269.5 2.3 copy-start.1
  269.6 2.3 copy-start.8
  269.6 2.3 copy-start.11
  274.0 2.5 copy-start.2
  337.0 2.8 copy-start.7
Sparse Core Ops, SparseCore 0:
  278.8 58.1 reduce-scatter.1

commit v6 on v5

--- a/solution.py
+++ b/solution.py
@@ -94,12 +94,11 @@
                 token_to_slot[k], returned[k], preferred_element_type=jnp.float32
             )
         err_b = rebuilt.astype(jnp.bfloat16)
-        error_rows = []
-        for k in range(len(rank_sets)):
-            send_err = pick_rows(token_to_slot[k], err_b)
-            if error_rows:
-                send_err = send_err + 0 * error_rows[0][:1, :1]
-            error_rows.append(exchange(send_err))
+        send_err = [pick_rows(token_to_slot[k], err_b) for k in range(len(rank_sets))]
+        error_rows = [exchange(send_err[0])]
+        held, rest = lax.optimization_barrier((error_rows[0], send_err[1:]))
+        error_rows[0] = held
+        error_rows += [exchange(r) for r in rest]
 
     with jax.named_scope("backward"):
         enc_grad = dec_grad_t = bias_grad = 0.0

time: 350 us -> 351 us (level)
  blocking collectives: 56.3 us -> 0 us
  waiting for transfers between devices: 154 us -> 200 us
  starting transfers between devices: 39.2 us -> 51 us
  matrix products: 42.3 us -> 47.6 us
  local copies, waits for them, and re-layouts: 33.2 us -> 29.2 us
    all_to_all x1 -> x0, blocking collectives: 56.3 us -> none  [exchange(): lax.all_to_all(rows, OWNER_AXES, split_axis=0, concat_axis=0, tiled=True)]
    all_to_all x5 -> x6, waiting for transfers between devices: 95.8 us -> 141 us  [exchange(): lax.all_to_all(rows, OWNER_AXES, split_axis=0, concat_axis=0, tiled=True)]
    all_to_all x5 -> x6, starting transfers between devices: 39.2 us -> 51 us  [exchange(): lax.all_to_all(rows, OWNER_AXES, split_axis=0, concat_axis=0, tiled=True)]
    unnamed x44 -> x42, local copies, waits for them, and re-layouts: 9.83 us -> 6.37 us
  transfers between devices with their start and end apart: 6 -> 7, of which waited for: 5 -> 6; matrix products, arithmetic and copies ran while one was open for 11% -> 13% of each run, Pallas kernels for 0% -> 0%
where the time goes in v6:
time: 351 us; the launch traced here: 349 us
  waiting for transfers between devices  200 us (57%)
  starting transfers between devices  51 us (15%)
  matrix products  47.6 us (14%)
  local copies, waits for them, and re-layouts  29.2 us (8%)
  between operations  14.4 us (4%)
  other arithmetic  7.44 us (2%)
    all_to_all x6, waiting for transfers between devices, exchange(): lax.all_to_all(rows, OWNER_AXES, split_axis=0, concat_axis=0, tiled=True)  141 us
    reduce_scatter x1, waiting for transfers between devices, shards(): lax.psum_scatter(stacked, 'batch', scatter_dimension=0, tiled=True)  58.3 us
    all_to_all x6, starting transfers between devices, exchange(): lax.all_to_all(rows, OWNER_AXES, split_axis=0, concat_axis=0, tiled=True)  51 us
    all_to_all x6, local copies, waits for them, and re-layouts, exchange(): lax.all_to_all(rows, OWNER_AXES, split_axis=0, concat_axis=0, tiled=True)  11.3 us
  transfers between devices with their start and end apart: 7, of which 6 were waited for; matrix products, arithmetic and copies ran while one was open for 13% of the time, Pallas kernels for 0%

profile of v6, /device:TPU:6, one launch (start us, length us, event | category | flops | bytes accessed | tf_op | source)
XLA Modules:
  0.0 349.1 jit_solution(16594243270270928477)
XLA Ops:
  7.2 0.9 copy.33
  8.1 0.7 broadcast_compare_fusion
  8.9 0.3 convert_reduce_fusion.1
  9.5 0.1 and.121
  9.7 0.1 copy.39
  9.8 0.9 convert_element_type.107
  10.7 0.1 copy.42
  11.0 0.2 convert_reduce_fusion.2
  11.2 0.3 copy-done.11
  11.5 0.3 fusion.36
  11.9 1.7 fusion.1
  13.6 1.2 all_to_all.54
  14.7 7.6 %all-to-all-start.2 = ((bf16[32,4,4224]{2,1,0:T(4,128)(2,1)}), bf16[32,4,4224]{2,1,0:T(4,128)(2,1)S(1)}, u32[]{:S(2)}, u32[]{:S(2)}) async-start(bf16[32,4,4224]{2,1,0:T(4,128)(2,1)} %all_to_all.54), calls=%async_computation.2 | async-start | bytes 2162688 | tf_op jit(solution)/shard_map/dispatch/all_to_all | solution.py:11
  22.4 0.2 convert_reduce_fusion
  22.6 1.5 fusion.30
  24.0 4.6 %add_convert_fusion = bf16[512,4224]{1,0:T(8,128)(2,1)} fusion(f32[512,64]{1,0:T(8,128)S(1)} %fusion.30, bf16[128,4096]{1,0:T(8,128)(2,1)} %param.7, s32[128,512]{1,0:T(8,128)S(1)} %convert_reduce_fusion), kind=kOutput, calls=%fused_computation.1 | convolution fusion | flops 558039040 | bytes 5767168 | tf_op jit(solution)/shard_map/dispatch/dot_general | solution.py:64
  28.6 8.6 %all-to-all-done.2 = bf16[32,4,4224]{2,1,0:T(4,128)(2,1)S(1)} async-done(((bf16[32,4,4224]{2,1,0:T(4,128)(2,1)}), bf16[32,4,4224]{2,1,0:T(4,128)(2,1)S(1)}, u32[]{:S(2)}, u32[]{:S(2)}) %all-to-all-start.2) | async-done | bytes 1081376 | tf_op jit(solution)/shard_map/dispatch/all_to_all | solution.py:11
  37.3 1.0 copy-done.4
  38.3 7.5 %all-to-all-start = ((bf16[32,16,4224]{2,1,0:T(8,128)(2,1)}), bf16[32,16,4224]{2,1,0:T(8,128)(2,1)}, u32[]{:S(2)}, u32[]{:S(2)}) async-start(bf16[32,16,4224]{2,1,0:T(8,128)(2,1)} %bitcast.44), calls=%async_computation | async-start | bytes 8650752 | tf_op jit(solution)/shard_map/dispatch/all_to_all | solution.py:11
  45.8 0.6 convert_element_type.112
  46.3 0.5 and_select_fusion
  46.9 0.6 and_select_fusion.1
  47.4 1.3 all_to_all.56
  48.9 0.7 tile.20
  49.6 1.6 copy.49
  51.2 2.1 fusion.25
  53.4 0.6 copy-done.9
  54.0 1.4 convolution_convert_fusion.4
  55.5 2.3 all_to_all.57
  57.7 38.6 %all-to-all-done = bf16[32,16,4224]{2,1,0:T(8,128)(2,1)} async-done(((bf16[32,16,4224]{2,1,0:T(8,128)(2,1)}), bf16[32,16,4224]{2,1,0:T(8,128)(2,1)}, u32[]{:S(2)}, u32[]{:S(2)}) %all-to-all-start) | async-done | bytes 4325408 | tf_op jit(solution)/shard_map/dispatch/all_to_all | solution.py:11
  96.3 9.3 %all-to-all-start.3 = ((bf16[32,4,4096]{2,1,0:T(4,128)(2,1)}), bf16[32,4,4096]{2,1,0:T(4,128)(2,1)}, u32[]{:S(2)}, u32[]{:S(2)}) async-start(bf16[32,4,4096]{2,1,0:T(4,128)(2,1)} %all_to_all.57), calls=%async_computation.3 | async-start | bytes 2097152 | tf_op jit(solution)/shard_map/encode_decode/all_to_all | solution.py:11
  105.6 1.6 slice.30
  107.2 1.6 copy.54
  108.8 1.7 tile.8
  110.5 2.0 copy.45
  112.5 4.2 %fusion.16 = bf16[512,256]{1,0:T(8,128)(2,1)S(1)} fusion(bf16[512,4224]{1,0:T(8,128)(2,1)} %bitcast.2, bf16[4096,256]{1,0:T(8,128)(2,1)} %param.10, f32[512,256]{1,0:T(8,128)} %copy.45, s32[256]{0:T(256)S(1)} %copy-done.15, f32[256]{0:T(256)S(1)} %copy-done.17, s32[512]{0:T(512)S(1)} %add_select_fusion.4), kind=kOutput, calls=%fused_computation.26 | convolution fusion | flops 1107951616 | bytes 7213056 | tf_op jit(solution)/shard_map/encode_decode/dot_general | solution.py:80
  116.7 0.7 copy-done.12
  117.4 3.3 convolution_convert_fusion.1
  120.7 7.6 %all-to-all-start.1 = ((bf16[32,16,4096]{2,1,0:T(8,128)(2,1)}), bf16[32,16,4096]{2,1,0:T(8,128)(2,1)}, u32[]{:S(2)}, u32[]{:S(2)}) async-start(bf16[32,16,4096]{2,1,0:T(8,128)(2,1)} %bitcast.41), calls=%async_computation.1 | async-start | bytes 8388608 | tf_op jit(solution)/shard_map/encode_decode/all_to_all | solution.py:11
  128.4 2.1 all_to_all.59
  130.6 46.6 %all-to-all-done.1 = bf16[32,16,4096]{2,1,0:T(8,128)(2,1)} async-done(((bf16[32,16,4096]{2,1,0:T(8,128)(2,1)}), bf16[32,16,4096]{2,1,0:T(8,128)(2,1)}, u32[]{:S(2)}, u32[]{:S(2)}) %all-to-all-start.1) | async-done | bytes 4194336 | tf_op jit(solution)/shard_map/encode_decode/all_to_all | solution.py:11
  177.2 3.3 convolution_add_fusion.4
  180.5 0.4 fusion.4
  181.0 3.3 convolution_convert_fusion
  184.2 9.6 %all-to-all-start.4 = ((bf16[32,16,4096]{2,1,0:T(8,128)(2,1)}), bf16[32,16,4096]{2,1,0:T(8,128)(2,1)}, u32[]{:S(2)}, u32[]{:S(2)}) async-start(bf16[32,16,4096]{2,1,0:T(8,128)(2,1)} %bitcast.39), calls=%async_computation.4 | async-start | bytes 8388608 | tf_op jit(solution)/shard_map/combine/all_to_all | solution.py:11
  193.9 2.7 convolution_convert_fusion.3
  196.5 46.1 %all-to-all-done.4 = bf16[32,16,4096]{2,1,0:T(8,128)(2,1)} async-done(((bf16[32,16,4096]{2,1,0:T(8,128)(2,1)}), bf16[32,16,4096]{2,1,0:T(8,128)(2,1)}, u32[]{:S(2)}, u32[]{:S(2)}) %all-to-all-start.4) | async-done | bytes 4194336 | tf_op jit(solution)/shard_map/combine/all_to_all | solution.py:11
  242.6 2.3 all_to_all.63
  244.9 9.4 %all-to-all-start.5 = ((bf16[32,4,4096]{2,1,0:T(4,128)(2,1)}), bf16[32,4,4096]{2,1,0:T(4,128)(2,1)}, u32[]{:S(2)}, u32[]{:S(2)}) async-start(bf16[32,4,4096]{2,1,0:T(4,128)(2,1)} %all_to_all.63), calls=%async_computation.5 | async-start | bytes 2097152 | tf_op jit(solution)/shard_map/combine/all_to_all | solution.py:11
  254.3 3.6 %fusion.54 = (f32[256]{0:T(256)S(1)}, bf16[512,256]{1,0:T(8,128)(2,1)S(1)}) fusion(f32[512,256]{1,0:T(8,128)} %copy.45, s32[256]{0:T(256)S(1)} %copy-done.15, s32[512]{0:T(512)S(1)} %add_select_fusion.4, bf16[512,4096]{1,0:T(8,128)(2,1)} %bitcast.8, bf16[256,4096]{1,0:T(8,128)(2,1)S(1)} %copy-done), kind=kOutput, calls=%fused_computation.99 | convolution fusion | flops 1074396928 | bytes 7081984 | tf_op jit(solution)/shard_map/backward/dot_general | solution.py:106
  257.9 3.6 %fusion.34 = bf16[4224,256]{1,0:T(8,128)(2,1)S(1)} fusion(bf16[512,4224]{1,0:T(8,128)(2,1)} %bitcast.2, bf16[512,256]{1,0:T(8,128)(2,1)S(1)} %get-tuple-element.37), kind=kOutput, calls=%fused_computation.44 | convolution fusion | flops 1107296256 | bytes 6750208 | tf_op jit(solution)/shard_map/backward/dot_general | solution.py:111
  261.5 1.5 slice.42
  263.0 4.8 %convolution_convert_fusion.2 = bf16[4096,256]{1,0:T(8,128)(2,1)} fusion(bf16[512,4096]{1,0:T(8,128)(2,1)} %bitcast.8, bf16[512,256]{1,0:T(8,128)(2,1)S(1)} %copy-done.13), kind=kOutput, calls=%fused_computation.11 | convolution fusion | flops 1074790400 | bytes 6553600 | tf_op jit(solution)/shard_map/backward/dot_general | solution.py:115
  267.8 1.2 all-to-all-done.5
  269.0 2.1 all_to_all.65
  271.2 2.2 fusion.55
  273.5 2.0 fusion.2
  275.6 2.5 fusion.3
  278.1 2.2 fusion.5
  280.3 58.3 %reduce-scatter.2.cloned.1.call-done = bf16[528,512]{1,0:T(8,128)(2,1)} async-done(((bf16[4224,512]{1,0:T(8,128)(2,1)}), bf16[528,512]{1,0:T(8,128)(2,1)}) %reduce-scatter.2.cloned.1.call-update) | async-done | bytes 540688 | tf_op jit(solution)/shard_map/grad_reduce/reduce_scatter | solution.py:144
  338.7 1.2 convert_element_type.133
  340.0 0.5 slice_bitcast_fusion.1
  340.5 1.0 copy.51
  341.5 0.8 slice.34
  (52 shorter events, 1.0 us)
Async XLA Ops:
  7.2 46.8 %copy-start = (bf16[256,4096]{1,0:T(8,128)(2,1)S(1)}, bf16[256,4096]{1,0:T(8,128)(2,1)}, u32[]{:S(2)}) copy-start(bf16[256,4096]{1,0:T(8,128)(2,1)} %param.12) | copy-start | bytes 6291460
  10.9 0.7 copy-start.11
  14.7 22.5 %all-to-all-start.2 = ((bf16[32,4,4224]{2,1,0:T(4,128)(2,1)}), bf16[32,4,4224]{2,1,0:T(4,128)(2,1)S(1)}, u32[]{:S(2)}, u32[]{:S(2)}) async-start(bf16[32,4,4224]{2,1,0:T(4,128)(2,1)} %all_to_all.54), calls=%async_computation.2 | async-start | bytes 2162688 | tf_op jit(solution)/shard_map/dispatch/all_to_all | solution.py:11
  37.3 1.0 copy-start.4
  37.3 8.5 %copy-start.18 = (bf16[256]{0:T(256)(128)(2,1)S(1)}, bf16[256]{0:T(256)(128)(2,1)}, u32[]{:S(2)}) copy-start(bf16[256]{0:T(256)(128)(2,1)} %param.11) | copy-start | bytes 1540
  38.3 58.0 %all-to-all-start = ((bf16[32,16,4224]{2,1,0:T(8,128)(2,1)}), bf16[32,16,4224]{2,1,0:T(8,128)(2,1)}, u32[]{:S(2)}, u32[]{:S(2)}) async-start(bf16[32,16,4224]{2,1,0:T(8,128)(2,1)} %bitcast.44), calls=%async_computation | async-start | bytes 8650752 | tf_op jit(solution)/shard_map/dispatch/all_to_all | solution.py:11
  53.4 0.6 copy-start.9
  57.7 54.8 %copy-start.15 = (s32[256]{0:T(256)S(1)}, s32[256]{0:T(256)}, u32[]{:S(2)}) copy-start(s32[256]{0:T(256)} %and_select_fusion.1) | copy-start | bytes 3076
  57.7 54.8 %copy-start.17 = (f32[256]{0:T(256)S(1)}, f32[256]{0:T(256)}, u32[]{:S(2)}) copy-start(f32[256]{0:T(256)} %convert_element_type.112) | copy-start | bytes 3076
  96.3 24.4 %all-to-all-start.3 = ((bf16[32,4,4096]{2,1,0:T(4,128)(2,1)}), bf16[32,4,4096]{2,1,0:T(4,128)(2,1)}, u32[]{:S(2)}, u32[]{:S(2)}) async-start(bf16[32,4,4096]{2,1,0:T(4,128)(2,1)} %all_to_all.57), calls=%async_computation.3 | async-start | bytes 2097152 | tf_op jit(solution)/shard_map/encode_decode/all_to_all | solution.py:11
  116.7 0.7 copy-start.12
  120.7 7.7 %copy-start.14 = (bf16[4096]{0:T(1024)(128)(2,1)S(1)}, bf16[4096]{0:T(1024)(128)(2,1)}, u32[]{:S(2)}) copy-start(bf16[4096]{0:T(1024)(128)(2,1)} %param.13) | copy-start | bytes 24580
  120.7 56.5 %all-to-all-start.1 = ((bf16[32,16,4096]{2,1,0:T(8,128)(2,1)}), bf16[32,16,4096]{2,1,0:T(8,128)(2,1)}, u32[]{:S(2)}, u32[]{:S(2)}) async-start(bf16[32,16,4096]{2,1,0:T(8,128)(2,1)} %bitcast.41), calls=%async_computation.1 | async-start | bytes 8388608 | tf_op jit(solution)/shard_map/encode_decode/all_to_all | solution.py:11
  177.2 3.3 copy-start.5
  180.9 3.3 copy-start.2
  184.2 58.4 %all-to-all-start.4 = ((bf16[32,16,4096]{2,1,0:T(8,128)(2,1)}), bf16[32,16,4096]{2,1,0:T(8,128)(2,1)}, u32[]{:S(2)}, u32[]{:S(2)}) async-start(bf16[32,16,4096]{2,1,0:T(8,128)(2,1)} %bitcast.39), calls=%async_computation.4 | async-start | bytes 8388608 | tf_op jit(solution)/shard_map/combine/all_to_all | solution.py:11
  244.9 24.1 %all-to-all-start.5 = ((bf16[32,4,4096]{2,1,0:T(4,128)(2,1)}), bf16[32,4,4096]{2,1,0:T(4,128)(2,1)}, u32[]{:S(2)}, u32[]{:S(2)}) async-start(bf16[32,4,4096]{2,1,0:T(4,128)(2,1)} %all_to_all.63), calls=%async_computation.5 | async-start | bytes 2097152 | tf_op jit(solution)/shard_map/combine/all_to_all | solution.py:11
  254.3 84.4 %reduce-scatter.2.cloned.1.call-start = ((), (), s32[]{:S(2)}) async-start(), calls=%async_computation.7 | async-start | bytes 4866048 | tf_op jit(solution)/shard_map/grad_reduce/reduce_scatter | solution.py:144
  261.5 1.5 copy-start.13
  263.0 8.2 %copy-start.16 = (s32[128]{0:T(128)S(1)}, s32[128]{0:T(128)}, u32[]{:S(2)}) copy-start(s32[128]{0:T(128)} %and_select_fusion) | copy-start | bytes 1540
  267.8 3.3 copy-start.8
  271.2 2.3 copy-start.1
  271.2 2.3 copy-start.7
  271.2 2.3 copy-start.10
  275.6 2.5 copy-start.3
  338.7 2.8 copy-start.6
Sparse Core Ops, SparseCore 0:
  280.5 58.1 reduce-scatter.1

commit v7 on v5

--- a/solution.py
+++ b/solution.py
@@ -127,7 +127,7 @@
     with jax.named_scope("grad_reduce"):
         rows_per = model_width // n_batch
         bias_per = local_lat // n_batch
-        pad_rows = 16
+        pad_rows = 8
         weights = jnp.concatenate(
             [
                 enc_grad.astype(jnp.bfloat16).reshape(n_batch, rows_per, local_lat),

time: 350 us -> 349 us (level)
  no operation moved by 1% of the time
where the time goes in v7:
time: 349 us; the launch traced here: 347 us
  waiting for transfers between devices  153 us (44%)
  blocking collectives  56.3 us (16%)
  matrix products  42.3 us (12%)
  starting transfers between devices  39.2 us (11%)
  local copies, waits for them, and re-layouts  33.2 us (10%)
  between operations  15 us (4%)
  other arithmetic  7.39 us (2%)
    all_to_all x5, waiting for transfers between devices, exchange(): lax.all_to_all(rows, OWNER_AXES, split_axis=0, concat_axis=0, tiled=True)  95.8 us
    reduce_scatter x1, waiting for transfers between devices, shards(): lax.psum_scatter(stacked, 'batch', scatter_dimension=0, tiled=True)  57.7 us
    all_to_all x1, blocking collectives, exchange(): lax.all_to_all(rows, OWNER_AXES, split_axis=0, concat_axis=0, tiled=True)  56.3 us
    all_to_all x5, starting transfers between devices, exchange(): lax.all_to_all(rows, OWNER_AXES, split_axis=0, concat_axis=0, tiled=True)  39.2 us
    all_to_all x6, local copies, waits for them, and re-layouts, exchange(): lax.all_to_all(rows, OWNER_AXES, split_axis=0, concat_axis=0, tiled=True)  11.3 us
    unnamed x44, local copies, waits for them, and re-layouts  9.83 us
  transfers between devices with their start and end apart: 6, of which 5 were waited for; matrix products, arithmetic and copies ran while one was open for 11% of the time, Pallas kernels for 0%

profile of v7, /device:TPU:6, one launch (start us, length us, event | category | flops | bytes accessed | tf_op | source)
XLA Modules:
  0.0 346.8 jit_solution(9337242078843341040)
XLA Ops:
  7.2 0.9 copy.33
  8.1 0.7 broadcast_compare_fusion
  8.9 0.3 convert_reduce_fusion.1
  9.7 0.1 copy.39
  9.8 0.9 convert_element_type.107
  11.0 0.2 convert_reduce_fusion.2
  11.2 0.3 copy-done.12
  11.5 0.3 fusion.37
  11.9 1.7 fusion.1
  13.6 1.1 all_to_all.54
  14.7 7.6 %all-to-all-start.2 = ((bf16[32,4,4224]{2,1,0:T(4,128)(2,1)}), bf16[32,4,4224]{2,1,0:T(4,128)(2,1)S(1)}, u32[]{:S(2)}, u32[]{:S(2)}) async-start(bf16[32,4,4224]{2,1,0:T(4,128)(2,1)} %all_to_all.54), calls=%async_computation.2 | async-start | bytes 2162688 | tf_op jit(solution)/shard_map/dispatch/all_to_all | solution.py:11
  22.4 0.2 convert_reduce_fusion
  22.6 1.5 fusion.31
  24.0 4.6 %add_convert_fusion = bf16[512,4224]{1,0:T(8,128)(2,1)} fusion(f32[512,64]{1,0:T(8,128)S(1)} %fusion.31, bf16[128,4096]{1,0:T(8,128)(2,1)} %param.7, s32[128,512]{1,0:T(8,128)S(1)} %convert_reduce_fusion), kind=kOutput, calls=%fused_computation | convolution fusion | flops 558039040 | bytes 5767168 | tf_op jit(solution)/shard_map/dispatch/dot_general | solution.py:64
  28.6 8.6 %all-to-all-done.2 = bf16[32,4,4224]{2,1,0:T(4,128)(2,1)S(1)} async-done(((bf16[32,4,4224]{2,1,0:T(4,128)(2,1)}), bf16[32,4,4224]{2,1,0:T(4,128)(2,1)S(1)}, u32[]{:S(2)}, u32[]{:S(2)}) %all-to-all-start.2) | async-done | bytes 1081376 | tf_op jit(solution)/shard_map/dispatch/all_to_all | solution.py:11
  37.3 1.0 copy-done.3
  38.3 7.5 %all-to-all-start = ((bf16[32,16,4224]{2,1,0:T(8,128)(2,1)}), bf16[32,16,4224]{2,1,0:T(8,128)(2,1)}, u32[]{:S(2)}, u32[]{:S(2)}) async-start(bf16[32,16,4224]{2,1,0:T(8,128)(2,1)} %bitcast.45), calls=%async_computation | async-start | bytes 8650752 | tf_op jit(solution)/shard_map/dispatch/all_to_all | solution.py:11
  45.8 0.6 convert_element_type.112
  46.3 0.5 and_select_fusion
  46.9 0.6 and_select_fusion.1
  47.4 1.3 all_to_all.56
  48.9 0.7 tile.20
  49.6 1.6 copy.49
  51.2 2.1 fusion.26
  53.4 0.6 copy-done.10
  54.0 1.4 convolution_convert_fusion.4
  55.4 2.3 all_to_all.57
  57.7 38.6 %all-to-all-done = bf16[32,16,4224]{2,1,0:T(8,128)(2,1)} async-done(((bf16[32,16,4224]{2,1,0:T(8,128)(2,1)}), bf16[32,16,4224]{2,1,0:T(8,128)(2,1)}, u32[]{:S(2)}, u32[]{:S(2)}) %all-to-all-start) | async-done | bytes 4325408 | tf_op jit(solution)/shard_map/dispatch/all_to_all | solution.py:11
  96.3 9.3 %all-to-all-start.3 = ((bf16[32,4,4096]{2,1,0:T(4,128)(2,1)}), bf16[32,4,4096]{2,1,0:T(4,128)(2,1)}, u32[]{:S(2)}, u32[]{:S(2)}) async-start(bf16[32,4,4096]{2,1,0:T(4,128)(2,1)} %all_to_all.57), calls=%async_computation.3 | async-start | bytes 2097152 | tf_op jit(solution)/shard_map/encode_decode/all_to_all | solution.py:11
  105.6 1.6 slice.34
  107.2 1.6 copy.54
  108.8 1.7 tile.8
  110.5 2.0 copy.45
  112.5 4.2 %fusion.17 = bf16[512,256]{1,0:T(8,128)(2,1)S(1)} fusion(bf16[512,4224]{1,0:T(8,128)(2,1)} %bitcast.2, bf16[4096,256]{1,0:T(8,128)(2,1)} %param.10, f32[512,256]{1,0:T(8,128)} %copy.45, s32[256]{0:T(256)S(1)} %copy-done.16, f32[256]{0:T(256)S(1)} %copy-done.18, s32[512]{0:T(512)S(1)} %add_select_fusion.4), kind=kOutput, calls=%fused_computation.27 | convolution fusion | flops 1107951616 | bytes 7213056 | tf_op jit(solution)/shard_map/encode_decode/dot_general | solution.py:80
  116.7 0.7 copy-done.13
  117.4 3.3 convolution_convert_fusion.1
  120.7 7.6 %all-to-all-start.1 = ((bf16[32,16,4096]{2,1,0:T(8,128)(2,1)}), bf16[32,16,4096]{2,1,0:T(8,128)(2,1)}, u32[]{:S(2)}, u32[]{:S(2)}) async-start(bf16[32,16,4096]{2,1,0:T(8,128)(2,1)} %bitcast.42), calls=%async_computation.1 | async-start | bytes 8388608 | tf_op jit(solution)/shard_map/encode_decode/all_to_all | solution.py:11
  128.4 2.1 all_to_all.59
  130.5 46.6 %all-to-all-done.1 = bf16[32,16,4096]{2,1,0:T(8,128)(2,1)} async-done(((bf16[32,16,4096]{2,1,0:T(8,128)(2,1)}), bf16[32,16,4096]{2,1,0:T(8,128)(2,1)}, u32[]{:S(2)}, u32[]{:S(2)}) %all-to-all-start.1) | async-done | bytes 4194336 | tf_op jit(solution)/shard_map/encode_decode/all_to_all | solution.py:11
  177.2 3.3 convolution_add_fusion.4
  180.5 0.4 fusion.4
  180.9 1.3 convolution_convert_fusion
  182.2 56.3 %all_to_all.72 = bf16[32,16,4096]{2,1,0:T(8,128)(2,1)S(1)} all-to-all(bf16[32,16,4096]{2,1,0:T(8,128)(2,1)S(1)} %bitcast.40), channel_id=1, replica_groups=mesh['loop'=4,'inner'=8,'batch'=8] {'loop','inner'}, dimensions={0} | all-to-all | bytes 8388608 | tf_op jit(solution)/shard_map/combine/all_to_all | solution.py:11
  238.5 2.0 copy-done.4
  240.5 0.5 slice.38
  241.6 1.5 fusion.5
  243.2 2.3 all_to_all.63
  245.4 7.2 %all-to-all-start.5 = ((bf16[32,4,4096]{2,1,0:T(4,128)(2,1)}), bf16[32,4,4096]{2,1,0:T(4,128)(2,1)}, u32[]{:S(2)}, u32[]{:S(2)}) async-start(bf16[32,4,4096]{2,1,0:T(4,128)(2,1)} %all_to_all.63), calls=%async_computation.5 | async-start | bytes 2097152 | tf_op jit(solution)/shard_map/combine/all_to_all | solution.py:11
  252.7 3.6 %fusion.55 = (f32[256]{0:T(256)S(1)}, bf16[512,256]{1,0:T(8,128)(2,1)S(1)}) fusion(f32[512,256]{1,0:T(8,128)} %copy.45, s32[256]{0:T(256)S(1)} %copy-done.16, s32[512]{0:T(512)S(1)} %add_select_fusion.4, bf16[512,4096]{1,0:T(8,128)(2,1)} %bitcast.47, bf16[256,4096]{1,0:T(8,128)(2,1)S(1)} %copy-done), kind=kOutput, calls=%fused_computation.100 | convolution fusion | flops 1074396928 | bytes 7081984 | tf_op jit(solution)/shard_map/backward/dot_general | solution.py:107
  256.3 3.6 %fusion.35 = bf16[4224,256]{1,0:T(8,128)(2,1)S(1)} fusion(bf16[512,4224]{1,0:T(8,128)(2,1)} %bitcast.2, bf16[512,256]{1,0:T(8,128)(2,1)S(1)} %get-tuple-element.33), kind=kOutput, calls=%fused_computation.45 | convolution fusion | flops 1107296256 | bytes 6750208 | tf_op jit(solution)/shard_map/backward/dot_general | solution.py:112
  260.0 1.5 slice.47
  261.4 1.5 copy-done.5
  262.9 2.6 convolution_convert_fusion.2
  265.5 1.9 all-to-all-done.5
  267.4 2.1 all_to_all.65
  269.6 2.2 fusion.56
  271.8 2.1 fusion.2
  274.0 2.5 fusion.3
  276.5 2.2 fusion.6
  278.7 57.7 %reduce-scatter.2.cloned.1.call-done = bf16[520,512]{1,0:T(8,128)(2,1)} async-done(((bf16[4160,512]{1,0:T(8,128)(2,1)}), bf16[520,512]{1,0:T(8,128)(2,1)}) %reduce-scatter.2.cloned.1.call-update) | async-done | bytes 532496 | tf_op jit(solution)/shard_map/grad_reduce/reduce_scatter | solution.py:145
  336.3 1.2 convert_element_type.133
  337.6 0.5 slice_bitcast_fusion.1
  338.1 1.0 copy.51
  339.1 0.8 slice.39
  (54 shorter events, 1.3 us)
Async XLA Ops:
  7.2 46.8 %copy-start = (bf16[256,4096]{1,0:T(8,128)(2,1)S(1)}, bf16[256,4096]{1,0:T(8,128)(2,1)}, u32[]{:S(2)}) copy-start(bf16[256,4096]{1,0:T(8,128)(2,1)} %param.12) | copy-start | bytes 6291460
  10.9 0.7 copy-start.12
  14.7 22.5 %all-to-all-start.2 = ((bf16[32,4,4224]{2,1,0:T(4,128)(2,1)}), bf16[32,4,4224]{2,1,0:T(4,128)(2,1)S(1)}, u32[]{:S(2)}, u32[]{:S(2)}) async-start(bf16[32,4,4224]{2,1,0:T(4,128)(2,1)} %all_to_all.54), calls=%async_computation.2 | async-start | bytes 2162688 | tf_op jit(solution)/shard_map/dispatch/all_to_all | solution.py:11
  37.3 1.0 copy-start.3
  37.3 8.5 %copy-start.19 = (bf16[256]{0:T(256)(128)(2,1)S(1)}, bf16[256]{0:T(256)(128)(2,1)}, u32[]{:S(2)}) copy-start(bf16[256]{0:T(256)(128)(2,1)} %param.11) | copy-start | bytes 1540
  38.3 58.0 %all-to-all-start = ((bf16[32,16,4224]{2,1,0:T(8,128)(2,1)}), bf16[32,16,4224]{2,1,0:T(8,128)(2,1)}, u32[]{:S(2)}, u32[]{:S(2)}) async-start(bf16[32,16,4224]{2,1,0:T(8,128)(2,1)} %bitcast.45), calls=%async_computation | async-start | bytes 8650752 | tf_op jit(solution)/shard_map/dispatch/all_to_all | solution.py:11
  53.3 0.6 copy-start.10
  57.7 54.8 %copy-start.16 = (s32[256]{0:T(256)S(1)}, s32[256]{0:T(256)}, u32[]{:S(2)}) copy-start(s32[256]{0:T(256)} %and_select_fusion.1) | copy-start | bytes 3076
  57.7 54.8 %copy-start.18 = (f32[256]{0:T(256)S(1)}, f32[256]{0:T(256)}, u32[]{:S(2)}) copy-start(f32[256]{0:T(256)} %convert_element_type.112) | copy-start | bytes 3076
  96.3 24.4 %all-to-all-start.3 = ((bf16[32,4,4096]{2,1,0:T(4,128)(2,1)}), bf16[32,4,4096]{2,1,0:T(4,128)(2,1)}, u32[]{:S(2)}, u32[]{:S(2)}) async-start(bf16[32,4,4096]{2,1,0:T(4,128)(2,1)} %all_to_all.57), calls=%async_computation.3 | async-start | bytes 2097152 | tf_op jit(solution)/shard_map/encode_decode/all_to_all | solution.py:11
  116.7 0.7 copy-start.13
  120.7 7.7 %copy-start.15 = (bf16[4096]{0:T(1024)(128)(2,1)S(1)}, bf16[4096]{0:T(1024)(128)(2,1)}, u32[]{:S(2)}) copy-start(bf16[4096]{0:T(1024)(128)(2,1)} %param.13) | copy-start | bytes 24580
  120.7 56.5 %all-to-all-start.1 = ((bf16[32,16,4096]{2,1,0:T(8,128)(2,1)}), bf16[32,16,4096]{2,1,0:T(8,128)(2,1)}, u32[]{:S(2)}, u32[]{:S(2)}) async-start(bf16[32,16,4096]{2,1,0:T(8,128)(2,1)} %bitcast.42), calls=%async_computation.1 | async-start | bytes 8388608 | tf_op jit(solution)/shard_map/encode_decode/all_to_all | solution.py:11
  177.2 3.3 copy-start.6
  238.5 2.0 copy-start.4
  245.4 22.0 %all-to-all-start.5 = ((bf16[32,4,4096]{2,1,0:T(4,128)(2,1)}), bf16[32,4,4096]{2,1,0:T(4,128)(2,1)}, u32[]{:S(2)}, u32[]{:S(2)}) async-start(bf16[32,4,4096]{2,1,0:T(4,128)(2,1)} %all_to_all.63), calls=%async_computation.5 | async-start | bytes 2097152 | tf_op jit(solution)/shard_map/combine/all_to_all | solution.py:11
  252.6 83.7 %reduce-scatter.2.cloned.1.call-start = ((), (), s32[]{:S(2)}) async-start(), calls=%async_computation.7 | async-start | bytes 4792320 | tf_op jit(solution)/shard_map/grad_reduce/reduce_scatter | solution.py:145
  256.3 5.1 %copy-start.14 = (bf16[512,256]{1,0:T(8,128)(2,1)S(1)}, bf16[512,256]{1,0:T(8,128)(2,1)}, u32[]{:S(2)}) copy-start(bf16[512,256]{1,0:T(8,128)(2,1)} %copy-done.13) | copy-start | bytes 786436
  259.9 2.9 copy-start.5
  262.9 6.7 %copy-start.17 = (s32[128]{0:T(128)S(1)}, s32[128]{0:T(128)}, u32[]{:S(2)}) copy-start(s32[128]{0:T(128)} %and_select_fusion) | copy-start | bytes 1540
  265.5 4.0 %copy-start.9 = (f32[128,256]{1,0:T(8,128)S(1)}, f32[128,256]{1,0:T(8,128)}, u32[]{:S(2)}) copy-start(f32[128,256]{1,0:T(8,128)} %copy.49) | copy-start | bytes 393220
  269.5 2.3 copy-start.1
  269.6 2.3 copy-start.8
  269.6 2.3 copy-start.11
  274.0 2.5 copy-start.2
  336.3 2.8 copy-start.7
Sparse Core Ops, SparseCore 0:
  278.8 57.5 reduce-scatter.1

commit v8 on v7

--- a/solution.py
+++ b/solution.py
@@ -142,12 +142,10 @@
         stacked = jnp.concatenate([weights, bias_block], axis=1).reshape(
             n_batch * (rows_per + pad_rows), 2 * local_lat
         )
-        reduced = lax.psum_scatter(stacked, "batch", scatter_dimension=0, tiled=True).astype(
-            jnp.float32
-        )
-        grad_enc_weight = reduced[:rows_per, :local_lat]
-        grad_dec_weight = reduced[:rows_per, local_lat:].T
-        bias_share = reduced[rows_per, :bias_per]
+        reduced = lax.psum_scatter(stacked, "batch", scatter_dimension=0, tiled=True)
+        grad_enc_weight = reduced[:rows_per, :local_lat].astype(jnp.float32)
+        grad_dec_weight = reduced[:rows_per, local_lat:].T.astype(jnp.float32)
+        bias_share = reduced[rows_per, :bias_per].astype(jnp.float32)
     return (grad_enc_weight, bias_share, grad_dec_weight)
 
 

time: 349 us -> 349 us (level)
    unnamed x44 -> x42, local copies, waits for them, and re-layouts: 9.83 us -> 9.83 us
where the time goes in v8:
time: 349 us; the launch traced here: 347 us
  waiting for transfers between devices  153 us (44%)
  blocking collectives  56.3 us (16%)
  matrix products  42.3 us (12%)
  starting transfers between devices  39.2 us (11%)
  local copies, waits for them, and re-layouts  31.8 us (9%)
  between operations  15 us (4%)
  other arithmetic  9.23 us (3%)
    all_to_all x5, waiting for transfers between devices, exchange(): lax.all_to_all(rows, OWNER_AXES, split_axis=0, concat_axis=0, tiled=True)  95.8 us
    reduce_scatter x1, waiting for transfers between devices, shards(): lax.psum_scatter(stacked, 'batch', scatter_dimension=0, tiled=True)  57.7 us
    all_to_all x1, blocking collectives, exchange(): lax.all_to_all(rows, OWNER_AXES, split_axis=0, concat_axis=0, tiled=True)  56.3 us
    all_to_all x5, starting transfers between devices, exchange(): lax.all_to_all(rows, OWNER_AXES, split_axis=0, concat_axis=0, tiled=True)  39.2 us
    all_to_all x6, local copies, waits for them, and re-layouts, exchange(): lax.all_to_all(rows, OWNER_AXES, split_axis=0, concat_axis=0, tiled=True)  11.3 us
    unnamed x42, local copies, waits for them, and re-layouts  9.83 us
  transfers between devices with their start and end apart: 6, of which 5 were waited for; matrix products, arithmetic and copies ran while one was open for 11% of the time, Pallas kernels for 0%

profile of v8, /device:TPU:6, one launch (start us, length us, event | category | flops | bytes accessed | tf_op | source)
XLA Modules:
  0.0 347.2 jit_solution(6672784740882366963)
XLA Ops:
  7.2 0.9 copy.33
  8.1 0.7 broadcast_compare_fusion
  8.9 0.3 convert_reduce_fusion.1
  9.7 0.1 copy.39
  9.8 0.9 convert_element_type.119
  10.7 0.1 copy.42
  11.0 0.2 convert_reduce_fusion.2
  11.2 0.3 copy-done.11
  11.5 0.3 fusion.37
  11.9 1.7 fusion.1
  13.6 1.1 all_to_all.54
  14.7 7.6 %all-to-all-start.2 = ((bf16[32,4,4224]{2,1,0:T(4,128)(2,1)}), bf16[32,4,4224]{2,1,0:T(4,128)(2,1)S(1)}, u32[]{:S(2)}, u32[]{:S(2)}) async-start(bf16[32,4,4224]{2,1,0:T(4,128)(2,1)} %all_to_all.54), calls=%async_computation.2 | async-start | bytes 2162688 | tf_op jit(solution)/shard_map/dispatch/all_to_all | solution.py:11
  22.4 0.2 convert_reduce_fusion
  22.6 1.5 fusion.31
  24.0 4.6 %add_convert_fusion = bf16[512,4224]{1,0:T(8,128)(2,1)} fusion(f32[512,64]{1,0:T(8,128)S(1)} %fusion.31, bf16[128,4096]{1,0:T(8,128)(2,1)} %param.7, s32[128,512]{1,0:T(8,128)S(1)} %convert_reduce_fusion), kind=kOutput, calls=%fused_computation | convolution fusion | flops 558039040 | bytes 5767168 | tf_op jit(solution)/shard_map/dispatch/dot_general | solution.py:64
  28.6 8.6 %all-to-all-done.2 = bf16[32,4,4224]{2,1,0:T(4,128)(2,1)S(1)} async-done(((bf16[32,4,4224]{2,1,0:T(4,128)(2,1)}), bf16[32,4,4224]{2,1,0:T(4,128)(2,1)S(1)}, u32[]{:S(2)}, u32[]{:S(2)}) %all-to-all-start.2) | async-done | bytes 1081376 | tf_op jit(solution)/shard_map/dispatch/all_to_all | solution.py:11
  37.3 1.0 copy-done.3
  38.3 7.5 %all-to-all-start = ((bf16[32,16,4224]{2,1,0:T(8,128)(2,1)}), bf16[32,16,4224]{2,1,0:T(8,128)(2,1)}, u32[]{:S(2)}, u32[]{:S(2)}) async-start(bf16[32,16,4224]{2,1,0:T(8,128)(2,1)} %bitcast.48), calls=%async_computation | async-start | bytes 8650752 | tf_op jit(solution)/shard_map/dispatch/all_to_all | solution.py:11
  45.8 0.6 convert_element_type.124
  46.3 0.5 and_select_fusion
  46.9 0.6 and_select_fusion.1
  47.4 1.3 all_to_all.56
  48.9 0.7 tile.20
  49.6 1.6 copy.49
  51.2 2.1 fusion.26
  53.4 0.6 copy-done.9
  54.0 1.4 convolution_convert_fusion.4
  55.4 2.3 all_to_all.57
  57.7 38.6 %all-to-all-done = bf16[32,16,4224]{2,1,0:T(8,128)(2,1)} async-done(((bf16[32,16,4224]{2,1,0:T(8,128)(2,1)}), bf16[32,16,4224]{2,1,0:T(8,128)(2,1)}, u32[]{:S(2)}, u32[]{:S(2)}) %all-to-all-start) | async-done | bytes 4325408 | tf_op jit(solution)/shard_map/dispatch/all_to_all | solution.py:11
  96.3 9.3 %all-to-all-start.3 = ((bf16[32,4,4096]{2,1,0:T(4,128)(2,1)}), bf16[32,4,4096]{2,1,0:T(4,128)(2,1)}, u32[]{:S(2)}, u32[]{:S(2)}) async-start(bf16[32,4,4096]{2,1,0:T(4,128)(2,1)} %all_to_all.57), calls=%async_computation.3 | async-start | bytes 2097152 | tf_op jit(solution)/shard_map/encode_decode/all_to_all | solution.py:11
  105.6 1.6 slice.34
  107.2 1.6 copy.54
  108.8 1.7 tile.8
  110.5 2.0 copy.45
  112.5 4.2 %fusion.17 = bf16[512,256]{1,0:T(8,128)(2,1)S(1)} fusion(bf16[512,4224]{1,0:T(8,128)(2,1)} %bitcast.2, bf16[4096,256]{1,0:T(8,128)(2,1)} %param.10, f32[512,256]{1,0:T(8,128)} %copy.45, s32[256]{0:T(256)S(1)} %copy-done.15, f32[256]{0:T(256)S(1)} %copy-done.17, s32[512]{0:T(512)S(1)} %add_select_fusion.4), kind=kOutput, calls=%fused_computation.27 | convolution fusion | flops 1107951616 | bytes 7213056 | tf_op jit(solution)/shard_map/encode_decode/dot_general | solution.py:80
  116.7 0.7 copy-done.12
  117.4 3.3 convolution_convert_fusion.1
  120.7 7.6 %all-to-all-start.1 = ((bf16[32,16,4096]{2,1,0:T(8,128)(2,1)}), bf16[32,16,4096]{2,1,0:T(8,128)(2,1)}, u32[]{:S(2)}, u32[]{:S(2)}) async-start(bf16[32,16,4096]{2,1,0:T(8,128)(2,1)} %bitcast.45), calls=%async_computation.1 | async-start | bytes 8388608 | tf_op jit(solution)/shard_map/encode_decode/all_to_all | solution.py:11
  128.4 2.1 all_to_all.59
  130.5 46.6 %all-to-all-done.1 = bf16[32,16,4096]{2,1,0:T(8,128)(2,1)} async-done(((bf16[32,16,4096]{2,1,0:T(8,128)(2,1)}), bf16[32,16,4096]{2,1,0:T(8,128)(2,1)}, u32[]{:S(2)}, u32[]{:S(2)}) %all-to-all-start.1) | async-done | bytes 4194336 | tf_op jit(solution)/shard_map/encode_decode/all_to_all | solution.py:11
  177.2 3.3 convolution_add_fusion.4
  180.5 0.4 fusion.4
  180.9 1.3 convolution_convert_fusion
  182.2 56.3 %all_to_all.72 = bf16[32,16,4096]{2,1,0:T(8,128)(2,1)S(1)} all-to-all(bf16[32,16,4096]{2,1,0:T(8,128)(2,1)S(1)} %bitcast.43), channel_id=1, replica_groups=mesh['loop'=4,'inner'=8,'batch'=8] {'loop','inner'}, dimensions={0} | all-to-all | bytes 8388608 | tf_op jit(solution)/shard_map/combine/all_to_all | solution.py:11
  238.5 2.0 copy-done.4
  240.5 0.5 slice.38
  241.6 1.5 fusion.5
  243.2 2.3 all_to_all.63
  245.4 7.2 %all-to-all-start.5 = ((bf16[32,4,4096]{2,1,0:T(4,128)(2,1)}), bf16[32,4,4096]{2,1,0:T(4,128)(2,1)}, u32[]{:S(2)}, u32[]{:S(2)}) async-start(bf16[32,4,4096]{2,1,0:T(4,128)(2,1)} %all_to_all.63), calls=%async_computation.5 | async-start | bytes 2097152 | tf_op jit(solution)/shard_map/combine/all_to_all | solution.py:11
  252.7 3.6 %fusion.56 = (f32[256]{0:T(256)S(1)}, bf16[512,256]{1,0:T(8,128)(2,1)S(1)}) fusion(f32[512,256]{1,0:T(8,128)} %copy.45, s32[256]{0:T(256)S(1)} %copy-done.15, s32[512]{0:T(512)S(1)} %add_select_fusion.4, bf16[512,4096]{1,0:T(8,128)(2,1)} %bitcast.50, bf16[256,4096]{1,0:T(8,128)(2,1)S(1)} %copy-done), kind=kOutput, calls=%fused_computation.102 | convolution fusion | flops 1074396928 | bytes 7081984 | tf_op jit(solution)/shard_map/backward/dot_general | solution.py:107
  256.3 3.6 %fusion.35 = bf16[4224,256]{1,0:T(8,128)(2,1)S(1)} fusion(bf16[512,4224]{1,0:T(8,128)(2,1)} %bitcast.2, bf16[512,256]{1,0:T(8,128)(2,1)S(1)} %get-tuple-element.35), kind=kOutput, calls=%fused_computation.46 | convolution fusion | flops 1107296256 | bytes 6750208 | tf_op jit(solution)/shard_map/backward/dot_general | solution.py:112
  260.0 1.5 slice.50
  261.4 1.5 copy-done.5
  262.9 2.6 convolution_convert_fusion.2
  265.5 1.9 all-to-all-done.5
  267.4 2.1 all_to_all.65
  269.6 2.2 fusion.57
  271.8 2.1 fusion.2
  274.0 2.5 fusion.3
  276.5 2.2 fusion.6
  278.7 57.7 %reduce-scatter.2.cloned.1.call-done = bf16[520,512]{1,0:T(8,128)(2,1)} async-done(((bf16[4160,512]{1,0:T(8,128)(2,1)}), bf16[520,512]{1,0:T(8,128)(2,1)}) %reduce-scatter.2.cloned.1.call-update) | async-done | bytes 532496 | tf_op jit(solution)/shard_map/grad_reduce/reduce_scatter | solution.py:145
  336.3 1.9 convert_bitcast_fusion
  338.2 1.0 copy.51
  339.2 1.2 fusion.45
  (50 shorter events, 1.1 us)
Async XLA Ops:
  7.2 46.8 %copy-start = (bf16[256,4096]{1,0:T(8,128)(2,1)S(1)}, bf16[256,4096]{1,0:T(8,128)(2,1)}, u32[]{:S(2)}) copy-start(bf16[256,4096]{1,0:T(8,128)(2,1)} %param.12) | copy-start | bytes 6291460
  10.9 0.7 copy-start.11
  14.7 22.5 %all-to-all-start.2 = ((bf16[32,4,4224]{2,1,0:T(4,128)(2,1)}), bf16[32,4,4224]{2,1,0:T(4,128)(2,1)S(1)}, u32[]{:S(2)}, u32[]{:S(2)}) async-start(bf16[32,4,4224]{2,1,0:T(4,128)(2,1)} %all_to_all.54), calls=%async_computation.2 | async-start | bytes 2162688 | tf_op jit(solution)/shard_map/dispatch/all_to_all | solution.py:11
  37.3 1.0 copy-start.3
  37.3 8.5 %copy-start.18 = (bf16[256]{0:T(256)(128)(2,1)S(1)}, bf16[256]{0:T(256)(128)(2,1)}, u32[]{:S(2)}) copy-start(bf16[256]{0:T(256)(128)(2,1)} %param.11) | copy-start | bytes 1540
  38.3 58.0 %all-to-all-start = ((bf16[32,16,4224]{2,1,0:T(8,128)(2,1)}), bf16[32,16,4224]{2,1,0:T(8,128)(2,1)}, u32[]{:S(2)}, u32[]{:S(2)}) async-start(bf16[32,16,4224]{2,1,0:T(8,128)(2,1)} %bitcast.48), calls=%async_computation | async-start | bytes 8650752 | tf_op jit(solution)/shard_map/dispatch/all_to_all | solution.py:11
  53.3 0.6 copy-start.9
  57.7 54.8 %copy-start.15 = (s32[256]{0:T(256)S(1)}, s32[256]{0:T(256)}, u32[]{:S(2)}) copy-start(s32[256]{0:T(256)} %and_select_fusion.1) | copy-start | bytes 3076
  57.7 54.8 %copy-start.17 = (f32[256]{0:T(256)S(1)}, f32[256]{0:T(256)}, u32[]{:S(2)}) copy-start(f32[256]{0:T(256)} %convert_element_type.124) | copy-start | bytes 3076
  96.3 24.4 %all-to-all-start.3 = ((bf16[32,4,4096]{2,1,0:T(4,128)(2,1)}), bf16[32,4,4096]{2,1,0:T(4,128)(2,1)}, u32[]{:S(2)}, u32[]{:S(2)}) async-start(bf16[32,4,4096]{2,1,0:T(4,128)(2,1)} %all_to_all.57), calls=%async_computation.3 | async-start | bytes 2097152 | tf_op jit(solution)/shard_map/encode_decode/all_to_all | solution.py:11
  116.7 0.7 copy-start.12
  120.7 7.7 %copy-start.14 = (bf16[4096]{0:T(1024)(128)(2,1)S(1)}, bf16[4096]{0:T(1024)(128)(2,1)}, u32[]{:S(2)}) copy-start(bf16[4096]{0:T(1024)(128)(2,1)} %param.13) | copy-start | bytes 24580
  120.7 56.5 %all-to-all-start.1 = ((bf16[32,16,4096]{2,1,0:T(8,128)(2,1)}), bf16[32,16,4096]{2,1,0:T(8,128)(2,1)}, u32[]{:S(2)}, u32[]{:S(2)}) async-start(bf16[32,16,4096]{2,1,0:T(8,128)(2,1)} %bitcast.45), calls=%async_computation.1 | async-start | bytes 8388608 | tf_op jit(solution)/shard_map/encode_decode/all_to_all | solution.py:11
  177.2 3.3 copy-start.6
  238.5 2.0 copy-start.4
  245.4 22.0 %all-to-all-start.5 = ((bf16[32,4,4096]{2,1,0:T(4,128)(2,1)}), bf16[32,4,4096]{2,1,0:T(4,128)(2,1)}, u32[]{:S(2)}, u32[]{:S(2)}) async-start(bf16[32,4,4096]{2,1,0:T(4,128)(2,1)} %all_to_all.63), calls=%async_computation.5 | async-start | bytes 2097152 | tf_op jit(solution)/shard_map/combine/all_to_all | solution.py:11
  252.6 83.7 %reduce-scatter.2.cloned.1.call-start = ((), (), s32[]{:S(2)}) async-start(), calls=%async_computation.7 | async-start | bytes 4792320 | tf_op jit(solution)/shard_map/grad_reduce/reduce_scatter | solution.py:145
  256.3 5.1 %copy-start.13 = (bf16[512,256]{1,0:T(8,128)(2,1)S(1)}, bf16[512,256]{1,0:T(8,128)(2,1)}, u32[]{:S(2)}) copy-start(bf16[512,256]{1,0:T(8,128)(2,1)} %copy-done.12) | copy-start | bytes 786436
  259.9 2.9 copy-start.5
  262.9 6.7 %copy-start.16 = (s32[128]{0:T(128)S(1)}, s32[128]{0:T(128)}, u32[]{:S(2)}) copy-start(s32[128]{0:T(128)} %and_select_fusion) | copy-start | bytes 1540
  265.5 4.0 %copy-start.8 = (f32[128,256]{1,0:T(8,128)S(1)}, f32[128,256]{1,0:T(8,128)}, u32[]{:S(2)}) copy-start(f32[128,256]{1,0:T(8,128)} %copy.49) | copy-start | bytes 393220
  269.5 2.3 copy-start.1
  269.6 2.3 copy-start.7
  269.6 2.3 copy-start.10
  274.0 2.5 copy-start.2
Sparse Core Ops, SparseCore 0:
  278.8 57.5 reduce-scatter.1

commit v9 on v7

--- a/solution.py
+++ b/solution.py
@@ -99,25 +99,30 @@
             send_err = pick_rows(token_to_slot[k], err_b)
             if error_rows:
                 send_err = send_err + 0 * error_rows[0][:1, :1]
+            if error_rows:
+                send_err = send_err.reshape(owners, -1, model_width)
             error_rows.append(exchange(send_err))
 
     with jax.named_scope("backward"):
         enc_grad = dec_grad_t = bias_grad = 0.0
         for k in range(len(rank_sets)):
+            err_k = error_rows[k]
+            lead = err_k.shape[:-1]
+            rows_k = tuple(range(len(lead)))
             pre_grad = lax.dot_general(
-                error_rows[k], dec_weight, (((1,), (1,)), ((), ())),
+                err_k, dec_weight, (((len(lead),), (1,)), ((), ())),
                 preferred_element_type=jnp.float32,
-            ) * gates[k]
+            ) * gates[k].reshape(lead + (local_lat,))
             pre_grad_b = pre_grad.astype(jnp.bfloat16)
             enc_grad = enc_grad + lax.dot_general(
-                payload[k], pre_grad_b, (((0,), (0,)), ((), ())),
+                payload[k].reshape(lead + (-1,)), pre_grad_b, ((rows_k, rows_k), ((), ())),
                 preferred_element_type=jnp.float32,
             )[:model_width]
             dec_grad_t = dec_grad_t + lax.dot_general(
-                error_rows[k], codes[k], (((0,), (0,)), ((), ())),
+                err_k, codes[k].reshape(lead + (local_lat,)), ((rows_k, rows_k), ((), ())),
                 preferred_element_type=jnp.float32,
             )
-            bias_grad = bias_grad + jnp.sum(pre_grad, axis=0)
+            bias_grad = bias_grad + jnp.sum(pre_grad, axis=rows_k)
             if k == 0:
                 enc_b, dec_b, bias_grad = lax.optimization_barrier(
                     (enc_grad.astype(jnp.bfloat16), dec_grad_t.astype(jnp.bfloat16), bias_grad)

time: 349 us -> 353 us (1.011)
  blocking collectives: 56.3 us -> 0 us
  waiting for transfers between devices: 153 us -> 201 us
  starting transfers between devices: 39.2 us -> 50.3 us
    all_to_all x1 -> x0, blocking collectives: 56.3 us -> none  [exchange(): lax.all_to_all(rows, OWNER_AXES, split_axis=0, concat_axis=0, tiled=True)]
    all_to_all x5 -> x6, waiting for transfers between devices: 95.8 us -> 143 us  [exchange(): lax.all_to_all(rows, OWNER_AXES, split_axis=0, concat_axis=0, tiled=True)]
    all_to_all x5 -> x6, starting transfers between devices: 39.2 us -> 50.3 us  [exchange(): lax.all_to_all(rows, OWNER_AXES, split_axis=0, concat_axis=0, tiled=True)]
    all_to_all x6 -> x4, local copies, waits for them, and re-layouts: 11.3 us -> 5.97 us  [exchange(): lax.all_to_all(rows, OWNER_AXES, split_axis=0, concat_axis=0, tiled=True)]
    another operation x4 -> x6, local copies, waits for them, and re-layouts: 6.05 us -> 7.8 us  [shards(): gate_k = jnp.where(in_block, jnp.tile(mask_k, (1, local_blocks)), 0.0)]
    unnamed x44 -> x47, local copies, waits for them, and re-layouts: 9.83 us -> 9.91 us
  transfers between devices with their start and end apart: 6 -> 7, of which waited for: 5 -> 6; matrix products, arithmetic and copies ran while one was open for 11% -> 12% of each run, Pallas kernels for 0% -> 0%
where the time goes in v9:
time: 353 us; the launch traced here: 351 us
  waiting for transfers between devices  201 us (57%)
  starting transfers between devices  50.3 us (14%)
  matrix products  43.9 us (12%)
  local copies, waits for them, and re-layouts  32.6 us (9%)
  between operations  15.1 us (4%)
  other arithmetic  7.96 us (2%)
    all_to_all x6, waiting for transfers between devices, exchange(): lax.all_to_all(rows, OWNER_AXES, split_axis=0, concat_axis=0, tiled=True)  143 us
    reduce_scatter x1, waiting for transfers between devices, shards(): lax.psum_scatter(stacked, 'batch', scatter_dimension=0, tiled=True)  57.7 us
    all_to_all x6, starting transfers between devices, exchange(): lax.all_to_all(rows, OWNER_AXES, split_axis=0, concat_axis=0, tiled=True)  50.3 us
    unnamed x47, local copies, waits for them, and re-layouts  9.91 us
    another operation x6, local copies, waits for them, and re-layouts, shards(): gate_k = jnp.where(in_block, jnp.tile(mask_k, (1, local_blocks)), 0.0)  7.8 us
    dot_general x2, matrix products, shards(): lax.dot_general(err_k, codes[k].reshape(lead + (local_lat,)), ((rows_k, r...  7.41 us
  transfers between devices with their start and end apart: 7, of which 6 were waited for; matrix products, arithmetic and copies ran while one was open for 12% of the time, Pallas kernels for 0%

profile of v9, /device:TPU:6, one launch (start us, length us, event | category | flops | bytes accessed | tf_op | source)
XLA Modules:
  0.0 350.7 jit_solution(9065455960185152379)
XLA Ops:
  7.2 0.9 copy.90
  8.1 0.7 broadcast_compare_fusion
  8.8 0.9 convert_element_type.107
  11.6 1.7 fusion.1
  13.3 1.2 all_to_all.49
  14.4 7.6 %all-to-all-start.2 = ((bf16[32,4,4224]{2,1,0:T(4,128)(2,1)}), bf16[32,4,4224]{2,1,0:T(4,128)(2,1)S(1)}, u32[]{:S(2)}, u32[]{:S(2)}) async-start(bf16[32,4,4224]{2,1,0:T(4,128)(2,1)} %all_to_all.49), calls=%async_computation.2 | async-start | bytes 2162688 | tf_op jit(solution)/shard_map/dispatch/all_to_all | solution.py:11
  22.3 1.5 fusion.37
  23.7 4.6 %add_convert_fusion = bf16[512,4224]{1,0:T(8,128)(2,1)} fusion(f32[512,64]{1,0:T(8,128)S(1)} %fusion.37, bf16[128,4096]{1,0:T(8,128)(2,1)} %param.7, s32[128,512]{1,0:T(8,128)S(1)} %convert_reduce_fusion), kind=kOutput, calls=%fused_computation | convolution fusion | flops 558039040 | bytes 5767168 | tf_op jit(solution)/shard_map/dispatch/dot_general | solution.py:64
  28.4 8.6 %all-to-all-done.2 = bf16[32,4,4224]{2,1,0:T(4,128)(2,1)S(1)} async-done(((bf16[32,4,4224]{2,1,0:T(4,128)(2,1)}), bf16[32,4,4224]{2,1,0:T(4,128)(2,1)S(1)}, u32[]{:S(2)}, u32[]{:S(2)}) %all-to-all-start.2) | async-done | bytes 1081376 | tf_op jit(solution)/shard_map/dispatch/all_to_all | solution.py:11
  37.0 1.0 copy-done.2
  38.0 7.5 %all-to-all-start = ((bf16[32,16,4224]{2,1,0:T(8,128)(2,1)}), bf16[32,16,4224]{2,1,0:T(8,128)(2,1)}, u32[]{:S(2)}, u32[]{:S(2)}) async-start(bf16[32,16,4224]{2,1,0:T(8,128)(2,1)} %bitcast.55), calls=%async_computation | async-start | bytes 8650752 | tf_op jit(solution)/shard_map/dispatch/all_to_all | solution.py:11
  45.5 0.6 convert_element_type.112
  46.0 0.5 and_select_fusion
  46.5 0.5 and_select_fusion.1
  47.1 1.3 all_to_all.51
  48.5 0.7 tile.22
  49.2 1.7 copy.106
  50.9 2.1 fusion.32
  53.0 0.6 copy-done.8
  53.6 0.4 convolution_convert_fusion.4
  54.1 1.2 all_to_all.52
  55.3 40.7 %all-to-all-done = bf16[32,16,4224]{2,1,0:T(8,128)(2,1)} async-done(((bf16[32,16,4224]{2,1,0:T(8,128)(2,1)}), bf16[32,16,4224]{2,1,0:T(8,128)(2,1)}, u32[]{:S(2)}, u32[]{:S(2)}) %all-to-all-start) | async-done | bytes 4325408 | tf_op jit(solution)/shard_map/dispatch/all_to_all | solution.py:11
  96.0 8.6 %all-to-all-start.3 = ((bf16[32,4,4096]{2,1,0:T(4,128)(2,1)}), bf16[32,4,4096]{2,1,0:T(4,128)(2,1)S(1)}, u32[]{:S(2)}, u32[]{:S(2)}) async-start(bf16[32,4,4096]{2,1,0:T(4,128)(2,1)} %all_to_all.52), calls=%async_computation.3 | async-start | bytes 2097152 | tf_op jit(solution)/shard_map/encode_decode/all_to_all | solution.py:11
  104.6 1.6 slice.33
  106.2 1.6 copy.117
  107.8 1.7 tile.20
  109.5 2.0 copy.102
  111.5 4.2 %fusion.20 = bf16[512,256]{1,0:T(8,128)(2,1)S(1)} fusion(bf16[512,4224]{1,0:T(8,128)(2,1)} %bitcast.2, bf16[4096,256]{1,0:T(8,128)(2,1)} %param.10, f32[512,256]{1,0:T(8,128)} %copy.102, s32[256]{0:T(256)S(1)} %copy-done.17, f32[256]{0:T(256)S(1)} %copy-done.18, s32[512]{0:T(512)S(1)} %add_select_fusion.5), kind=kOutput, calls=%fused_computation.31 | convolution fusion | flops 1107951616 | bytes 7213056 | tf_op jit(solution)/shard_map/encode_decode/dot_general | solution.py:80
  115.8 0.7 copy-done.12
  116.5 3.3 convolution_convert_fusion.1
  119.7 1.0 copy-done.5
  120.7 7.5 %all-to-all-start.1 = ((bf16[32,16,4096]{2,1,0:T(8,128)(2,1)}), bf16[32,16,4096]{2,1,0:T(8,128)(2,1)}, u32[]{:S(2)}, u32[]{:S(2)}) async-start(bf16[32,16,4096]{2,1,0:T(8,128)(2,1)} %bitcast.53), calls=%async_computation.1 | async-start | bytes 8388608 | tf_op jit(solution)/shard_map/encode_decode/all_to_all | solution.py:11
  128.3 2.2 all_to_all.54
  130.5 46.5 %all-to-all-done.1 = bf16[32,16,4096]{2,1,0:T(8,128)(2,1)} async-done(((bf16[32,16,4096]{2,1,0:T(8,128)(2,1)}), bf16[32,16,4096]{2,1,0:T(8,128)(2,1)}, u32[]{:S(2)}, u32[]{:S(2)}) %all-to-all-start.1) | async-done | bytes 4194336 | tf_op jit(solution)/shard_map/encode_decode/all_to_all | solution.py:11
  177.1 3.0 convolution_add_fusion.2
  180.1 0.4 fusion.4
  180.5 3.3 convolution_convert_fusion
  183.8 9.8 %all-to-all-start.4 = ((bf16[32,16,4096]{2,1,0:T(8,128)(2,1)}), bf16[32,16,4096]{2,1,0:T(8,128)(2,1)}, u32[]{:S(2)}, u32[]{:S(2)}) async-start(bf16[32,16,4096]{2,1,0:T(8,128)(2,1)} %bitcast.51), calls=%async_computation.4 | async-start | bytes 8388608 | tf_op jit(solution)/shard_map/combine/all_to_all | solution.py:11
  193.6 0.7 copy.122
  194.3 0.6 reshape.217
  195.0 0.9 tile.22.clone
  195.9 0.9 tile.24
  196.7 45.6 %all-to-all-done.4 = bf16[32,16,4096]{2,1,0:T(8,128)(2,1)} async-done(((bf16[32,16,4096]{2,1,0:T(8,128)(2,1)}), bf16[32,16,4096]{2,1,0:T(8,128)(2,1)}, u32[]{:S(2)}, u32[]{:S(2)}) %all-to-all-start.4) | async-done | bytes 4194336 | tf_op jit(solution)/shard_map/combine/all_to_all | solution.py:11
  242.4 1.2 slice.36
  244.2 1.5 fusion.5
  245.7 2.3 reshape.215
  248.0 9.4 %all-to-all-start.5 = ((bf16[32,4,4096]{2,1,0:T(4,128)(2,1)}), bf16[32,4,4096]{2,1,0:T(4,128)(2,1)}, u32[]{:S(2)}, u32[]{:S(2)}) async-start(bf16[32,4,4096]{2,1,0:T(4,128)(2,1)} %reshape.215), calls=%async_computation.5 | async-start | bytes 2097152 | tf_op jit(solution)/shard_map/combine/all_to_all | solution.py:11
  257.5 3.5 fusion.67
  261.0 3.6 %fusion.43 = bf16[4224,256]{1,0:T(8,128)(2,1)S(1)} fusion(bf16[512,4224]{1,0:T(8,128)(2,1)} %bitcast.2, bf16[512,256]{1,0:T(8,128)(2,1)S(1)} %get-tuple-element.39), kind=kOutput, calls=%fused_computation.51 | convolution fusion | flops 1107296256 | bytes 6750208 | tf_op jit(solution)/shard_map/backward/dot_general | solution.py:117
  264.6 1.1 copy-done.13
  265.7 4.9 %convolution_convert_fusion.2 = bf16[4096,256]{1,0:T(8,128)(2,1)} fusion(bf16[512,4096]{1,0:T(8,128)(2,1)} %bitcast.8, bf16[512,256]{1,0:T(8,128)(2,1)S(1)} %copy-done.13), kind=kOutput, calls=%fused_computation.11 | convolution fusion | flops 1074790400 | bytes 6553600 | tf_op jit(solution)/shard_map/backward/dot_general | solution.py:121
  270.6 1.6 all-to-all-done.5
  272.2 2.3 fusion.68
  274.6 0.8 convolution_bitcast_fusion
  275.4 0.8 slice-done
  276.2 0.6 fusion.7
  277.0 0.8 copy-done.20
  277.8 2.5 fusion.3
  280.4 2.2 fusion.6
  282.6 57.7 %reduce-scatter.2.cloned.1.call-done = bf16[520,512]{1,0:T(8,128)(2,1)} async-done(((bf16[4160,512]{1,0:T(8,128)(2,1)}), bf16[520,512]{1,0:T(8,128)(2,1)}) %reduce-scatter.2.cloned.1.call-update) | async-done | bytes 532496 | tf_op jit(solution)/shard_map/grad_reduce/reduce_scatter | solution.py:150
  340.2 1.2 convert_element_type.133
  341.5 0.5 slice_bitcast_fusion.1
  342.0 1.0 copy.114
  343.0 0.8 slice.38
  (63 shorter events, 2.6 us)
Async XLA Ops:
  7.2 46.5 %copy-start = (bf16[256,4096]{1,0:T(8,128)(2,1)S(1)}, bf16[256,4096]{1,0:T(8,128)(2,1)}, u32[]{:S(2)}) copy-start(bf16[256,4096]{1,0:T(8,128)(2,1)} %param.12) | copy-start | bytes 6291460
  9.9 1.3 copy-start.10
  14.4 22.5 %all-to-all-start.2 = ((bf16[32,4,4224]{2,1,0:T(4,128)(2,1)}), bf16[32,4,4224]{2,1,0:T(4,128)(2,1)S(1)}, u32[]{:S(2)}, u32[]{:S(2)}) async-start(bf16[32,4,4224]{2,1,0:T(4,128)(2,1)} %all_to_all.49), calls=%async_computation.2 | async-start | bytes 2162688 | tf_op jit(solution)/shard_map/dispatch/all_to_all | solution.py:11
  37.0 1.0 copy-start.2
  37.0 8.5 %copy-start.19 = (bf16[256]{0:T(256)(128)(2,1)S(1)}, bf16[256]{0:T(256)(128)(2,1)}, u32[]{:S(2)}) copy-start(bf16[256]{0:T(256)(128)(2,1)} %param.11) | copy-start | bytes 1540
  38.0 58.0 %all-to-all-start = ((bf16[32,16,4224]{2,1,0:T(8,128)(2,1)}), bf16[32,16,4224]{2,1,0:T(8,128)(2,1)}, u32[]{:S(2)}, u32[]{:S(2)}) async-start(bf16[32,16,4224]{2,1,0:T(8,128)(2,1)} %bitcast.55), calls=%async_computation | async-start | bytes 8650752 | tf_op jit(solution)/shard_map/dispatch/all_to_all | solution.py:11
  53.0 0.6 copy-start.8
  55.3 56.2 %copy-start.17 = (s32[256]{0:T(256)S(1)}, s32[256]{0:T(256)}, u32[]{:S(2)}) copy-start(s32[256]{0:T(256)} %and_select_fusion.1) | copy-start | bytes 3076
  55.3 56.2 %copy-start.18 = (f32[256]{0:T(256)S(1)}, f32[256]{0:T(256)}, u32[]{:S(2)}) copy-start(f32[256]{0:T(256)} %convert_element_type.112) | copy-start | bytes 3076
  96.0 23.7 %all-to-all-start.3 = ((bf16[32,4,4096]{2,1,0:T(4,128)(2,1)}), bf16[32,4,4096]{2,1,0:T(4,128)(2,1)S(1)}, u32[]{:S(2)}, u32[]{:S(2)}) async-start(bf16[32,4,4096]{2,1,0:T(4,128)(2,1)} %all_to_all.52), calls=%async_computation.3 | async-start | bytes 2097152 | tf_op jit(solution)/shard_map/encode_decode/all_to_all | solution.py:11
  115.8 0.7 copy-start.12
  119.7 1.0 copy-start.5
  119.7 8.5 %copy-start.16 = (bf16[4096]{0:T(1024)(128)(2,1)S(1)}, bf16[4096]{0:T(1024)(128)(2,1)}, u32[]{:S(2)}) copy-start(bf16[4096]{0:T(1024)(128)(2,1)} %param.13) | copy-start | bytes 24580
  120.7 56.3 %all-to-all-start.1 = ((bf16[32,16,4096]{2,1,0:T(8,128)(2,1)}), bf16[32,16,4096]{2,1,0:T(8,128)(2,1)}, u32[]{:S(2)}, u32[]{:S(2)}) async-start(bf16[32,16,4096]{2,1,0:T(8,128)(2,1)} %bitcast.53), calls=%async_computation.1 | async-start | bytes 8388608 | tf_op jit(solution)/shard_map/encode_decode/all_to_all | solution.py:11
  128.3 48.8 %copy-start.4 = (bf16[128,4096]{1,0:T(8,128)(2,1)S(1)}, bf16[128,4096]{1,0:T(8,128)(2,1)}, u32[]{:S(2)}) copy-start(bf16[128,4096]{1,0:T(8,128)(2,1)} %param.7) | copy-start | bytes 3145732
  177.1 3.0 copy-start.6
  183.8 10.5 %copy-start.9 = (bf16[128,256]{1,0:T(8,128)(2,1)S(1)}, bf16[128,256]{1,0:T(8,128)(2,1)}, u32[]{:S(2)}) copy-start(bf16[128,256]{1,0:T(8,128)(2,1)} %copy-done.8) | copy-start | bytes 196612
  183.8 58.6 %all-to-all-start.4 = ((bf16[32,16,4096]{2,1,0:T(8,128)(2,1)}), bf16[32,16,4096]{2,1,0:T(8,128)(2,1)}, u32[]{:S(2)}, u32[]{:S(2)}) async-start(bf16[32,16,4096]{2,1,0:T(8,128)(2,1)} %bitcast.51), calls=%async_computation.4 | async-start | bytes 8388608 | tf_op jit(solution)/shard_map/combine/all_to_all | solution.py:11
  245.7 11.8 %copy-start.11 = (f32[512,256]{1,0:T(8,128)S(1)}, f32[512,256]{1,0:T(8,128)}, u32[]{:S(2)}) copy-start(f32[512,256]{1,0:T(8,128)} %copy.102) | copy-start | bytes 1572868
  248.0 24.1 %all-to-all-start.5 = ((bf16[32,4,4096]{2,1,0:T(4,128)(2,1)}), bf16[32,4,4096]{2,1,0:T(4,128)(2,1)}, u32[]{:S(2)}, u32[]{:S(2)}) async-start(bf16[32,4,4096]{2,1,0:T(4,128)(2,1)} %reshape.215), calls=%async_computation.5 | async-start | bytes 2097152 | tf_op jit(solution)/shard_map/combine/all_to_all | solution.py:11
  257.4 82.8 %reduce-scatter.2.cloned.1.call-start = ((), (), s32[]{:S(2)}) async-start(), calls=%async_computation.7 | async-start | bytes 4792320 | tf_op jit(solution)/shard_map/grad_reduce/reduce_scatter | solution.py:150
  264.5 6.0 %copy-start.1 = (bf16[4224,256]{1,0:T(8,128)(2,1)}, bf16[4224,256]{1,0:T(8,128)(2,1)S(1)}, u32[]{:S(2)}) copy-start(bf16[4224,256]{1,0:T(8,128)(2,1)S(1)} %fusion.43) | copy-start | bytes 6488068
  264.5 1.1 copy-start.13
  265.7 6.5 %copy-start.14 = (f32[32,4,256]{2,1,0:T(4,128)S(1)}, f32[32,4,256]{2,1,0:T(4,128)}, u32[]{:S(2)}) copy-start(f32[32,4,256]{2,1,0:T(4,128)} %tile.24) | copy-start | bytes 393220
  270.6 4.0 %copy-start.3 = (bf16[32,4,4224]{2,1,0:T(4,128)(2,1)S(1)}, bf16[32,4,4224]{2,1,0:T(4,128)(2,1)}, u32[]{:S(2)}) copy-start(bf16[32,4,4224]{2,1,0:T(4,128)(2,1)} %copy-done.2) | copy-start | bytes 3244036
  274.6 1.6 slice-start
  276.2 0.8 copy-start.15
  276.2 1.6 copy-start.20
  340.2 2.8 copy-start.7
Sparse Core Ops, SparseCore 0:
  282.7 57.4 reduce-scatter.1
